TPU v7x, 32 devices: a whole 2x2x4 slice. The times are simulated.
32 devices in a mesh: groups: 2 (over x), seq: 16 (over z, y, core).
Axes of the slice: x: 2, y: 2, z: 4, core: 2. Of those that a mesh axis runs over, the one named last changes fastest.
Arguments:
- queries: bfloat16 [12288, 1536], P(('groups', 'seq')), parts along dimension 0, may hold values from -6 to 6
- keys: bfloat16 [12288, 1536], P(('groups', 'seq')), parts along dimension 0, may hold values from -6 to 6
- values: bfloat16 [12288, 1536], P(('groups', 'seq')), parts along dimension 0, may hold values from -6 to 6
- tile_lengths: int32 [32], P(('groups', 'seq')), parts along dimension 0, may hold values from 192 to 384
- head_windows: int32 [12, 2], replicated, may hold values from 0 to 1
- out_weight: bfloat16 [1536, 3072], P('seq'), may hold values from -0.4375 to 0.4375
- gate: float32 [6144], P('groups'), parts along dimension 0, may hold values from 0.5 to 2
Outputs:
- attn_branch: bfloat16 [12288, 3072], P(('groups', 'seq')), parts along dimension 0
There are 2 independent parts, one for each index of `groups`. A program takes and returns all parts, laid end to end along the dimension named above; an argument that names none is the same for every part. Nothing has to cross between parts.
All inputs are finite; a program needn't handle non-finite values.
Results may differ from a plain program's by a relative error of at most 0.0057.
Values may be sent and summed in bfloat16 or wider, within the bound.
No kernel may reach another device: no remote copies, remote signals or barrier semaphores. Data moves between devices by JAX's collectives and lax.ppermute only.
A program may use at most 128 MiB of HBM per device.

v0:
```python
import math

import jax
import jax.numpy as jnp
from jax import lax
from jax.experimental import pallas as pl
from jax.sharding import PartitionSpec as P

TW = 8
GROUPS = 4


def group_attention(queries, slots, usable, head_base, group_heads, head_dim, score_scale):
    tile_rows, feat_width = queries.shape
    count = len(slots)

    def kernel(*refs):
        query = refs[0][...]
        key_refs = refs[1:1 + 2 * count:2]
        value_refs = refs[2:2 + 2 * count:2]
        mask_ref = refs[1 + 2 * count]
        out_ref = refs[-1]
        scores = []
        allowed = []
        for j in range(count):
            part = lax.dot_general(
                query, key_refs[j][...], (((1,), (1,)), ((), ())),
                preferred_element_type=jnp.float32,
            ) * score_scale
            ok = mask_ref[0, j:j + 1, :] != 0
            scores.append(jnp.where(ok, part, -1e30))
            allowed.append(ok)
        maximum = scores[0].max(axis=1, keepdims=True)
        for part in scores[1:]:
            maximum = jnp.maximum(maximum, part.max(axis=1, keepdims=True))
        exponents = [
            jnp.where(ok, jnp.exp(part - maximum), 0.0) for part, ok in zip(scores, allowed)
        ]
        denominator = exponents[0].sum(axis=1, keepdims=True)
        for part in exponents[1:]:
            denominator = denominator + part.sum(axis=1, keepdims=True)
        total = None
        for j in range(count):
            weights = (exponents[j] / denominator).astype(jnp.bfloat16)
            term = jnp.dot(weights, value_refs[j][...], preferred_element_type=jnp.float32)
            total = term if total is None else total + term
        out_ref[...] = total.astype(out_ref.dtype)

    in_specs = [pl.BlockSpec((tile_rows, head_dim), lambda h: (0, head_base + h))]
    operands = [queries]
    for key_array, value_array, key_block, value_block in slots:
        in_specs.append(pl.BlockSpec((tile_rows, head_dim), lambda h, b=key_block: (0, b + h)))
        in_specs.append(pl.BlockSpec((tile_rows, head_dim), lambda h, b=value_block: (0, b + h)))
        operands += [key_array, value_array]
    in_specs.append(pl.BlockSpec((1, count, tile_rows), lambda h: (h, 0, 0)))
    operands.append(usable.astype(jnp.int32))
    return pl.pallas_call(
        kernel,
        grid=(group_heads,),
        in_specs=in_specs,
        out_specs=pl.BlockSpec((tile_rows, head_dim), lambda h: (0, h)),
        out_shape=jax.ShapeDtypeStruct((tile_rows, group_heads * head_dim), queries.dtype),
    )(*operands)


def vertical_parts(devices, grid_rows):
    if grid_rows == 1:
        return []
    down = [(i, i + TW) for i in range(devices - TW)]
    up = [(i + TW, i) for i in range(devices - TW)]
    if grid_rows == 2:
        return [down + up]
    return [down, up]


def on_device(queries, keys, values, tile_lengths, head_windows, out_weight, gate):
    devices = lax.axis_size("seq")
    grid_rows = devices // TW
    tile_rows = queries.shape[0]
    feat_width = queries.shape[1]
    head_count = head_windows.shape[0]
    head_dim = feat_width // head_count
    score_scale = 1.0 / math.sqrt(head_dim)
    groups = GROUPS if head_count % GROUPS == 0 else 1
    group_heads = head_count // groups
    group_width = group_heads * head_dim

    to_right = [(i, i + 1) for i in range(devices) if i % TW < TW - 1]
    to_left = [(i + 1, i) for i in range(devices) if i % TW < TW - 1]
    sideways = lambda x: (lax.ppermute(x, "seq", to_right), lax.ppermute(x, "seq", to_left))

    weight_all = lax.all_gather(out_weight, "seq", axis=0, tiled=True)
    (left_k, left_v, left_len), (right_k, right_v, right_len) = sideways(
        (keys, values, tile_lengths)
    )
    verticals = vertical_parts(devices, grid_rows)

    positions = jnp.arange(tile_rows, dtype=jnp.int32)
    query_real = positions < tile_lengths[0]

    def chunk(x, g):
        return lax.slice_in_dim(x, g * group_width, (g + 1) * group_width, axis=1)

    outputs = []
    previous = None
    for g in range(groups):
        own = jnp.concatenate([chunk(keys, g), chunk(values, g)], axis=1)
        if previous is not None:
            own, _ = lax.optimization_barrier((own, previous))
        got = [lax.ppermute((own, tile_lengths), "seq", pairs) for pairs in verticals]
        if got:
            previous = got[-1][0]
        forwarded = [sideways(item) for item in got]
        base = g * group_heads
        slots = [(keys, values, base, base)]
        lengths = [tile_lengths]
        rows = [0]
        cols = [0]
        for item in got:
            slots.append((item[0], item[0], 0, group_heads))
            lengths.append(item[1])
            rows.append(1)
            cols.append(0)
        slots += [(left_k, left_v, base, base), (right_k, right_v, base, base)]
        lengths += [left_len, right_len]
        rows += [0, 0]
        cols += [1, 1]
        for from_left, from_right in forwarded:
            slots += [(from_left[0], from_left[0], 0, group_heads),
                      (from_right[0], from_right[0], 0, group_heads)]
            lengths += [from_left[1], from_right[1]]
            rows += [1, 1]
            cols += [1, 1]
        length_stack = jnp.concatenate(lengths)
        key_real = positions[None, :] < length_stack[:, None]
        far_rows = jnp.array(rows, jnp.int32)
        far_cols = jnp.array(cols, jnp.int32)
        reach = lax.slice_in_dim(head_windows, base, base + group_heads, axis=0)
        window = (far_rows[None, :] <= reach[:, 0:1]) & (far_cols[None, :] <= reach[:, 1:2])
        usable = key_real[None, :, :] & window[:, :, None]
        attended = group_attention(
            queries, slots, usable, base, group_heads, head_dim, score_scale
        )
        outputs.append(jnp.where(query_real[:, None], attended, 0))

    attended_all = jnp.concatenate(outputs, axis=1)
    projected = jnp.dot(attended_all, weight_all, preferred_element_type=jnp.float32)
    return (projected * gate[None, :]).astype(jnp.bfloat16)


def solution(mesh):
    placed = (
        P(("groups", "seq"), None),
        P(("groups", "seq"), None),
        P(("groups", "seq"), None),
        P(("groups", "seq")),
        P(),
        P("seq", None),
        P("groups"),
    )
    return jax.shard_map(
        on_device, mesh=mesh, in_specs=placed, out_specs=P(("groups", "seq"), None), check_vma=False
    )
```

profile of v0, /device:TPU:27, one launch (start us, length us, event | category | flops | bytes accessed | tf_op | source)
XLA Modules:
  0.0 269.5 jit_solution(9677056973160046391)
XLA Ops:
  7.3 1.5 fusion.8
  9.3 47.5 %collective-permute-done.refs_3_.refs_4_ = bf16[384,768]{1,0:T(8,128)(2,1)S(1)} collective-permute-done((bf16[384,768]{1,0:T(8,128)(2,1)S(1)}, bf16[384,768]{1,0:T(8,128)(2,1)S(1)}, u32[]{:S(2)}, u32[]{:S(2)}) %collective-permute-start) | collective-permute-done | bytes 589856 | tf_op jit(solution)/shard_map/ppermute | solution.py:110
  56.8 3.5 %collective-permute-start.1 = (bf16[384,1536]{1,0:T(8,128)(2,1)S(1)}, bf16[384,1536]{1,0:T(8,128)(2,1)S(1)}, u32[]{:S(2)}, u32[]{:S(2)}) collective-permute-start(bf16[384,1536]{1,0:T(8,128)(2,1)S(1)} %copy-done), channel_id=1, source_target_pairs={{0,1},{1,2},{2,3},{3,4},{4,5},{5,6},{6,7},{8,9},{9,10},{10,11},{11... | collective-permute-start | bytes 3538952 | tf_op jit(solution)/shard_map/ppermute | solution.py:90
  60.3 1.9 collective-permute-start.2
  62.3 2.4 collective-permute-start.3
  64.8 61.8 %collective-permute-done.12.refs_3_.refs_4_ = bf16[384,768]{1,0:T(8,128)(2,1)} collective-permute-done((bf16[384,768]{1,0:T(8,128)(2,1)S(1)}, bf16[384,768]{1,0:T(8,128)(2,1)}, u32[]{:S(2)}, u32[]{:S(2)}) %collective-permute-start.12) | collective-permute-done | bytes 589856 | tf_op jit(solution)/shard_map/ppermute | solution.py:110
  126.6 2.6 collective-permute-start.4
  129.2 16.3 %collective-permute-done.15.refs_3_.refs_4_ = bf16[384,768]{1,0:T(8,128)(2,1)} collective-permute-done((bf16[384,768]{1,0:T(8,128)(2,1)S(1)}, bf16[384,768]{1,0:T(8,128)(2,1)}, u32[]{:S(2)}, u32[]{:S(2)}) %collective-permute-start.15) | collective-permute-done | bytes 589856 | tf_op jit(solution)/shard_map/ppermute | solution.py:110
  145.5 3.7 %collective-permute-done.7 = s32[1]{0:T(128)} collective-permute-done((s32[1]{0:T(128)}, s32[1]{0:T(128)}, u32[]{:S(2)}, u32[]{:S(2)}) %collective-permute-start.7) | collective-permute-done | bytes 36 | tf_op jit(solution)/shard_map/ppermute | solution.py:110
  149.2 1.9 collective-permute-start.8
  151.1 6.1 %collective-permute-done.8 = s32[1]{0:T(128)} collective-permute-done((s32[1]{0:T(128)}, s32[1]{0:T(128)}, u32[]{:S(2)}, u32[]{:S(2)}) %collective-permute-start.8) | collective-permute-done | bytes 36 | tf_op jit(solution)/shard_map/ppermute | solution.py:90
  157.2 5.1 %collective-permute-start.9 = (s32[1]{0:T(128)}, s32[1]{0:T(128)}, u32[]{:S(2)}, u32[]{:S(2)}) collective-permute-start(s32[1]{0:T(128)} %param.18), channel_id=1, source_target_pairs={{1,0},{2,1},{3,2},{4,3},{5,4},{6,5},{7,6},{9,8},{10,9},{11,10},{12... | collective-permute-start | bytes 20 | tf_op jit(solution)/shard_map/ppermute | solution.py:90
  163.4 1.9 collective-permute-start.10
  165.3 1.5 collective-permute-done.10
  166.7 4.8 %collective-permute-start.11 = (s32[1]{0:T(128)}, s32[1]{0:T(128)}, u32[]{:S(2)}, u32[]{:S(2)}) collective-permute-start(s32[1]{0:T(128)} %collective-permute-done.7), channel_id=1, source_target_pairs={{1,0},{2,1},{3,2},{4,3},{5,4},{6,5},{7,6},{9,8},{10,9},{11,10},{12... | collective-permute-start | bytes 20 | tf_op jit(solution)/shard_map/ppermute | solution.py:90
  172.6 1.9 collective-permute-start.5
  174.5 2.4 collective-permute-start.6
  177.0 3.2 %collective-permute-start.18 = (bf16[384,768]{1,0:T(8,128)(2,1)S(1)}, bf16[384,768]{1,0:T(8,128)(2,1)}, u32[]{:S(2)}, u32[]{:S(2)}) collective-permute-start(bf16[384,768]{1,0:T(8,128)(2,1)S(1)} %pad_maximum_fusion.3), channel_id=1, source_target_pairs={{0,8},{1,9},{2,10},{3,11},{4,12},{5,13},{6,14},{7,15},{8,0},{9,1},... | collective-permute-start | bytes 1769480 | tf_op jit(solution)/shard_map/ppermute | solution.py:110
  180.2 3.4 %collective-permute-start.13 = (bf16[384,768]{1,0:T(8,128)(2,1)}, bf16[384,768]{1,0:T(8,128)(2,1)S(1)}, u32[]{:S(2)}, u32[]{:S(2)}) collective-permute-start(bf16[384,768]{1,0:T(8,128)(2,1)} %collective-permute-done.12.refs_3_.refs_4_), channel_id=1, source_target_pairs={{0,1},{1,2},{2,3},{3,4},{4,5},{5,6},{6,7},{8,9},{9,10},{10,11},{11... | collective-permute-start | bytes 1769480 | tf_op jit(solution)/shard_map/ppermute | solution.py:90
  183.7 3.4 %collective-permute-start.14 = (bf16[384,768]{1,0:T(8,128)(2,1)}, bf16[384,768]{1,0:T(8,128)(2,1)S(1)}, u32[]{:S(2)}, u32[]{:S(2)}) collective-permute-start(bf16[384,768]{1,0:T(8,128)(2,1)} %collective-permute-done.12.refs_3_.refs_4_), channel_id=1, source_target_pairs={{1,0},{2,1},{3,2},{4,3},{5,4},{6,5},{7,6},{9,8},{10,9},{11,10},{12... | collective-permute-start | bytes 1769480 | tf_op jit(solution)/shard_map/ppermute | solution.py:90
  187.1 2.2 collective-permute-start.16
  189.4 7.4 %collective-permute-start.17 = (bf16[384,768]{1,0:T(8,128)(2,1)}, bf16[384,768]{1,0:T(8,128)(2,1)}, u32[]{:S(2)}, u32[]{:S(2)}) collective-permute-start(bf16[384,768]{1,0:T(8,128)(2,1)} %collective-permute-done.15.refs_3_.refs_4_), channel_id=1, source_target_pairs={{1,0},{2,1},{3,2},{4,3},{5,4},{6,5},{7,6},{9,8},{10,9},{11,10},{12... | collective-permute-start | bytes 1769480 | tf_op jit(solution)/shard_map/ppermute | solution.py:90
  196.8 9.8 %collective-permute-done.18.refs_3_.refs_4_ = bf16[384,768]{1,0:T(8,128)(2,1)} collective-permute-done((bf16[384,768]{1,0:T(8,128)(2,1)S(1)}, bf16[384,768]{1,0:T(8,128)(2,1)}, u32[]{:S(2)}, u32[]{:S(2)}) %collective-permute-start.18) | collective-permute-done | bytes 589856 | tf_op jit(solution)/shard_map/ppermute | solution.py:110
  206.5 1.9 collective-permute-start.19
  208.5 2.6 collective-permute-start.20
  212.4 3.7 %concatenate.22 = s32[6]{0:T(128)} concatenate(s32[1]{0:T(128)} %copy.16, s32[1]{0:T(128)} %collective-permute-done.7, s32[1]{0:T(128)} %collective-permute-done.8, s32[1]{0:T(128)} %collective-permute-done.9, s32[1]{0:T(128)} %collective-permute-done.10, s32[1]{0:T(128)} %collective-permute-done.11), dimensions={0} | concatenate | bytes 48 | tf_op jit(solution)/shard_map/concatenate | solution.py:134
  217.6 8.0 %shard_map.145 = bf16[384,384]{1,0:T(8,128)(2,1)} custom-call(bf16[384,1536]{1,0:T(8,128)(2,1)} %refs_0_.7, bf16[384,1536]{1,0:T(8,128)(2,1)} %refs_1_.7, bf16[384,1536]{1,0:T(8,128)(2,1)} %refs_2_.7, bf16[384,768]{1,0:T(8,128)(2,1)} %copy-done.6, bf16[384,768]{1,0:T(8,128)(2,1)} %copy-done.6, bf16[384,1536]{1,0:T(8,128)(2,1)} %copy-done.2, ...), custom_call_target="tpu_custom_call" | custom-call | tf_op jit(solution)/shard_map/pallas_call | solution.py:57
  226.5 8.1 %shard_map.146 = bf16[384,384]{1,0:T(8,128)(2,1)} custom-call(bf16[384,1536]{1,0:T(8,128)(2,1)} %refs_0_.7, bf16[384,1536]{1,0:T(8,128)(2,1)} %refs_1_.7, bf16[384,1536]{1,0:T(8,128)(2,1)} %refs_2_.7, bf16[384,768]{1,0:T(8,128)(2,1)} %collective-permute-done.12.refs_3_.refs_4_, bf16[384,768]{1,0:T(8,128)(2,1)} %collective-permute-done.12.refs_3_.refs_4_, ...), custom_call_target="tpu_custom_call" | custom-call | tf_op jit(solution)/shard_map/pallas_call | solution.py:57
  235.4 8.1 %shard_map.147 = bf16[384,384]{1,0:T(8,128)(2,1)} custom-call(bf16[384,1536]{1,0:T(8,128)(2,1)} %refs_0_.7, bf16[384,1536]{1,0:T(8,128)(2,1)} %refs_1_.7, bf16[384,1536]{1,0:T(8,128)(2,1)} %refs_2_.7, bf16[384,768]{1,0:T(8,128)(2,1)} %collective-permute-done.15.refs_3_.refs_4_, bf16[384,768]{1,0:T(8,128)(2,1)} %collective-permute-done.15.refs_3_.refs_4_, ...), custom_call_target="tpu_custom_call" | custom-call | tf_op jit(solution)/shard_map/pallas_call | solution.py:57
  244.3 8.1 %shard_map.148 = bf16[384,384]{1,0:T(8,128)(2,1)} custom-call(bf16[384,1536]{1,0:T(8,128)(2,1)} %refs_0_.7, bf16[384,1536]{1,0:T(8,128)(2,1)} %refs_1_.7, bf16[384,1536]{1,0:T(8,128)(2,1)} %refs_2_.7, bf16[384,768]{1,0:T(8,128)(2,1)} %collective-permute-done.18.refs_3_.refs_4_, bf16[384,768]{1,0:T(8,128)(2,1)} %collective-permute-done.18.refs_3_.refs_4_, ...), custom_call_target="tpu_custom_call" | custom-call | tf_op jit(solution)/shard_map/pallas_call | solution.py:57
  252.5 1.2 broadcast_select_fusion.3
  253.8 8.9 %multiply_convert_fusion = bf16[384,3072]{1,0:T(8,128)(2,1)} fusion(bf16[1536,3072]{1,0:T(8,128)(2,1)} %all-gather.2.cloned.1.call-done, f32[3072]{0:T(1024)S(1)} %copy-done.20, bf16[384,384]{1,0:T(8,128)(2,1)S(1)} %get-tuple-element.38, bf16[384,384]{1,0:T(8,128)(2,1)S(1)} %get-tuple-element.37, bf16[384,384]{1,0:T(8,128)(2,1)S(1)} %get-tuple-element.36, ...), kind=kOutput, calls=%fused_computation | convolution fusion | flops 3630956544 | bytes 12988416 | tf_op jit(solution)/shard_map/dot_general | solution.py:147
  (73 shorter events, 8.2 us)
Async XLA Ops:
  6.5 247.2 %all-gather.2.cloned.1.call-start = ((), (), s32[]{:S(2)}) async-start(), calls=%async_computation | async-start | bytes 10027008 | tf_op jit(solution)/shard_map/all_gather | solution.py:92
  9.0 47.8 %copy-start = (bf16[384,1536]{1,0:T(8,128)(2,1)S(1)}, bf16[384,1536]{1,0:T(8,128)(2,1)}, u32[]{:S(2)}) copy-start(bf16[384,1536]{1,0:T(8,128)(2,1)} %refs_1_.7) | copy-start | bytes 3538948
  9.1 47.7 %collective-permute-start = (bf16[384,768]{1,0:T(8,128)(2,1)S(1)}, bf16[384,768]{1,0:T(8,128)(2,1)S(1)}, u32[]{:S(2)}, u32[]{:S(2)}) collective-permute-start(bf16[384,768]{1,0:T(8,128)(2,1)S(1)} %pad_maximum_fusion), channel_id=1, source_target_pairs={{0,8},{1,9},{2,10},{3,11},{4,12},{5,13},{6,14},{7,15},{8,0},{9,1},... | collective-permute-start | bytes 1769480 | tf_op jit(solution)/shard_map/ppermute | solution.py:110
  56.8 117.7 %copy-start.6 = (bf16[384,768]{1,0:T(8,128)(2,1)}, bf16[384,768]{1,0:T(8,128)(2,1)S(1)}, u32[]{:S(2)}) copy-start(bf16[384,768]{1,0:T(8,128)(2,1)S(1)} %collective-permute-done.refs_3_.refs_4_) | copy-start | bytes 1769476
  56.8 69.8 %collective-permute-start.12 = (bf16[384,768]{1,0:T(8,128)(2,1)S(1)}, bf16[384,768]{1,0:T(8,128)(2,1)}, u32[]{:S(2)}, u32[]{:S(2)}) collective-permute-start(bf16[384,768]{1,0:T(8,128)(2,1)S(1)} %pad_maximum_fusion.1), channel_id=1, source_target_pairs={{0,8},{1,9},{2,10},{3,11},{4,12},{5,13},{6,14},{7,15},{8,0},{9,1},... | collective-permute-start | bytes 1769480 | tf_op jit(solution)/shard_map/ppermute | solution.py:110
  56.8 117.7 %collective-permute-start.1 = (bf16[384,1536]{1,0:T(8,128)(2,1)S(1)}, bf16[384,1536]{1,0:T(8,128)(2,1)S(1)}, u32[]{:S(2)}, u32[]{:S(2)}) collective-permute-start(bf16[384,1536]{1,0:T(8,128)(2,1)S(1)} %copy-done), channel_id=1, source_target_pairs={{0,1},{1,2},{2,3},{3,4},{4,5},{5,6},{6,7},{8,9},{9,10},{10,11},{11... | collective-permute-start | bytes 3538952 | tf_op jit(solution)/shard_map/ppermute | solution.py:90
  60.3 116.6 %collective-permute-start.2 = (bf16[384,1536]{1,0:T(8,128)(2,1)S(1)}, bf16[384,1536]{1,0:T(8,128)(2,1)S(1)}, u32[]{:S(2)}, u32[]{:S(2)}) collective-permute-start(bf16[384,1536]{1,0:T(8,128)(2,1)S(1)} %copy-done.1), channel_id=1, source_target_pairs={{0,1},{1,2},{2,3},{3,4},{4,5},{5,6},{6,7},{8,9},{9,10},{10,11},{11... | collective-permute-start | bytes 3538952 | tf_op jit(solution)/shard_map/ppermute | solution.py:90
  62.3 117.9 %collective-permute-start.3 = (bf16[384,1536]{1,0:T(8,128)(2,1)S(1)}, bf16[384,1536]{1,0:T(8,128)(2,1)S(1)}, u32[]{:S(2)}, u32[]{:S(2)}) collective-permute-start(bf16[384,1536]{1,0:T(8,128)(2,1)S(1)} %copy-done), channel_id=1, source_target_pairs={{1,0},{2,1},{3,2},{4,3},{5,4},{6,5},{7,6},{9,8},{10,9},{11,10},{12... | collective-permute-start | bytes 3538952 | tf_op jit(solution)/shard_map/ppermute | solution.py:90
  64.7 119.0 %copy-start.16 = (s32[12,2]{0,1:T(2,128)S(1)}, s32[12,2]{0,1:T(2,128)}, u32[]{:S(2)}) copy-start(s32[12,2]{0,1:T(2,128)} %param.19) | copy-start | bytes 292
  64.7 146.4 %copy-start.18 = (s32[6]{0:T(128)S(1)}, s32[6]{0:T(128)}, u32[]{:S(2)}) copy-start(s32[6]{0:T(128)} %constant.7.clone) | copy-start | bytes 76
  64.7 146.4 %copy-start.19 = (s32[6]{0:T(128)S(1)}, s32[6]{0:T(128)}, u32[]{:S(2)}) copy-start(s32[6]{0:T(128)} %constant.8.clone) | copy-start | bytes 76
  126.6 18.9 %collective-permute-start.15 = (bf16[384,768]{1,0:T(8,128)(2,1)S(1)}, bf16[384,768]{1,0:T(8,128)(2,1)}, u32[]{:S(2)}, u32[]{:S(2)}) collective-permute-start(bf16[384,768]{1,0:T(8,128)(2,1)S(1)} %pad_maximum_fusion.2), channel_id=1, source_target_pairs={{0,8},{1,9},{2,10},{3,11},{4,12},{5,13},{6,14},{7,15},{8,0},{9,1},... | collective-permute-start | bytes 1769480 | tf_op jit(solution)/shard_map/ppermute | solution.py:110
  126.6 57.2 %collective-permute-start.4 = (bf16[384,1536]{1,0:T(8,128)(2,1)S(1)}, bf16[384,1536]{1,0:T(8,128)(2,1)S(1)}, u32[]{:S(2)}, u32[]{:S(2)}) collective-permute-start(bf16[384,1536]{1,0:T(8,128)(2,1)S(1)} %copy-done.1), channel_id=1, source_target_pairs={{1,0},{2,1},{3,2},{4,3},{5,4},{6,5},{7,6},{9,8},{10,9},{11,10},{12... | collective-permute-start | bytes 3538952 | tf_op jit(solution)/shard_map/ppermute | solution.py:90
  145.5 3.7 %collective-permute-start.7 = (s32[1]{0:T(128)}, s32[1]{0:T(128)}, u32[]{:S(2)}, u32[]{:S(2)}) collective-permute-start(s32[1]{0:T(128)} %param.18), channel_id=1, source_target_pairs={{0,8},{1,9},{2,10},{3,11},{4,12},{5,13},{6,14},{7,15},{8,0},{9,1},... | collective-permute-start | bytes 20 | tf_op jit(solution)/shard_map/ppermute | solution.py:110
  149.2 8.0 %collective-permute-start.8 = (s32[1]{0:T(128)}, s32[1]{0:T(128)}, u32[]{:S(2)}, u32[]{:S(2)}) collective-permute-start(s32[1]{0:T(128)} %param.18), channel_id=1, source_target_pairs={{0,1},{1,2},{2,3},{3,4},{4,5},{5,6},{6,7},{8,9},{9,10},{10,11},{11... | collective-permute-start | bytes 20 | tf_op jit(solution)/shard_map/ppermute | solution.py:90
  157.2 6.2 %collective-permute-start.9 = (s32[1]{0:T(128)}, s32[1]{0:T(128)}, u32[]{:S(2)}, u32[]{:S(2)}) collective-permute-start(s32[1]{0:T(128)} %param.18), channel_id=1, source_target_pairs={{1,0},{2,1},{3,2},{4,3},{5,4},{6,5},{7,6},{9,8},{10,9},{11,10},{12... | collective-permute-start | bytes 20 | tf_op jit(solution)/shard_map/ppermute | solution.py:90
  163.4 3.4 %collective-permute-start.10 = (s32[1]{0:T(128)}, s32[1]{0:T(128)}, u32[]{:S(2)}, u32[]{:S(2)}) collective-permute-start(s32[1]{0:T(128)} %collective-permute-done.7), channel_id=1, source_target_pairs={{0,1},{1,2},{2,3},{3,4},{4,5},{5,6},{6,7},{8,9},{9,10},{10,11},{11... | collective-permute-start | bytes 20 | tf_op jit(solution)/shard_map/ppermute | solution.py:90
  166.7 5.8 %collective-permute-start.11 = (s32[1]{0:T(128)}, s32[1]{0:T(128)}, u32[]{:S(2)}, u32[]{:S(2)}) collective-permute-start(s32[1]{0:T(128)} %collective-permute-done.7), channel_id=1, source_target_pairs={{1,0},{2,1},{3,2},{4,3},{5,4},{6,5},{7,6},{9,8},{10,9},{11,10},{12... | collective-permute-start | bytes 20 | tf_op jit(solution)/shard_map/ppermute | solution.py:90
  172.6 14.5 %collective-permute-start.5 = (bf16[384,768]{1,0:T(8,128)(2,1)S(1)}, bf16[384,768]{1,0:T(8,128)(2,1)S(1)}, u32[]{:S(2)}, u32[]{:S(2)}) collective-permute-start(bf16[384,768]{1,0:T(8,128)(2,1)S(1)} %collective-permute-done.refs_3_.refs_4_), channel_id=1, source_target_pairs={{0,1},{1,2},{2,3},{3,4},{4,5},{5,6},{6,7},{8,9},{9,10},{10,11},{11... | collective-permute-start | bytes 1769480 | tf_op jit(solution)/shard_map/ppermute | solution.py:90
  174.5 43.1 %copy-start.2 = (bf16[384,1536]{1,0:T(8,128)(2,1)}, bf16[384,1536]{1,0:T(8,128)(2,1)S(1)}, u32[]{:S(2)}) copy-start(bf16[384,1536]{1,0:T(8,128)(2,1)S(1)} %collective-permute-done.1.refs_5_) | copy-start | bytes 3538948
  174.5 14.8 %collective-permute-start.6 = (bf16[384,768]{1,0:T(8,128)(2,1)S(1)}, bf16[384,768]{1,0:T(8,128)(2,1)S(1)}, u32[]{:S(2)}, u32[]{:S(2)}) collective-permute-start(bf16[384,768]{1,0:T(8,128)(2,1)S(1)} %collective-permute-done.refs_3_.refs_4_), channel_id=1, source_target_pairs={{1,0},{2,1},{3,2},{4,3},{5,4},{6,5},{7,6},{9,8},{10,9},{11,10},{12... | collective-permute-start | bytes 1769480 | tf_op jit(solution)/shard_map/ppermute | solution.py:90
  177.0 29.6 %collective-permute-start.18 = (bf16[384,768]{1,0:T(8,128)(2,1)S(1)}, bf16[384,768]{1,0:T(8,128)(2,1)}, u32[]{:S(2)}, u32[]{:S(2)}) collective-permute-start(bf16[384,768]{1,0:T(8,128)(2,1)S(1)} %pad_maximum_fusion.3), channel_id=1, source_target_pairs={{0,8},{1,9},{2,10},{3,11},{4,12},{5,13},{6,14},{7,15},{8,0},{9,1},... | collective-permute-start | bytes 1769480 | tf_op jit(solution)/shard_map/ppermute | solution.py:110
  180.2 28.2 %collective-permute-start.13 = (bf16[384,768]{1,0:T(8,128)(2,1)}, bf16[384,768]{1,0:T(8,128)(2,1)S(1)}, u32[]{:S(2)}, u32[]{:S(2)}) collective-permute-start(bf16[384,768]{1,0:T(8,128)(2,1)} %collective-permute-done.12.refs_3_.refs_4_), channel_id=1, source_target_pairs={{0,1},{1,2},{2,3},{3,4},{4,5},{5,6},{6,7},{8,9},{9,10},{10,11},{11... | collective-permute-start | bytes 1769480 | tf_op jit(solution)/shard_map/ppermute | solution.py:90
  183.7 41.9 %collective-permute-start.14 = (bf16[384,768]{1,0:T(8,128)(2,1)}, bf16[384,768]{1,0:T(8,128)(2,1)S(1)}, u32[]{:S(2)}, u32[]{:S(2)}) collective-permute-start(bf16[384,768]{1,0:T(8,128)(2,1)} %collective-permute-done.12.refs_3_.refs_4_), channel_id=1, source_target_pairs={{1,0},{2,1},{3,2},{4,3},{5,4},{6,5},{7,6},{9,8},{10,9},{11,10},{12... | collective-permute-start | bytes 1769480 | tf_op jit(solution)/shard_map/ppermute | solution.py:90
  187.1 47.4 %collective-permute-start.16 = (bf16[384,768]{1,0:T(8,128)(2,1)}, bf16[384,768]{1,0:T(8,128)(2,1)S(1)}, u32[]{:S(2)}, u32[]{:S(2)}) collective-permute-start(bf16[384,768]{1,0:T(8,128)(2,1)} %collective-permute-done.15.refs_3_.refs_4_), channel_id=1, source_target_pairs={{0,1},{1,2},{2,3},{3,4},{4,5},{5,6},{6,7},{8,9},{9,10},{10,11},{11... | collective-permute-start | bytes 1769480 | tf_op jit(solution)/shard_map/ppermute | solution.py:90
  189.4 45.2 %collective-permute-start.17 = (bf16[384,768]{1,0:T(8,128)(2,1)}, bf16[384,768]{1,0:T(8,128)(2,1)}, u32[]{:S(2)}, u32[]{:S(2)}) collective-permute-start(bf16[384,768]{1,0:T(8,128)(2,1)} %collective-permute-done.15.refs_3_.refs_4_), channel_id=1, source_target_pairs={{1,0},{2,1},{3,2},{4,3},{5,4},{6,5},{7,6},{9,8},{10,9},{11,10},{12... | collective-permute-start | bytes 1769480 | tf_op jit(solution)/shard_map/ppermute | solution.py:90
  206.5 37.0 %collective-permute-start.19 = (bf16[384,768]{1,0:T(8,128)(2,1)}, bf16[384,768]{1,0:T(8,128)(2,1)S(1)}, u32[]{:S(2)}, u32[]{:S(2)}) collective-permute-start(bf16[384,768]{1,0:T(8,128)(2,1)} %collective-permute-done.18.refs_3_.refs_4_), channel_id=1, source_target_pairs={{0,1},{1,2},{2,3},{3,4},{4,5},{5,6},{6,7},{8,9},{9,10},{10,11},{11... | collective-permute-start | bytes 1769480 | tf_op jit(solution)/shard_map/ppermute | solution.py:90
  208.5 17.2 %copy-start.9 = (bf16[384,768]{1,0:T(8,128)(2,1)}, bf16[384,768]{1,0:T(8,128)(2,1)S(1)}, u32[]{:S(2)}) copy-start(bf16[384,768]{1,0:T(8,128)(2,1)S(1)} %collective-permute-done.13.refs_9_.refs_10_) | copy-start | bytes 1769476
  208.5 35.0 %collective-permute-start.20 = (bf16[384,768]{1,0:T(8,128)(2,1)}, bf16[384,768]{1,0:T(8,128)(2,1)}, u32[]{:S(2)}, u32[]{:S(2)}) collective-permute-start(bf16[384,768]{1,0:T(8,128)(2,1)} %collective-permute-done.18.refs_3_.refs_4_), channel_id=1, source_target_pairs={{1,0},{2,1},{3,2},{4,3},{5,4},{6,5},{7,6},{9,8},{10,9},{11,10},{12... | collective-permute-start | bytes 1769480 | tf_op jit(solution)/shard_map/ppermute | solution.py:90
  244.3 8.2 %copy-start.14 = (bf16[384,384]{1,0:T(8,128)(2,1)S(1)}, bf16[384,384]{1,0:T(8,128)(2,1)}, u32[]{:S(2)}) copy-start(bf16[384,384]{1,0:T(8,128)(2,1)} %shard_map.146) | copy-start | bytes 884740
  244.3 8.2 %copy-start.15 = (bf16[384,384]{1,0:T(8,128)(2,1)S(1)}, bf16[384,384]{1,0:T(8,128)(2,1)}, u32[]{:S(2)}) copy-start(bf16[384,384]{1,0:T(8,128)(2,1)} %shard_map.147) | copy-start | bytes 884740
  244.3 8.2 %copy-start.17 = (pred[384]{0:T(512)(128)(4,1)S(1)}, pred[384]{0:T(512)(128)(4,1)}, u32[]{:S(2)}) copy-start(pred[384]{0:T(512)(128)(4,1)} %iota_compare_fusion.1) | copy-start | bytes 1156
  (11 other events, 40.2 us)
Sparse Core Ops, SparseCore 0:
  9.6 127.9 all-gather.1
where the time goes:
time: 273 us; the launch traced here: 270 us
  waiting for transfers between devices  149 us (55%)
  starting transfers between devices  52.7 us (19%)
  Pallas kernels  32.3 us (12%)
  between operations  14.6 us (5%)
  matrix products  8.91 us (3%)
  local copies, waits for them, and re-layouts  8.11 us (3%)
  other arithmetic  3.49 us (1%)
    ppermute x5, waiting for transfers between devices, on_device(): lax.ppermute((own, tile_lengths), 'seq', pairs)  139 us
    pallas_call x4, Pallas kernels, group_attention(): pl.pallas_call(kernel, grid=(group_heads,), in_specs=in_specs, out_specs=...  32.3 us
    ppermute x8, starting transfers between devices, on_device(): lax.ppermute(x, 'seq', to_left)  30.6 us
    ppermute x8, starting transfers between devices, on_device(): lax.ppermute(x, 'seq', to_right)  18.7 us
    dot_general x1, matrix products, on_device(): jnp.dot(attended_all, weight_all, preferred_element_type=jnp.float32)  8.91 us
    ppermute x8, waiting for transfers between devices, on_device(): lax.ppermute(x, 'seq', to_right)  7.54 us
  transfers between devices with their start and end apart: 22, of which 9 were waited for; matrix products, arithmetic and copies ran while one was open for 3% of the time, Pallas kernels for 12%

commit v1 on v0

--- a/solution.py
+++ b/solution.py
@@ -6,12 +6,13 @@
 from jax.experimental import pallas as pl
 from jax.sharding import PartitionSpec as P
 
+
 TW = 8
 GROUPS = 4
 
 
 def group_attention(queries, slots, usable, head_base, group_heads, head_dim, score_scale):
-    tile_rows, feat_width = queries.shape
+    tile_rows, _ = queries.shape
     count = len(slots)
 
     def kernel(*refs):
@@ -90,13 +91,19 @@
     sideways = lambda x: (lax.ppermute(x, "seq", to_right), lax.ppermute(x, "seq", to_left))
 
     weight_all = lax.all_gather(out_weight, "seq", axis=0, tiled=True)
-    (left_k, left_v, left_len), (right_k, right_v, right_len) = sideways(
-        (keys, values, tile_lengths)
-    )
     verticals = vertical_parts(devices, grid_rows)
+    vert_lens = [lax.ppermute(tile_lengths, "seq", pairs) for pairs in verticals]
+    column_lens = jnp.concatenate([tile_lengths] + vert_lens)
+    left_lens, right_lens = sideways(column_lens)
+    (left_k, left_v), (right_k, right_v) = sideways((keys, values))
 
     positions = jnp.arange(tile_rows, dtype=jnp.int32)
     query_real = positions < tile_lengths[0]
+    rows = [0] + [1] * len(verticals)
+    far_rows = jnp.array(rows * 3, jnp.int32)
+    far_cols = jnp.array([0] * len(rows) + [1] * (2 * len(rows)), jnp.int32)
+    length_stack = jnp.concatenate([column_lens, left_lens, right_lens])
+    key_real = positions[None, :] < length_stack[:, None]
 
     def chunk(x, g):
         return lax.slice_in_dim(x, g * group_width, (g + 1) * group_width, axis=1)
@@ -107,40 +114,21 @@
         own = jnp.concatenate([chunk(keys, g), chunk(values, g)], axis=1)
         if previous is not None:
             own, _ = lax.optimization_barrier((own, previous))
-        got = [lax.ppermute((own, tile_lengths), "seq", pairs) for pairs in verticals]
+        got = [lax.ppermute(own, "seq", pairs) for pairs in verticals]
         if got:
-            previous = got[-1][0]
+            previous = got[-1]
         forwarded = [sideways(item) for item in got]
         base = g * group_heads
         slots = [(keys, values, base, base)]
-        lengths = [tile_lengths]
-        rows = [0]
-        cols = [0]
-        for item in got:
-            slots.append((item[0], item[0], 0, group_heads))
-            lengths.append(item[1])
-            rows.append(1)
-            cols.append(0)
-        slots += [(left_k, left_v, base, base), (right_k, right_v, base, base)]
-        lengths += [left_len, right_len]
-        rows += [0, 0]
-        cols += [1, 1]
-        for from_left, from_right in forwarded:
-            slots += [(from_left[0], from_left[0], 0, group_heads),
-                      (from_right[0], from_right[0], 0, group_heads)]
-            lengths += [from_left[1], from_right[1]]
-            rows += [1, 1]
-            cols += [1, 1]
-        length_stack = jnp.concatenate(lengths)
-        key_real = positions[None, :] < length_stack[:, None]
-        far_rows = jnp.array(rows, jnp.int32)
-        far_cols = jnp.array(cols, jnp.int32)
+        slots += [(item, item, 0, group_heads) for item in got]
+        slots += [(left_k, left_v, base, base)]
+        slots += [(item[0], item[0], 0, group_heads) for item in forwarded]
+        slots += [(right_k, right_v, base, base)]
+        slots += [(item[1], item[1], 0, group_heads) for item in forwarded]
         reach = lax.slice_in_dim(head_windows, base, base + group_heads, axis=0)
         window = (far_rows[None, :] <= reach[:, 0:1]) & (far_cols[None, :] <= reach[:, 1:2])
         usable = key_real[None, :, :] & window[:, :, None]
-        attended = group_attention(
-            queries, slots, usable, base, group_heads, head_dim, score_scale
-        )
+        attended = group_attention(queries, slots, usable, base, group_heads, head_dim, score_scale)
         outputs.append(jnp.where(query_real[:, None], attended, 0))
 
     attended_all = jnp.concatenate(outputs, axis=1)
@@ -158,6 +146,7 @@
         P("seq", None),
         P("groups"),
     )
+
     return jax.shard_map(
         on_device, mesh=mesh, in_specs=placed, out_specs=P(("groups", "seq"), None), check_vma=False
     )

time: 273 us -> 257 us (0.941)
  starting transfers between devices: 52.7 us -> 40 us
  local copies, waits for them, and re-layouts: 8.11 us -> 4.32 us
    ppermute x8 -> x7, waiting for transfers between devices: 2.09 us -> 18.6 us  [on_device(): lax.ppermute(x, 'seq', to_left)]
    ppermute x8 -> x7, starting transfers between devices: 30.6 us -> 19 us  [on_device(): lax.ppermute(x, 'seq', to_left)]
    ppermute x5, waiting for transfers between devices: 139 us -> 131 us  [the longest x4 114 us: on_device(): got = [lax.ppermute(own, 'seq', pairs) for pairs in verticals]]
    ppermute x8 -> x7, waiting for transfers between devices: 7.54 us -> 0.72 us  [on_device(): lax.ppermute(x, 'seq', to_right)]
    concatenate x1 -> x0, local copies, waits for them, and re-layouts: 3.74 us -> none  [on_device(): length_stack = jnp.concatenate(lengths)]
    ppermute x8 -> x7, starting transfers between devices: 18.7 us -> 18.5 us  [on_device(): lax.ppermute(x, 'seq', to_right)]
  transfers between devices with their start and end apart: 22 -> 20, of which waited for: 9 -> 7; matrix products, arithmetic and copies ran while one was open for 3% -> 2% of each run, Pallas kernels for 12% -> 13%
where the time goes in v1:
time: 257 us; the launch traced here: 254 us
  waiting for transfers between devices  151 us (59%)
  starting transfers between devices  40 us (16%)
  Pallas kernels  32.3 us (13%)
  between operations  14.5 us (6%)
  matrix products  8.93 us (3%)
  local copies, waits for them, and re-layouts  4.32 us (2%)
  other arithmetic  3.55 us (1%)
    ppermute x4, waiting for transfers between devices, on_device(): got = [lax.ppermute(own, 'seq', pairs) for pairs in verticals]  114 us
    pallas_call x4, Pallas kernels, group_attention(): pl.pallas_call(kernel, grid=(group_heads,), in_specs=in_specs, out_specs=...  32.3 us
    ppermute x7, starting transfers between devices, on_device(): lax.ppermute(x, 'seq', to_left)  19 us
    ppermute x7, waiting for transfers between devices, on_device(): lax.ppermute(x, 'seq', to_left)  18.6 us
    ppermute x7, starting transfers between devices, on_device(): lax.ppermute(x, 'seq', to_right)  18.5 us
    ppermute x1, waiting for transfers between devices, on_device(): lax.ppermute(tile_lengths, 'seq', pairs)  16.5 us
    dot_general x1, matrix products, on_device(): jnp.dot(attended_all, weight_all, preferred_element_type=jnp.float32)  8.93 us
  transfers between devices with their start and end apart: 20, of which 7 were waited for; matrix products, arithmetic and copies ran while one was open for 2% of the time, Pallas kernels for 13%

profile of v1, /device:TPU:27, one launch (start us, length us, event | category | flops | bytes accessed | tf_op | source)
XLA Modules:
  0.0 254.3 jit_solution(1806228202127602725)
XLA Ops:
  7.3 1.5 fusion.8
  9.3 47.5 %collective-permute-done.refs_3_.refs_4_ = bf16[384,768]{1,0:T(8,128)(2,1)S(1)} collective-permute-done((bf16[384,768]{1,0:T(8,128)(2,1)S(1)}, bf16[384,768]{1,0:T(8,128)(2,1)S(1)}, u32[]{:S(2)}, u32[]{:S(2)}) %collective-permute-start) | collective-permute-done | bytes 589856 | tf_op jit(solution)/shard_map/ppermute | solution.py:117
  56.8 3.5 %collective-permute-start.1 = (bf16[384,1536]{1,0:T(8,128)(2,1)S(1)}, bf16[384,1536]{1,0:T(8,128)(2,1)S(1)}, u32[]{:S(2)}, u32[]{:S(2)}) collective-permute-start(bf16[384,1536]{1,0:T(8,128)(2,1)S(1)} %copy-done), channel_id=1, source_target_pairs={{0,1},{1,2},{2,3},{3,4},{4,5},{5,6},{6,7},{8,9},{9,10},{10,11},{11... | collective-permute-start | bytes 3538952 | tf_op jit(solution)/shard_map/ppermute | solution.py:91
  60.3 1.9 collective-permute-start.2
  62.3 2.4 collective-permute-start.4
  64.8 61.8 %collective-permute-done.10.refs_3_.refs_4_ = bf16[384,768]{1,0:T(8,128)(2,1)} collective-permute-done((bf16[384,768]{1,0:T(8,128)(2,1)S(1)}, bf16[384,768]{1,0:T(8,128)(2,1)}, u32[]{:S(2)}, u32[]{:S(2)}) %collective-permute-start.10) | collective-permute-done | bytes 589856 | tf_op jit(solution)/shard_map/ppermute | solution.py:117
  126.6 2.4 collective-permute-start.7
  128.9 16.5 %collective-permute-done.7 = s32[1]{0:T(128)} collective-permute-done((s32[1]{0:T(128)}, s32[1]{0:T(128)}, u32[]{:S(2)}, u32[]{:S(2)}) %collective-permute-start.7) | collective-permute-done | bytes 36 | tf_op jit(solution)/shard_map/ppermute | solution.py:95
  145.5 2.7 %collective-permute-start.5 = (bf16[384,1536]{1,0:T(8,128)(2,1)S(1)}, bf16[384,1536]{1,0:T(8,128)(2,1)S(1)}, u32[]{:S(2)}, u32[]{:S(2)}) collective-permute-start(bf16[384,1536]{1,0:T(8,128)(2,1)S(1)} %copy-done.1), channel_id=1, source_target_pairs={{1,0},{2,1},{3,2},{4,3},{5,4},{6,5},{7,6},{9,8},{10,9},{11,10},{12... | collective-permute-start | bytes 3538952 | tf_op jit(solution)/shard_map/ppermute | solution.py:91
  149.6 2.8 %collective-permute-start.8 = (s32[2]{0:T(128)S(1)}, s32[2]{0:T(128)S(1)}, u32[]{:S(2)}, u32[]{:S(2)}) collective-permute-start(s32[2]{0:T(128)S(1)} %pad_add_fusion), channel_id=1, source_target_pairs={{0,1},{1,2},{2,3},{3,4},{4,5},{5,6},{6,7},{8,9},{9,10},{10,11},{11... | collective-permute-start | bytes 32 | tf_op jit(solution)/shard_map/ppermute | solution.py:91
  153.1 4.6 %collective-permute-start.9 = (s32[2]{0:T(128)S(1)}, s32[2]{0:T(128)S(1)}, u32[]{:S(2)}, u32[]{:S(2)}) collective-permute-start(s32[2]{0:T(128)S(1)} %pad_add_fusion), channel_id=1, source_target_pairs={{1,0},{2,1},{3,2},{4,3},{5,4},{6,5},{7,6},{9,8},{10,9},{11,10},{12... | collective-permute-start | bytes 32 | tf_op jit(solution)/shard_map/ppermute | solution.py:91
  157.7 5.6 %collective-permute-done.9 = s32[2]{0:T(128)S(1)} collective-permute-done((s32[2]{0:T(128)S(1)}, s32[2]{0:T(128)S(1)}, u32[]{:S(2)}, u32[]{:S(2)}) %collective-permute-start.9) | collective-permute-done | bytes 40 | tf_op jit(solution)/shard_map/ppermute | solution.py:91
  163.3 1.9 collective-permute-start.3
  165.3 2.4 collective-permute-start.6
  167.8 3.2 %collective-permute-start.11 = (bf16[384,768]{1,0:T(8,128)(2,1)}, bf16[384,768]{1,0:T(8,128)(2,1)S(1)}, u32[]{:S(2)}, u32[]{:S(2)}) collective-permute-start(bf16[384,768]{1,0:T(8,128)(2,1)} %collective-permute-done.10.refs_3_.refs_4_), channel_id=1, source_target_pairs={{0,1},{1,2},{2,3},{3,4},{4,5},{5,6},{6,7},{8,9},{9,10},{10,11},{11... | collective-permute-start | bytes 1769480 | tf_op jit(solution)/shard_map/ppermute | solution.py:91
  171.2 2.5 collective-permute-start.12
  173.7 3.1 %collective-permute-start.14 = (bf16[384,768]{1,0:T(8,128)(2,1)}, bf16[384,768]{1,0:T(8,128)(2,1)S(1)}, u32[]{:S(2)}, u32[]{:S(2)}) collective-permute-start(bf16[384,768]{1,0:T(8,128)(2,1)} %collective-permute-done.13.refs_3_.refs_4_), channel_id=1, source_target_pairs={{0,1},{1,2},{2,3},{3,4},{4,5},{5,6},{6,7},{8,9},{9,10},{10,11},{11... | collective-permute-start | bytes 1769480 | tf_op jit(solution)/shard_map/ppermute | solution.py:91
  176.8 12.9 %collective-permute-done.6.refs_11_.refs_12_ = bf16[384,768]{1,0:T(8,128)(2,1)S(1)} collective-permute-done((bf16[384,768]{1,0:T(8,128)(2,1)S(1)}, bf16[384,768]{1,0:T(8,128)(2,1)S(1)}, u32[]{:S(2)}, u32[]{:S(2)}) %collective-permute-start.6) | collective-permute-done | bytes 589856 | tf_op jit(solution)/shard_map/ppermute | solution.py:91
  189.8 1.9 collective-permute-start.15
  191.7 4.8 %collective-permute-done.16.refs_3_.refs_4_ = bf16[384,768]{1,0:T(8,128)(2,1)} collective-permute-done((bf16[384,768]{1,0:T(8,128)(2,1)S(1)}, bf16[384,768]{1,0:T(8,128)(2,1)}, u32[]{:S(2)}, u32[]{:S(2)}) %collective-permute-start.16) | collective-permute-done | bytes 589856 | tf_op jit(solution)/shard_map/ppermute | solution.py:117
  196.5 2.1 collective-permute-start.17
  198.6 2.4 collective-permute-start.18
  201.7 0.7 and_convert_fusion.3
  202.5 8.0 %shard_map.91 = bf16[384,384]{1,0:T(8,128)(2,1)} custom-call(bf16[384,1536]{1,0:T(8,128)(2,1)} %refs_0_.7, bf16[384,1536]{1,0:T(8,128)(2,1)} %refs_1_.7, bf16[384,1536]{1,0:T(8,128)(2,1)} %refs_2_.7, bf16[384,768]{1,0:T(8,128)(2,1)} %copy-done.6, bf16[384,768]{1,0:T(8,128)(2,1)} %copy-done.6, bf16[384,1536]{1,0:T(8,128)(2,1)} %copy-done.2, ...), custom_call_target="tpu_custom_call" | custom-call | tf_op jit(solution)/shard_map/pallas_call | solution.py:58
  210.5 0.8 copy-done.12
  211.3 8.0 %shard_map.92 = bf16[384,384]{1,0:T(8,128)(2,1)} custom-call(bf16[384,1536]{1,0:T(8,128)(2,1)} %refs_0_.7, bf16[384,1536]{1,0:T(8,128)(2,1)} %refs_1_.7, bf16[384,1536]{1,0:T(8,128)(2,1)} %refs_2_.7, bf16[384,768]{1,0:T(8,128)(2,1)} %collective-permute-done.10.refs_3_.refs_4_, bf16[384,768]{1,0:T(8,128)(2,1)} %collective-permute-done.10.refs_3_.refs_4_, ...), custom_call_target="tpu_custom_call" | custom-call | tf_op jit(solution)/shard_map/pallas_call | solution.py:58
  219.4 0.8 copy-done.11
  220.2 8.1 %shard_map.93 = bf16[384,384]{1,0:T(8,128)(2,1)} custom-call(bf16[384,1536]{1,0:T(8,128)(2,1)} %refs_0_.7, bf16[384,1536]{1,0:T(8,128)(2,1)} %refs_1_.7, bf16[384,1536]{1,0:T(8,128)(2,1)} %refs_2_.7, bf16[384,768]{1,0:T(8,128)(2,1)} %collective-permute-done.13.refs_3_.refs_4_, bf16[384,768]{1,0:T(8,128)(2,1)} %collective-permute-done.13.refs_3_.refs_4_, ...), custom_call_target="tpu_custom_call" | custom-call | tf_op jit(solution)/shard_map/pallas_call | solution.py:58
  228.3 0.8 copy-done.10
  229.1 8.2 %shard_map.94 = bf16[384,384]{1,0:T(8,128)(2,1)} custom-call(bf16[384,1536]{1,0:T(8,128)(2,1)} %refs_0_.7, bf16[384,1536]{1,0:T(8,128)(2,1)} %refs_1_.7, bf16[384,1536]{1,0:T(8,128)(2,1)} %refs_2_.7, bf16[384,768]{1,0:T(8,128)(2,1)} %collective-permute-done.16.refs_3_.refs_4_, bf16[384,768]{1,0:T(8,128)(2,1)} %collective-permute-done.16.refs_3_.refs_4_, ...), custom_call_target="tpu_custom_call" | custom-call | tf_op jit(solution)/shard_map/pallas_call | solution.py:58
  237.3 1.2 broadcast_select_fusion.3
  238.5 8.9 %multiply_convert_fusion = bf16[384,3072]{1,0:T(8,128)(2,1)} fusion(bf16[1536,3072]{1,0:T(8,128)(2,1)} %all-gather.2.cloned.1.call-done, f32[3072]{0:T(1024)S(1)} %copy-done.19, bf16[384,384]{1,0:T(8,128)(2,1)S(1)} %get-tuple-element.38, bf16[384,384]{1,0:T(8,128)(2,1)S(1)} %get-tuple-element.37, bf16[384,384]{1,0:T(8,128)(2,1)S(1)} %get-tuple-element.36, ...), kind=kOutput, calls=%fused_computation | convolution fusion | flops 3630956544 | bytes 12988416 | tf_op jit(solution)/shard_map/dot_general | solution.py:135
  (68 shorter events, 3.8 us)
Async XLA Ops:
  6.5 232.0 %all-gather.2.cloned.1.call-start = ((), (), s32[]{:S(2)}) async-start(), calls=%async_computation | async-start | bytes 10027008 | tf_op jit(solution)/shard_map/all_gather | solution.py:93
  9.0 47.8 %copy-start = (bf16[384,1536]{1,0:T(8,128)(2,1)S(1)}, bf16[384,1536]{1,0:T(8,128)(2,1)}, u32[]{:S(2)}) copy-start(bf16[384,1536]{1,0:T(8,128)(2,1)} %refs_1_.7) | copy-start | bytes 3538948
  9.1 47.7 %collective-permute-start = (bf16[384,768]{1,0:T(8,128)(2,1)S(1)}, bf16[384,768]{1,0:T(8,128)(2,1)S(1)}, u32[]{:S(2)}, u32[]{:S(2)}) collective-permute-start(bf16[384,768]{1,0:T(8,128)(2,1)S(1)} %pad_maximum_fusion), channel_id=1, source_target_pairs={{0,8},{1,9},{2,10},{3,11},{4,12},{5,13},{6,14},{7,15},{8,0},{9,1},... | collective-permute-start | bytes 1769480 | tf_op jit(solution)/shard_map/ppermute | solution.py:117
  56.8 108.5 %copy-start.6 = (bf16[384,768]{1,0:T(8,128)(2,1)}, bf16[384,768]{1,0:T(8,128)(2,1)S(1)}, u32[]{:S(2)}) copy-start(bf16[384,768]{1,0:T(8,128)(2,1)S(1)} %collective-permute-done.refs_3_.refs_4_) | copy-start | bytes 1769476
  56.8 69.8 %collective-permute-start.10 = (bf16[384,768]{1,0:T(8,128)(2,1)S(1)}, bf16[384,768]{1,0:T(8,128)(2,1)}, u32[]{:S(2)}, u32[]{:S(2)}) collective-permute-start(bf16[384,768]{1,0:T(8,128)(2,1)S(1)} %pad_maximum_fusion.1), channel_id=1, source_target_pairs={{0,8},{1,9},{2,10},{3,11},{4,12},{5,13},{6,14},{7,15},{8,0},{9,1},... | collective-permute-start | bytes 1769480 | tf_op jit(solution)/shard_map/ppermute | solution.py:117
  56.8 108.4 %collective-permute-start.1 = (bf16[384,1536]{1,0:T(8,128)(2,1)S(1)}, bf16[384,1536]{1,0:T(8,128)(2,1)S(1)}, u32[]{:S(2)}, u32[]{:S(2)}) collective-permute-start(bf16[384,1536]{1,0:T(8,128)(2,1)S(1)} %copy-done), channel_id=1, source_target_pairs={{0,1},{1,2},{2,3},{3,4},{4,5},{5,6},{6,7},{8,9},{9,10},{10,11},{11... | collective-permute-start | bytes 3538952 | tf_op jit(solution)/shard_map/ppermute | solution.py:91
  60.3 107.4 %collective-permute-start.2 = (bf16[384,1536]{1,0:T(8,128)(2,1)S(1)}, bf16[384,1536]{1,0:T(8,128)(2,1)S(1)}, u32[]{:S(2)}, u32[]{:S(2)}) collective-permute-start(bf16[384,1536]{1,0:T(8,128)(2,1)S(1)} %copy-done.1), channel_id=1, source_target_pairs={{0,1},{1,2},{2,3},{3,4},{4,5},{5,6},{6,7},{8,9},{9,10},{10,11},{11... | collective-permute-start | bytes 3538952 | tf_op jit(solution)/shard_map/ppermute | solution.py:91
  62.3 105.5 %collective-permute-start.4 = (bf16[384,1536]{1,0:T(8,128)(2,1)S(1)}, bf16[384,1536]{1,0:T(8,128)(2,1)S(1)}, u32[]{:S(2)}, u32[]{:S(2)}) collective-permute-start(bf16[384,1536]{1,0:T(8,128)(2,1)S(1)} %copy-done), channel_id=1, source_target_pairs={{1,0},{2,1},{3,2},{4,3},{5,4},{6,5},{7,6},{9,8},{10,9},{11,10},{12... | collective-permute-start | bytes 3538952 | tf_op jit(solution)/shard_map/ppermute | solution.py:91
  64.7 106.3 %copy-start.16 = (s32[12,2]{0,1:T(2,128)S(1)}, s32[12,2]{0,1:T(2,128)}, u32[]{:S(2)}) copy-start(s32[12,2]{0,1:T(2,128)} %param.13) | copy-start | bytes 292
  64.7 106.4 %copy-start.17 = (s32[6]{0:T(128)S(1)}, s32[6]{0:T(128)}, u32[]{:S(2)}) copy-start(s32[6]{0:T(128)} %constant.7.clone) | copy-start | bytes 76
  64.7 106.4 %copy-start.18 = (s32[6]{0:T(128)S(1)}, s32[6]{0:T(128)}, u32[]{:S(2)}) copy-start(s32[6]{0:T(128)} %constant.8.clone) | copy-start | bytes 76
  126.6 23.0 %collective-permute-start.13 = (bf16[384,768]{1,0:T(8,128)(2,1)S(1)}, bf16[384,768]{1,0:T(8,128)(2,1)}, u32[]{:S(2)}, u32[]{:S(2)}) collective-permute-start(bf16[384,768]{1,0:T(8,128)(2,1)S(1)} %pad_maximum_fusion.2), channel_id=1, source_target_pairs={{0,8},{1,9},{2,10},{3,11},{4,12},{5,13},{6,14},{7,15},{8,0},{9,1},... | collective-permute-start | bytes 1769480 | tf_op jit(solution)/shard_map/ppermute | solution.py:117
  126.6 18.9 %collective-permute-start.7 = (s32[1]{0:T(128)}, s32[1]{0:T(128)}, u32[]{:S(2)}, u32[]{:S(2)}) collective-permute-start(s32[1]{0:T(128)} %param.12), channel_id=1, source_target_pairs={{0,8},{1,9},{2,10},{3,11},{4,12},{5,13},{6,14},{7,15},{8,0},{9,1},... | collective-permute-start | bytes 20 | tf_op jit(solution)/shard_map/ppermute | solution.py:95
  145.5 25.7 %collective-permute-start.5 = (bf16[384,1536]{1,0:T(8,128)(2,1)S(1)}, bf16[384,1536]{1,0:T(8,128)(2,1)S(1)}, u32[]{:S(2)}, u32[]{:S(2)}) collective-permute-start(bf16[384,1536]{1,0:T(8,128)(2,1)S(1)} %copy-done.1), channel_id=1, source_target_pairs={{1,0},{2,1},{3,2},{4,3},{5,4},{6,5},{7,6},{9,8},{10,9},{11,10},{12... | collective-permute-start | bytes 3538952 | tf_op jit(solution)/shard_map/ppermute | solution.py:91
  149.6 3.5 %collective-permute-start.8 = (s32[2]{0:T(128)S(1)}, s32[2]{0:T(128)S(1)}, u32[]{:S(2)}, u32[]{:S(2)}) collective-permute-start(s32[2]{0:T(128)S(1)} %pad_add_fusion), channel_id=1, source_target_pairs={{0,1},{1,2},{2,3},{3,4},{4,5},{5,6},{6,7},{8,9},{9,10},{10,11},{11... | collective-permute-start | bytes 32 | tf_op jit(solution)/shard_map/ppermute | solution.py:91
  153.1 10.2 %collective-permute-start.9 = (s32[2]{0:T(128)S(1)}, s32[2]{0:T(128)S(1)}, u32[]{:S(2)}, u32[]{:S(2)}) collective-permute-start(s32[2]{0:T(128)S(1)} %pad_add_fusion), channel_id=1, source_target_pairs={{1,0},{2,1},{3,2},{4,3},{5,4},{6,5},{7,6},{9,8},{10,9},{11,10},{12... | collective-permute-start | bytes 32 | tf_op jit(solution)/shard_map/ppermute | solution.py:91
  163.3 10.4 %collective-permute-start.3 = (bf16[384,768]{1,0:T(8,128)(2,1)S(1)}, bf16[384,768]{1,0:T(8,128)(2,1)S(1)}, u32[]{:S(2)}, u32[]{:S(2)}) collective-permute-start(bf16[384,768]{1,0:T(8,128)(2,1)S(1)} %collective-permute-done.refs_3_.refs_4_), channel_id=1, source_target_pairs={{0,1},{1,2},{2,3},{3,4},{4,5},{5,6},{6,7},{8,9},{9,10},{10,11},{11... | collective-permute-start | bytes 1769480 | tf_op jit(solution)/shard_map/ppermute | solution.py:91
  165.3 37.2 %copy-start.2 = (bf16[384,1536]{1,0:T(8,128)(2,1)}, bf16[384,1536]{1,0:T(8,128)(2,1)S(1)}, u32[]{:S(2)}) copy-start(bf16[384,1536]{1,0:T(8,128)(2,1)S(1)} %collective-permute-done.1.refs_5_) | copy-start | bytes 3538948
  165.3 24.5 %collective-permute-start.6 = (bf16[384,768]{1,0:T(8,128)(2,1)S(1)}, bf16[384,768]{1,0:T(8,128)(2,1)S(1)}, u32[]{:S(2)}, u32[]{:S(2)}) collective-permute-start(bf16[384,768]{1,0:T(8,128)(2,1)S(1)} %collective-permute-done.refs_3_.refs_4_), channel_id=1, source_target_pairs={{1,0},{2,1},{3,2},{4,3},{5,4},{6,5},{7,6},{9,8},{10,9},{11,10},{12... | collective-permute-start | bytes 1769480 | tf_op jit(solution)/shard_map/ppermute | solution.py:91
  167.7 28.7 %collective-permute-start.16 = (bf16[384,768]{1,0:T(8,128)(2,1)S(1)}, bf16[384,768]{1,0:T(8,128)(2,1)}, u32[]{:S(2)}, u32[]{:S(2)}) collective-permute-start(bf16[384,768]{1,0:T(8,128)(2,1)S(1)} %pad_maximum_fusion.3), channel_id=1, source_target_pairs={{0,8},{1,9},{2,10},{3,11},{4,12},{5,13},{6,14},{7,15},{8,0},{9,1},... | collective-permute-start | bytes 1769480 | tf_op jit(solution)/shard_map/ppermute | solution.py:117
  167.8 5.9 %copy-start.4 = (bf16[384,1536]{1,0:T(8,128)(2,1)}, bf16[384,1536]{1,0:T(8,128)(2,1)S(1)}, u32[]{:S(2)}) copy-start(bf16[384,1536]{1,0:T(8,128)(2,1)S(1)} %collective-permute-done.4.refs_9_) | copy-start | bytes 3538948
  167.8 30.7 %collective-permute-start.11 = (bf16[384,768]{1,0:T(8,128)(2,1)}, bf16[384,768]{1,0:T(8,128)(2,1)S(1)}, u32[]{:S(2)}, u32[]{:S(2)}) collective-permute-start(bf16[384,768]{1,0:T(8,128)(2,1)} %collective-permute-done.10.refs_3_.refs_4_), channel_id=1, source_target_pairs={{0,1},{1,2},{2,3},{3,4},{4,5},{5,6},{6,7},{8,9},{9,10},{10,11},{11... | collective-permute-start | bytes 1769480 | tf_op jit(solution)/shard_map/ppermute | solution.py:91
  171.2 39.3 %collective-permute-start.12 = (bf16[384,768]{1,0:T(8,128)(2,1)}, bf16[384,768]{1,0:T(8,128)(2,1)S(1)}, u32[]{:S(2)}, u32[]{:S(2)}) collective-permute-start(bf16[384,768]{1,0:T(8,128)(2,1)} %collective-permute-done.10.refs_3_.refs_4_), channel_id=1, source_target_pairs={{1,0},{2,1},{3,2},{4,3},{5,4},{6,5},{7,6},{9,8},{10,9},{11,10},{12... | collective-permute-start | bytes 1769480 | tf_op jit(solution)/shard_map/ppermute | solution.py:91
  173.7 16.0 %copy-start.7 = (bf16[384,768]{1,0:T(8,128)(2,1)}, bf16[384,768]{1,0:T(8,128)(2,1)S(1)}, u32[]{:S(2)}) copy-start(bf16[384,768]{1,0:T(8,128)(2,1)S(1)} %collective-permute-done.3.refs_7_.refs_8_) | copy-start | bytes 1769476
  173.7 45.6 %collective-permute-start.14 = (bf16[384,768]{1,0:T(8,128)(2,1)}, bf16[384,768]{1,0:T(8,128)(2,1)S(1)}, u32[]{:S(2)}, u32[]{:S(2)}) collective-permute-start(bf16[384,768]{1,0:T(8,128)(2,1)} %collective-permute-done.13.refs_3_.refs_4_), channel_id=1, source_target_pairs={{0,1},{1,2},{2,3},{3,4},{4,5},{5,6},{6,7},{8,9},{9,10},{10,11},{11... | collective-permute-start | bytes 1769480 | tf_op jit(solution)/shard_map/ppermute | solution.py:91
  189.8 29.6 %collective-permute-start.15 = (bf16[384,768]{1,0:T(8,128)(2,1)}, bf16[384,768]{1,0:T(8,128)(2,1)}, u32[]{:S(2)}, u32[]{:S(2)}) collective-permute-start(bf16[384,768]{1,0:T(8,128)(2,1)} %collective-permute-done.13.refs_3_.refs_4_), channel_id=1, source_target_pairs={{1,0},{2,1},{3,2},{4,3},{5,4},{6,5},{7,6},{9,8},{10,9},{11,10},{12... | collective-permute-start | bytes 1769480 | tf_op jit(solution)/shard_map/ppermute | solution.py:91
  196.5 31.8 %collective-permute-start.17 = (bf16[384,768]{1,0:T(8,128)(2,1)}, bf16[384,768]{1,0:T(8,128)(2,1)S(1)}, u32[]{:S(2)}, u32[]{:S(2)}) collective-permute-start(bf16[384,768]{1,0:T(8,128)(2,1)} %collective-permute-done.16.refs_3_.refs_4_), channel_id=1, source_target_pairs={{0,1},{1,2},{2,3},{3,4},{4,5},{5,6},{6,7},{8,9},{9,10},{10,11},{11... | collective-permute-start | bytes 1769480 | tf_op jit(solution)/shard_map/ppermute | solution.py:91
  198.5 11.9 %copy-start.9 = (bf16[384,768]{1,0:T(8,128)(2,1)}, bf16[384,768]{1,0:T(8,128)(2,1)S(1)}, u32[]{:S(2)}) copy-start(bf16[384,768]{1,0:T(8,128)(2,1)S(1)} %collective-permute-done.11.refs_7_.refs_8_) | copy-start | bytes 1769476
  198.6 29.7 %collective-permute-start.18 = (bf16[384,768]{1,0:T(8,128)(2,1)}, bf16[384,768]{1,0:T(8,128)(2,1)}, u32[]{:S(2)}, u32[]{:S(2)}) collective-permute-start(bf16[384,768]{1,0:T(8,128)(2,1)} %collective-permute-done.16.refs_3_.refs_4_), channel_id=1, source_target_pairs={{1,0},{2,1},{3,2},{4,3},{5,4},{6,5},{7,6},{9,8},{10,9},{11,10},{12... | collective-permute-start | bytes 1769480 | tf_op jit(solution)/shard_map/ppermute | solution.py:91
  229.1 8.2 %copy-start.13 = (bf16[384,384]{1,0:T(8,128)(2,1)S(1)}, bf16[384,384]{1,0:T(8,128)(2,1)}, u32[]{:S(2)}) copy-start(bf16[384,384]{1,0:T(8,128)(2,1)} %shard_map.91) | copy-start | bytes 884740
  229.1 8.2 %copy-start.14 = (bf16[384,384]{1,0:T(8,128)(2,1)S(1)}, bf16[384,384]{1,0:T(8,128)(2,1)}, u32[]{:S(2)}) copy-start(bf16[384,384]{1,0:T(8,128)(2,1)} %shard_map.92) | copy-start | bytes 884740
  229.1 8.2 %copy-start.15 = (bf16[384,384]{1,0:T(8,128)(2,1)S(1)}, bf16[384,384]{1,0:T(8,128)(2,1)}, u32[]{:S(2)}) copy-start(bf16[384,384]{1,0:T(8,128)(2,1)} %shard_map.93) | copy-start | bytes 884740
  (8 other events, 13.2 us)
Sparse Core Ops, SparseCore 0:
  9.6 127.9 all-gather.1

commit v2 on v1

--- a/solution.py
+++ b/solution.py
@@ -90,11 +90,22 @@
     to_left = [(i + 1, i) for i in range(devices) if i % TW < TW - 1]
     sideways = lambda x: (lax.ppermute(x, "seq", to_right), lax.ppermute(x, "seq", to_left))
 
-    weight_all = lax.all_gather(out_weight, "seq", axis=0, tiled=True)
     verticals = vertical_parts(devices, grid_rows)
-    vert_lens = [lax.ppermute(tile_lengths, "seq", pairs) for pairs in verticals]
-    column_lens = jnp.concatenate([tile_lengths] + vert_lens)
-    left_lens, right_lens = sideways(column_lens)
+    vertical_sources = []
+    for pairs in verticals:
+        table = [-1] * devices
+        for s, r in pairs:
+            table[r] = s
+        vertical_sources.append(table)
+    column_tables = [list(range(devices))] + vertical_sources
+    left_tables = [[t[r - 1] if r % TW > 0 else -1 for r in range(devices)] for t in column_tables]
+    right_tables = [[t[r + 1] if r % TW < TW - 1 else -1 for r in range(devices)] for t in column_tables]
+    tables = jnp.array(column_tables + left_tables + right_tables, jnp.int32)
+    all_lens = lax.all_gather(tile_lengths, "seq", axis=0, tiled=True)
+    slot_source = tables[:, lax.axis_index("seq")]
+    length_stack = jnp.where(slot_source >= 0, all_lens[jnp.maximum(slot_source, 0)], 0)
+    weight_part, _ = lax.optimization_barrier((out_weight, all_lens))
+    weight_all = lax.all_gather(weight_part, "seq", axis=0, tiled=True)
     (left_k, left_v), (right_k, right_v) = sideways((keys, values))
 
     positions = jnp.arange(tile_rows, dtype=jnp.int32)
@@ -102,7 +113,6 @@
     rows = [0] + [1] * len(verticals)
     far_rows = jnp.array(rows * 3, jnp.int32)
     far_cols = jnp.array([0] * len(rows) + [1] * (2 * len(rows)), jnp.int32)
-    length_stack = jnp.concatenate([column_lens, left_lens, right_lens])
     key_real = positions[None, :] < length_stack[:, None]
 
     def chunk(x, g):

time: 257 us -> 254 us (0.988)
  waiting for transfers between devices: 151 us -> 107 us
  starting transfers between devices: 40 us -> 67.2 us
  blocking collectives: 0 us -> 6.49 us
  local copies, waits for them, and re-layouts: 4.32 us -> 8.22 us
  other arithmetic: 3.55 us -> 6.35 us
    ppermute x7 -> x6, starting transfers between devices: 19 us -> 51.5 us  [on_device(): lax.ppermute(x, 'seq', to_left)]
    ppermute x7 -> x6, waiting for transfers between devices: 18.6 us -> 0.02 us  [on_device(): lax.ppermute(x, 'seq', to_left)]
    ppermute x1 -> x0, waiting for transfers between devices: 16.5 us -> none  [on_device(): lax.ppermute(tile_lengths, 'seq', pairs)]
    ppermute x4, waiting for transfers between devices: 114 us -> 107 us  [on_device(): got = [lax.ppermute(own, 'seq', pairs) for pairs in verticals]]
    unnamed x0 -> x1, blocking collectives: none -> 6.49 us
    ppermute x7 -> x6, starting transfers between devices: 18.5 us -> 13.2 us  [on_device(): lax.ppermute(x, 'seq', to_right)]
    concatenate x4, other arithmetic: 0.2 us -> 2.87 us  [on_device(): own = jnp.concatenate([chunk(keys, g), chunk(values, g)], axis=1)]
  transfers between devices with their start and end apart: 20 -> 17, of which waited for: 7 -> 4; matrix products, arithmetic and copies ran while one was open for 2% -> 4% of each run, Pallas kernels for 13% -> 13%
where the time goes in v2:
time: 254 us; the launch traced here: 251 us
  waiting for transfers between devices  107 us (42%)
  starting transfers between devices  67.2 us (26%)
  Pallas kernels  32.4 us (13%)
  between operations  14.4 us (6%)
  matrix products  8.9 us (4%)
  local copies, waits for them, and re-layouts  8.22 us (3%)
  blocking collectives  6.49 us (3%)
  other arithmetic  6.35 us (2%)
    ppermute x4, waiting for transfers between devices, on_device(): got = [lax.ppermute(own, 'seq', pairs) for pairs in verticals]  107 us
    ppermute x6, starting transfers between devices, on_device(): lax.ppermute(x, 'seq', to_left)  51.5 us
    pallas_call x4, Pallas kernels, group_attention(): pl.pallas_call(kernel, grid=(group_heads,), in_specs=in_specs, out_specs=...  32.4 us
    ppermute x6, starting transfers between devices, on_device(): lax.ppermute(x, 'seq', to_right)  13.2 us
    dot_general x1, matrix products, on_device(): jnp.dot(attended_all, weight_all, preferred_element_type=jnp.float32)  8.9 us
    unnamed x1, blocking collectives  6.49 us
  transfers between devices with their start and end apart: 17, of which 4 were waited for; matrix products, arithmetic and copies ran while one was open for 4% of the time, Pallas kernels for 13%

profile of v2, /device:TPU:27, one launch (start us, length us, event | category | flops | bytes accessed | tf_op | source)
XLA Modules:
  0.0 250.7 jit_solution(2751385988284793629)
XLA Ops:
  7.2 1.2 dynamic-slice
  9.2 6.5 %all-reduce = s32[16]{0:T(128)S(1)} all-reduce(s32[16]{0:T(128)S(1)} %dynamic-update-slice), channel_id=1, replica_groups=mesh['groups'=2,'seq'=16] {'seq'}, use_global_device_ids=true, to_apply=%add | all-reduce | flops 16 | bytes 128
  15.7 2.2 fusion.9
  17.9 0.9 fusion.10
  18.8 2.4 collective-permute-start
  21.2 44.5 %collective-permute-done.refs_3_.refs_4_ = bf16[384,768]{1,0:T(8,128)(2,1)} collective-permute-done((bf16[384,768]{1,0:T(8,128)(2,1)S(1)}, bf16[384,768]{1,0:T(8,128)(2,1)}, u32[]{:S(2)}, u32[]{:S(2)}) %collective-permute-start) | collective-permute-done | bytes 589856 | tf_op jit(solution)/shard_map/ppermute | solution.py:127
  65.7 3.7 %collective-permute-start.1 = (bf16[384,1536]{1,0:T(8,128)(2,1)S(1)}, bf16[384,1536]{1,0:T(8,128)(2,1)S(1)}, u32[]{:S(2)}, u32[]{:S(2)}) collective-permute-start(bf16[384,1536]{1,0:T(8,128)(2,1)S(1)} %copy-done), channel_id=1, source_target_pairs={{0,1},{1,2},{2,3},{3,4},{4,5},{5,6},{6,7},{8,9},{9,10},{10,11},{11... | collective-permute-start | bytes 3538952 | tf_op jit(solution)/shard_map/ppermute | solution.py:91
  69.4 1.9 collective-permute-start.2
  71.3 2.4 collective-permute-start.4
  73.7 0.9 pad_maximum_fusion.2
  74.6 44.4 %collective-permute-done.7.refs_3_.refs_4_ = bf16[384,768]{1,0:T(8,128)(2,1)} collective-permute-done((bf16[384,768]{1,0:T(8,128)(2,1)S(1)}, bf16[384,768]{1,0:T(8,128)(2,1)}, u32[]{:S(2)}, u32[]{:S(2)}) %collective-permute-start.7) | collective-permute-done | bytes 589856 | tf_op jit(solution)/shard_map/ppermute | solution.py:127
  119.0 23.6 %collective-permute-start.5 = (bf16[384,1536]{1,0:T(8,128)(2,1)S(1)}, bf16[384,1536]{1,0:T(8,128)(2,1)}, u32[]{:S(2)}, u32[]{:S(2)}) collective-permute-start(bf16[384,1536]{1,0:T(8,128)(2,1)S(1)} %copy-done.1), channel_id=1, source_target_pairs={{1,0},{2,1},{3,2},{4,3},{5,4},{6,5},{7,6},{9,8},{10,9},{11,10},{12... | collective-permute-start | bytes 3538952 | tf_op jit(solution)/shard_map/ppermute | solution.py:91
  142.6 1.9 pad_maximum_fusion.3
  144.5 10.7 %collective-permute-done.10.refs_3_.refs_4_ = bf16[384,768]{1,0:T(8,128)(2,1)} collective-permute-done((bf16[384,768]{1,0:T(8,128)(2,1)}, bf16[384,768]{1,0:T(8,128)(2,1)}, u32[]{:S(2)}, u32[]{:S(2)}) %collective-permute-start.10) | collective-permute-done | bytes 589856 | tf_op jit(solution)/shard_map/ppermute | solution.py:127
  155.2 1.9 collective-permute-start.3
  157.2 5.2 %collective-permute-start.6 = (bf16[384,768]{1,0:T(8,128)(2,1)}, bf16[384,768]{1,0:T(8,128)(2,1)}, u32[]{:S(2)}, u32[]{:S(2)}) collective-permute-start(bf16[384,768]{1,0:T(8,128)(2,1)} %collective-permute-done.refs_3_.refs_4_), channel_id=1, source_target_pairs={{1,0},{2,1},{3,2},{4,3},{5,4},{6,5},{7,6},{9,8},{10,9},{11,10},{12... | collective-permute-start | bytes 1769480 | tf_op jit(solution)/shard_map/ppermute | solution.py:91
  162.3 1.9 collective-permute-start.8
  166.5 4.5 %collective-permute-start.9 = (bf16[384,768]{1,0:T(8,128)(2,1)}, bf16[384,768]{1,0:T(8,128)(2,1)S(1)}, u32[]{:S(2)}, u32[]{:S(2)}) collective-permute-start(bf16[384,768]{1,0:T(8,128)(2,1)} %collective-permute-done.7.refs_3_.refs_4_), channel_id=1, source_target_pairs={{1,0},{2,1},{3,2},{4,3},{5,4},{6,5},{7,6},{9,8},{10,9},{11,10},{12... | collective-permute-start | bytes 1769480 | tf_op jit(solution)/shard_map/ppermute | solution.py:91
  171.0 1.9 collective-permute-start.11
  173.0 12.5 %collective-permute-start.12 = (bf16[384,768]{1,0:T(8,128)(2,1)}, bf16[384,768]{1,0:T(8,128)(2,1)}, u32[]{:S(2)}, u32[]{:S(2)}) collective-permute-start(bf16[384,768]{1,0:T(8,128)(2,1)} %collective-permute-done.10.refs_3_.refs_4_), channel_id=1, source_target_pairs={{1,0},{2,1},{3,2},{4,3},{5,4},{6,5},{7,6},{9,8},{10,9},{11,10},{12... | collective-permute-start | bytes 1769480 | tf_op jit(solution)/shard_map/ppermute | solution.py:91
  185.5 7.1 %collective-permute-done.13.refs_3_.refs_4_ = bf16[384,768]{1,0:T(8,128)(2,1)S(1)} collective-permute-done((bf16[384,768]{1,0:T(8,128)(2,1)}, bf16[384,768]{1,0:T(8,128)(2,1)S(1)}, u32[]{:S(2)}, u32[]{:S(2)}) %collective-permute-start.13) | collective-permute-done | bytes 589856 | tf_op jit(solution)/shard_map/ppermute | solution.py:127
  192.6 1.9 collective-permute-start.14
  194.5 3.3 %collective-permute-start.15 = (bf16[384,768]{1,0:T(8,128)(2,1)S(1)}, bf16[384,768]{1,0:T(8,128)(2,1)}, u32[]{:S(2)}, u32[]{:S(2)}) collective-permute-start(bf16[384,768]{1,0:T(8,128)(2,1)S(1)} %collective-permute-done.13.refs_3_.refs_4_), channel_id=1, source_target_pairs={{1,0},{2,1},{3,2},{4,3},{5,4},{6,5},{7,6},{9,8},{10,9},{11,10},{12... | collective-permute-start | bytes 1769480 | tf_op jit(solution)/shard_map/ppermute | solution.py:91
  198.8 8.1 %shard_map.100 = bf16[384,384]{1,0:T(8,128)(2,1)} custom-call(bf16[384,1536]{1,0:T(8,128)(2,1)} %refs_0_.7, bf16[384,1536]{1,0:T(8,128)(2,1)} %refs_1_.7, bf16[384,1536]{1,0:T(8,128)(2,1)} %refs_2_.7, bf16[384,768]{1,0:T(8,128)(2,1)} %collective-permute-done.refs_3_.refs_4_, bf16[384,768]{1,0:T(8,128)(2,1)} %collective-permute-done.refs_3_.refs_4_, ...), custom_call_target="tpu_custom_call" | custom-call | tf_op jit(solution)/shard_map/pallas_call | solution.py:58
  206.9 0.8 copy-done.6
  207.7 8.1 %shard_map.101 = bf16[384,384]{1,0:T(8,128)(2,1)} custom-call(bf16[384,1536]{1,0:T(8,128)(2,1)} %refs_0_.7, bf16[384,1536]{1,0:T(8,128)(2,1)} %refs_1_.7, bf16[384,1536]{1,0:T(8,128)(2,1)} %refs_2_.7, bf16[384,768]{1,0:T(8,128)(2,1)} %collective-permute-done.7.refs_3_.refs_4_, bf16[384,768]{1,0:T(8,128)(2,1)} %collective-permute-done.7.refs_3_.refs_4_, ...), custom_call_target="tpu_custom_call" | custom-call | tf_op jit(solution)/shard_map/pallas_call | solution.py:58
  215.8 0.8 copy-done.5
  216.6 8.1 %shard_map.102 = bf16[384,384]{1,0:T(8,128)(2,1)} custom-call(bf16[384,1536]{1,0:T(8,128)(2,1)} %refs_0_.7, bf16[384,1536]{1,0:T(8,128)(2,1)} %refs_1_.7, bf16[384,1536]{1,0:T(8,128)(2,1)} %refs_2_.7, bf16[384,768]{1,0:T(8,128)(2,1)} %collective-permute-done.10.refs_3_.refs_4_, bf16[384,768]{1,0:T(8,128)(2,1)} %collective-permute-done.10.refs_3_.refs_4_, ...), custom_call_target="tpu_custom_call" | custom-call | tf_op jit(solution)/shard_map/pallas_call | solution.py:58
  224.8 0.8 copy-done.4
  225.6 8.1 %shard_map.103 = bf16[384,384]{1,0:T(8,128)(2,1)} custom-call(bf16[384,1536]{1,0:T(8,128)(2,1)} %refs_0_.7, bf16[384,1536]{1,0:T(8,128)(2,1)} %refs_1_.7, bf16[384,1536]{1,0:T(8,128)(2,1)} %refs_2_.7, bf16[384,768]{1,0:T(8,128)(2,1)} %copy-done.3, bf16[384,768]{1,0:T(8,128)(2,1)} %copy-done.3, bf16[384,1536]{1,0:T(8,128)(2,1)} %copy-done.2, ...), custom_call_target="tpu_custom_call" | custom-call | tf_op jit(solution)/shard_map/pallas_call | solution.py:58
  233.8 1.2 broadcast_select_fusion.3
  235.0 8.9 %multiply_convert_fusion = bf16[384,3072]{1,0:T(8,128)(2,1)} fusion(bf16[1536,3072]{1,0:T(8,128)(2,1)} %all-gather.2.cloned.1.call-done, f32[3072]{0:T(1024)S(1)} %copy-done.13, bf16[384,384]{1,0:T(8,128)(2,1)S(1)} %get-tuple-element.40, bf16[384,384]{1,0:T(8,128)(2,1)S(1)} %get-tuple-element.39, bf16[384,384]{1,0:T(8,128)(2,1)S(1)} %get-tuple-element.38, ...), kind=kOutput, calls=%fused_computation.1 | convolution fusion | flops 3630956544 | bytes 12988416 | tf_op jit(solution)/shard_map/dot_general | solution.py:145
  (56 shorter events, 4.1 us)
Async XLA Ops:
  6.5 228.4 %all-gather.2.cloned.1.call-start = ((), (), s32[]{:S(2)}) async-start(), calls=%async_computation | async-start | bytes 10027008 | tf_op jit(solution)/shard_map/all_gather | solution.py:108
  15.7 2.2 copy-start.1
  18.7 47.0 %copy-start = (bf16[384,1536]{1,0:T(8,128)(2,1)S(1)}, bf16[384,1536]{1,0:T(8,128)(2,1)}, u32[]{:S(2)}) copy-start(bf16[384,1536]{1,0:T(8,128)(2,1)} %refs_1_.7) | copy-start | bytes 3538948
  18.8 46.9 %collective-permute-start = (bf16[384,768]{1,0:T(8,128)(2,1)S(1)}, bf16[384,768]{1,0:T(8,128)(2,1)}, u32[]{:S(2)}, u32[]{:S(2)}) collective-permute-start(bf16[384,768]{1,0:T(8,128)(2,1)S(1)} %pad_maximum_fusion), channel_id=1, source_target_pairs={{0,8},{1,9},{2,10},{3,11},{4,12},{5,13},{6,14},{7,15},{8,0},{9,1},... | collective-permute-start | bytes 1769480 | tf_op jit(solution)/shard_map/ppermute | solution.py:127
  65.7 53.3 %collective-permute-start.7 = (bf16[384,768]{1,0:T(8,128)(2,1)S(1)}, bf16[384,768]{1,0:T(8,128)(2,1)}, u32[]{:S(2)}, u32[]{:S(2)}) collective-permute-start(bf16[384,768]{1,0:T(8,128)(2,1)S(1)} %pad_maximum_fusion.1), channel_id=1, source_target_pairs={{0,8},{1,9},{2,10},{3,11},{4,12},{5,13},{6,14},{7,15},{8,0},{9,1},... | collective-permute-start | bytes 1769480 | tf_op jit(solution)/shard_map/ppermute | solution.py:127
  65.7 91.4 %collective-permute-start.1 = (bf16[384,1536]{1,0:T(8,128)(2,1)S(1)}, bf16[384,1536]{1,0:T(8,128)(2,1)S(1)}, u32[]{:S(2)}, u32[]{:S(2)}) collective-permute-start(bf16[384,1536]{1,0:T(8,128)(2,1)S(1)} %copy-done), channel_id=1, source_target_pairs={{0,1},{1,2},{2,3},{3,4},{4,5},{5,6},{6,7},{8,9},{9,10},{10,11},{11... | collective-permute-start | bytes 3538952 | tf_op jit(solution)/shard_map/ppermute | solution.py:91
  69.4 93.0 %collective-permute-start.2 = (bf16[384,1536]{1,0:T(8,128)(2,1)S(1)}, bf16[384,1536]{1,0:T(8,128)(2,1)}, u32[]{:S(2)}, u32[]{:S(2)}) collective-permute-start(bf16[384,1536]{1,0:T(8,128)(2,1)S(1)} %copy-done.1), channel_id=1, source_target_pairs={{0,1},{1,2},{2,3},{3,4},{4,5},{5,6},{6,7},{8,9},{9,10},{10,11},{11... | collective-permute-start | bytes 3538952 | tf_op jit(solution)/shard_map/ppermute | solution.py:91
  71.3 93.0 %collective-permute-start.4 = (bf16[384,1536]{1,0:T(8,128)(2,1)S(1)}, bf16[384,1536]{1,0:T(8,128)(2,1)}, u32[]{:S(2)}, u32[]{:S(2)}) collective-permute-start(bf16[384,1536]{1,0:T(8,128)(2,1)S(1)} %copy-done), channel_id=1, source_target_pairs={{1,0},{2,1},{3,2},{4,3},{5,4},{6,5},{7,6},{9,8},{10,9},{11,10},{12... | collective-permute-start | bytes 3538952 | tf_op jit(solution)/shard_map/ppermute | solution.py:91
  73.7 92.7 %copy-start.10 = (s32[12,2]{0,1:T(2,128)S(1)}, s32[12,2]{0,1:T(2,128)}, u32[]{:S(2)}) copy-start(s32[12,2]{0,1:T(2,128)} %param.14) | copy-start | bytes 292
  73.7 124.2 %copy-start.11 = (s32[6]{0:T(128)S(1)}, s32[6]{0:T(128)}, u32[]{:S(2)}) copy-start(s32[6]{0:T(128)} %constant.20.clone) | copy-start | bytes 76
  73.7 124.2 %copy-start.12 = (s32[6]{0:T(128)S(1)}, s32[6]{0:T(128)}, u32[]{:S(2)}) copy-start(s32[6]{0:T(128)} %constant.21.clone) | copy-start | bytes 76
  119.0 36.3 %collective-permute-start.10 = (bf16[384,768]{1,0:T(8,128)(2,1)}, bf16[384,768]{1,0:T(8,128)(2,1)}, u32[]{:S(2)}, u32[]{:S(2)}) collective-permute-start(bf16[384,768]{1,0:T(8,128)(2,1)} %pad_maximum_fusion.2), channel_id=1, source_target_pairs={{0,8},{1,9},{2,10},{3,11},{4,12},{5,13},{6,14},{7,15},{8,0},{9,1},... | collective-permute-start | bytes 1769480 | tf_op jit(solution)/shard_map/ppermute | solution.py:127
  119.0 47.5 %collective-permute-start.5 = (bf16[384,1536]{1,0:T(8,128)(2,1)S(1)}, bf16[384,1536]{1,0:T(8,128)(2,1)}, u32[]{:S(2)}, u32[]{:S(2)}) collective-permute-start(bf16[384,1536]{1,0:T(8,128)(2,1)S(1)} %copy-done.1), channel_id=1, source_target_pairs={{1,0},{2,1},{3,2},{4,3},{5,4},{6,5},{7,6},{9,8},{10,9},{11,10},{12... | collective-permute-start | bytes 3538952 | tf_op jit(solution)/shard_map/ppermute | solution.py:91
  155.2 15.8 %collective-permute-start.3 = (bf16[384,768]{1,0:T(8,128)(2,1)}, bf16[384,768]{1,0:T(8,128)(2,1)}, u32[]{:S(2)}, u32[]{:S(2)}) collective-permute-start(bf16[384,768]{1,0:T(8,128)(2,1)} %collective-permute-done.refs_3_.refs_4_), channel_id=1, source_target_pairs={{0,1},{1,2},{2,3},{3,4},{4,5},{5,6},{6,7},{8,9},{9,10},{10,11},{11... | collective-permute-start | bytes 1769480 | tf_op jit(solution)/shard_map/ppermute | solution.py:91
  157.1 41.6 %copy-start.2 = (bf16[384,1536]{1,0:T(8,128)(2,1)}, bf16[384,1536]{1,0:T(8,128)(2,1)S(1)}, u32[]{:S(2)}) copy-start(bf16[384,1536]{1,0:T(8,128)(2,1)S(1)} %collective-permute-done.1.refs_5_) | copy-start | bytes 3538948
  157.2 15.8 %collective-permute-start.6 = (bf16[384,768]{1,0:T(8,128)(2,1)}, bf16[384,768]{1,0:T(8,128)(2,1)}, u32[]{:S(2)}, u32[]{:S(2)}) collective-permute-start(bf16[384,768]{1,0:T(8,128)(2,1)} %collective-permute-done.refs_3_.refs_4_), channel_id=1, source_target_pairs={{1,0},{2,1},{3,2},{4,3},{5,4},{6,5},{7,6},{9,8},{10,9},{11,10},{12... | collective-permute-start | bytes 1769480 | tf_op jit(solution)/shard_map/ppermute | solution.py:91
  162.3 32.2 %collective-permute-start.8 = (bf16[384,768]{1,0:T(8,128)(2,1)}, bf16[384,768]{1,0:T(8,128)(2,1)}, u32[]{:S(2)}, u32[]{:S(2)}) collective-permute-start(bf16[384,768]{1,0:T(8,128)(2,1)} %collective-permute-done.7.refs_3_.refs_4_), channel_id=1, source_target_pairs={{0,1},{1,2},{2,3},{3,4},{4,5},{5,6},{6,7},{8,9},{9,10},{10,11},{11... | collective-permute-start | bytes 1769480 | tf_op jit(solution)/shard_map/ppermute | solution.py:91
  164.3 28.3 %collective-permute-start.13 = (bf16[384,768]{1,0:T(8,128)(2,1)}, bf16[384,768]{1,0:T(8,128)(2,1)S(1)}, u32[]{:S(2)}, u32[]{:S(2)}) collective-permute-start(bf16[384,768]{1,0:T(8,128)(2,1)} %pad_maximum_fusion.3), channel_id=1, source_target_pairs={{0,8},{1,9},{2,10},{3,11},{4,12},{5,13},{6,14},{7,15},{8,0},{9,1},... | collective-permute-start | bytes 1769480 | tf_op jit(solution)/shard_map/ppermute | solution.py:127
  166.5 40.4 %collective-permute-start.9 = (bf16[384,768]{1,0:T(8,128)(2,1)}, bf16[384,768]{1,0:T(8,128)(2,1)S(1)}, u32[]{:S(2)}, u32[]{:S(2)}) collective-permute-start(bf16[384,768]{1,0:T(8,128)(2,1)} %collective-permute-done.7.refs_3_.refs_4_), channel_id=1, source_target_pairs={{1,0},{2,1},{3,2},{4,3},{5,4},{6,5},{7,6},{9,8},{10,9},{11,10},{12... | collective-permute-start | bytes 1769480 | tf_op jit(solution)/shard_map/ppermute | solution.py:91
  171.0 44.8 %collective-permute-start.11 = (bf16[384,768]{1,0:T(8,128)(2,1)}, bf16[384,768]{1,0:T(8,128)(2,1)S(1)}, u32[]{:S(2)}, u32[]{:S(2)}) collective-permute-start(bf16[384,768]{1,0:T(8,128)(2,1)} %collective-permute-done.10.refs_3_.refs_4_), channel_id=1, source_target_pairs={{0,1},{1,2},{2,3},{3,4},{4,5},{5,6},{6,7},{8,9},{9,10},{10,11},{11... | collective-permute-start | bytes 1769480 | tf_op jit(solution)/shard_map/ppermute | solution.py:91
  173.0 42.8 %collective-permute-start.12 = (bf16[384,768]{1,0:T(8,128)(2,1)}, bf16[384,768]{1,0:T(8,128)(2,1)}, u32[]{:S(2)}, u32[]{:S(2)}) collective-permute-start(bf16[384,768]{1,0:T(8,128)(2,1)} %collective-permute-done.10.refs_3_.refs_4_), channel_id=1, source_target_pairs={{1,0},{2,1},{3,2},{4,3},{5,4},{6,5},{7,6},{9,8},{10,9},{11,10},{12... | collective-permute-start | bytes 1769480 | tf_op jit(solution)/shard_map/ppermute | solution.py:91
  192.6 14.3 %copy-start.3 = (bf16[384,768]{1,0:T(8,128)(2,1)}, bf16[384,768]{1,0:T(8,128)(2,1)S(1)}, u32[]{:S(2)}) copy-start(bf16[384,768]{1,0:T(8,128)(2,1)S(1)} %collective-permute-done.13.refs_3_.refs_4_) | copy-start | bytes 1769476
  192.6 32.2 %collective-permute-start.14 = (bf16[384,768]{1,0:T(8,128)(2,1)S(1)}, bf16[384,768]{1,0:T(8,128)(2,1)S(1)}, u32[]{:S(2)}, u32[]{:S(2)}) collective-permute-start(bf16[384,768]{1,0:T(8,128)(2,1)S(1)} %collective-permute-done.13.refs_3_.refs_4_), channel_id=1, source_target_pairs={{0,1},{1,2},{2,3},{3,4},{4,5},{5,6},{6,7},{8,9},{9,10},{10,11},{11... | collective-permute-start | bytes 1769480 | tf_op jit(solution)/shard_map/ppermute | solution.py:91
  194.5 30.2 %collective-permute-start.15 = (bf16[384,768]{1,0:T(8,128)(2,1)S(1)}, bf16[384,768]{1,0:T(8,128)(2,1)}, u32[]{:S(2)}, u32[]{:S(2)}) collective-permute-start(bf16[384,768]{1,0:T(8,128)(2,1)S(1)} %collective-permute-done.13.refs_3_.refs_4_), channel_id=1, source_target_pairs={{1,0},{2,1},{3,2},{4,3},{5,4},{6,5},{7,6},{9,8},{10,9},{11,10},{12... | collective-permute-start | bytes 1769480 | tf_op jit(solution)/shard_map/ppermute | solution.py:91
  206.9 0.8 copy-start.6
  215.8 0.8 copy-start.5
  224.8 0.8 copy-start.4
  225.6 8.2 %copy-start.7 = (bf16[384,384]{1,0:T(8,128)(2,1)S(1)}, bf16[384,384]{1,0:T(8,128)(2,1)}, u32[]{:S(2)}) copy-start(bf16[384,384]{1,0:T(8,128)(2,1)} %shard_map.100) | copy-start | bytes 884740
  225.6 8.2 %copy-start.8 = (bf16[384,384]{1,0:T(8,128)(2,1)S(1)}, bf16[384,384]{1,0:T(8,128)(2,1)}, u32[]{:S(2)}) copy-start(bf16[384,384]{1,0:T(8,128)(2,1)} %shard_map.101) | copy-start | bytes 884740
  225.6 8.2 %copy-start.9 = (bf16[384,384]{1,0:T(8,128)(2,1)S(1)}, bf16[384,384]{1,0:T(8,128)(2,1)}, u32[]{:S(2)}) copy-start(bf16[384,384]{1,0:T(8,128)(2,1)} %shard_map.102) | copy-start | bytes 884740
  233.7 1.2 copy-start.13
Sparse Core Ops, SparseCore 0:
  15.8 137.5 all-gather.1

commit v3 on v1

--- a/solution.py
+++ b/solution.py
@@ -8,7 +8,7 @@
 
 
 TW = 8
-GROUPS = 4
+GROUPS = 3
 
 
 def group_attention(queries, slots, usable, head_base, group_heads, head_dim, score_scale):
@@ -90,11 +90,14 @@
     to_left = [(i + 1, i) for i in range(devices) if i % TW < TW - 1]
     sideways = lambda x: (lax.ppermute(x, "seq", to_right), lax.ppermute(x, "seq", to_left))
 
-    weight_all = lax.all_gather(out_weight, "seq", axis=0, tiled=True)
     verticals = vertical_parts(devices, grid_rows)
-    vert_lens = [lax.ppermute(tile_lengths, "seq", pairs) for pairs in verticals]
+    left_of = lambda pairs: [(s, r + 1) for s, r in pairs if r % TW < TW - 1]
+    right_of = lambda pairs: [(s, r - 1) for s, r in pairs if r % TW > 0]
+    fetch = lambda pairs: lax.ppermute(tile_lengths, "seq", pairs)
+    vert_lens = [fetch(pairs) for pairs in verticals]
     column_lens = jnp.concatenate([tile_lengths] + vert_lens)
-    left_lens, right_lens = sideways(column_lens)
+    left_lens = jnp.concatenate([fetch(to_right)] + [fetch(left_of(p)) for p in verticals])
+    right_lens = jnp.concatenate([fetch(to_left)] + [fetch(right_of(p)) for p in verticals])
     (left_k, left_v), (right_k, right_v) = sideways((keys, values))
 
     positions = jnp.arange(tile_rows, dtype=jnp.int32)
@@ -117,6 +120,9 @@
         got = [lax.ppermute(own, "seq", pairs) for pairs in verticals]
         if got:
             previous = got[-1]
+        if g == 0:
+            weight_part, _ = lax.optimization_barrier((out_weight, got[-1] if got else own))
+            weight_all = lax.all_gather(weight_part, "seq", axis=0, tiled=True)
         forwarded = [sideways(item) for item in got]
         base = g * group_heads
         slots = [(keys, values, base, base)]

time: 257 us -> 273 us (1.062)
  starting transfers between devices: 40 us -> 82.5 us
  waiting for transfers between devices: 151 us -> 119 us
  local copies, waits for them, and re-layouts: 4.32 us -> 8.7 us
    ppermute x1 -> x5, starting transfers between devices: 2.36 us -> 52.9 us  [on_device(): fetch = lambda pairs: lax.ppermute(tile_lengths, 'seq', pairs)]
    ppermute x7 -> x5, waiting for transfers between devices: 18.6 us -> 0.01 us  [on_device(): lax.ppermute(x, 'seq', to_left)]
    ppermute x4 -> x3, waiting for transfers between devices: 114 us -> 101 us  [on_device(): got = [lax.ppermute(own, 'seq', pairs) for pairs in verticals]]
    ppermute x7 -> x5, starting transfers between devices: 18.5 us -> 11.2 us  [on_device(): lax.ppermute(x, 'seq', to_right)]
    concatenate x0 -> x1, local copies, waits for them, and re-layouts: none -> 3.22 us  [on_device(): length_stack = jnp.concatenate([column_lens, left_lens, right_lens])]
    ppermute x7 -> x5, starting transfers between devices: 19 us -> 16.5 us  [on_device(): lax.ppermute(x, 'seq', to_left)]
    ppermute x1 -> x5, waiting for transfers between devices: 16.5 us -> 18.8 us  [on_device(): fetch = lambda pairs: lax.ppermute(tile_lengths, 'seq', pairs)]
    pallas_call x4 -> x3, Pallas kernels: 32.3 us -> 30.4 us  [group_attention(): pl.pallas_call(kernel, grid=(group_heads,), in_specs=in_specs, out_specs=...]
  transfers between devices with their start and end apart: 20 -> 19, of which waited for: 7 -> 8; matrix products, arithmetic and copies ran while one was open for 2% -> 3% of each run, Pallas kernels for 13% -> 11%
where the time goes in v3:
time: 273 us; the launch traced here: 269 us
  waiting for transfers between devices  119 us (44%)
  starting transfers between devices  82.5 us (30%)
  Pallas kernels  30.4 us (11%)
  between operations  14.4 us (5%)
  matrix products  8.73 us (3%)
  local copies, waits for them, and re-layouts  8.7 us (3%)
  other arithmetic  5.06 us (2%)
    ppermute x3, waiting for transfers between devices, on_device(): got = [lax.ppermute(own, 'seq', pairs) for pairs in verticals]  101 us
    ppermute x5, starting transfers between devices, on_device(): fetch = lambda pairs: lax.ppermute(tile_lengths, 'seq', pairs)  52.9 us
    pallas_call x3, Pallas kernels, group_attention(): pl.pallas_call(kernel, grid=(group_heads,), in_specs=in_specs, out_specs=...  30.4 us
    ppermute x5, waiting for transfers between devices, on_device(): fetch = lambda pairs: lax.ppermute(tile_lengths, 'seq', pairs)  18.8 us
    ppermute x5, starting transfers between devices, on_device(): lax.ppermute(x, 'seq', to_left)  16.5 us
    ppermute x5, starting transfers between devices, on_device(): lax.ppermute(x, 'seq', to_right)  11.2 us
    dot_general x1, matrix products, on_device(): jnp.dot(attended_all, weight_all, preferred_element_type=jnp.float32)  8.73 us
  transfers between devices with their start and end apart: 19, of which 8 were waited for; matrix products, arithmetic and copies ran while one was open for 3% of the time, Pallas kernels for 11%

profile of v3, /device:TPU:27, one launch (start us, length us, event | category | flops | bytes accessed | tf_op | source)
XLA Modules:
  0.0 269.3 jit_solution(1120510167252603700)
XLA Ops:
  6.5 2.3 fusion.6
  8.9 1.0 fusion.7
  10.1 37.2 %collective-permute-done.refs_3_.refs_4_ = bf16[384,1024]{1,0:T(8,128)(2,1)} collective-permute-done((bf16[384,1024]{1,0:T(8,128)(2,1)S(1)}, bf16[384,1024]{1,0:T(8,128)(2,1)}, u32[]{:S(2)}, u32[]{:S(2)}) %collective-permute-start) | collective-permute-done | bytes 786464 | tf_op jit(solution)/shard_map/ppermute | solution.py:120
  47.3 3.5 %collective-permute-start.1 = (bf16[384,1536]{1,0:T(8,128)(2,1)S(1)}, bf16[384,1536]{1,0:T(8,128)(2,1)S(1)}, u32[]{:S(2)}, u32[]{:S(2)}) collective-permute-start(bf16[384,1536]{1,0:T(8,128)(2,1)S(1)} %copy-done), channel_id=1, source_target_pairs={{0,1},{1,2},{2,3},{3,4},{4,5},{5,6},{6,7},{8,9},{9,10},{10,11},{11... | collective-permute-start | bytes 3538952 | tf_op jit(solution)/shard_map/ppermute | solution.py:91
  50.8 1.2 pad_maximum_fusion.1
  52.1 1.9 collective-permute-start.2
  54.1 2.4 collective-permute-start.4
  56.5 2.9 %collective-permute-start.5 = (bf16[384,1536]{1,0:T(8,128)(2,1)S(1)}, bf16[384,1536]{1,0:T(8,128)(2,1)S(1)}, u32[]{:S(2)}, u32[]{:S(2)}) collective-permute-start(bf16[384,1536]{1,0:T(8,128)(2,1)S(1)} %copy-done.1), channel_id=1, source_target_pairs={{1,0},{2,1},{3,2},{4,3},{5,4},{6,5},{7,6},{9,8},{10,9},{11,10},{12... | collective-permute-start | bytes 3538952 | tf_op jit(solution)/shard_map/ppermute | solution.py:91
  59.4 1.2 pad_maximum_fusion.2
  60.6 44.0 %collective-permute-done.12.refs_3_.refs_4_ = bf16[384,1024]{1,0:T(8,128)(2,1)} collective-permute-done((bf16[384,1024]{1,0:T(8,128)(2,1)S(1)}, bf16[384,1024]{1,0:T(8,128)(2,1)}, u32[]{:S(2)}, u32[]{:S(2)}) %collective-permute-start.12) | collective-permute-done | bytes 786464 | tf_op jit(solution)/shard_map/ppermute | solution.py:120
  104.6 2.3 collective-permute-start.10
  107.0 4.1 %collective-permute-done.10 = s32[1]{0:T(128)} collective-permute-done((s32[1]{0:T(128)}, s32[1]{0:T(128)}, u32[]{:S(2)}, u32[]{:S(2)}) %collective-permute-start.10) | collective-permute-done | bytes 36 | tf_op jit(solution)/shard_map/ppermute | solution.py:96
  111.1 46.8 %collective-permute-start.11 = (s32[1]{0:T(128)}, s32[1]{0:T(128)}, u32[]{:S(2)}, u32[]{:S(2)}) collective-permute-start(s32[1]{0:T(128)} %param.12), channel_id=1, source_target_pairs={{1,8},{2,9},{3,10},{4,11},{5,12},{6,13},{7,14},{9,0},{10,1},{11,2}... | collective-permute-start | bytes 20 | tf_op jit(solution)/shard_map/ppermute | solution.py:96
  158.7 3.4 %collective-permute-done.7 = s32[1]{0:T(128)} collective-permute-done((s32[1]{0:T(128)}, s32[1]{0:T(128)}, u32[]{:S(2)}, u32[]{:S(2)}) %collective-permute-start.7) | collective-permute-done | bytes 36 | tf_op jit(solution)/shard_map/ppermute | solution.py:96
  162.1 1.9 collective-permute-start.8
  164.1 5.3 %collective-permute-done.8 = s32[1]{0:T(128)} collective-permute-done((s32[1]{0:T(128)}, s32[1]{0:T(128)}, u32[]{:S(2)}, u32[]{:S(2)}) %collective-permute-start.8) | collective-permute-done | bytes 36 | tf_op jit(solution)/shard_map/ppermute | solution.py:96
  169.4 1.9 collective-permute-start.9
  171.3 5.1 %collective-permute-done.9 = s32[1]{0:T(128)} collective-permute-done((s32[1]{0:T(128)}, s32[1]{0:T(128)}, u32[]{:S(2)}, u32[]{:S(2)}) %collective-permute-start.9) | collective-permute-done | bytes 36 | tf_op jit(solution)/shard_map/ppermute | solution.py:96
  176.4 1.7 collective-permute-start.15
  178.1 1.9 collective-permute-start.3
  180.7 4.3 %collective-permute-start.6 = (bf16[384,1024]{1,0:T(8,128)(2,1)}, bf16[384,1024]{1,0:T(8,128)(2,1)}, u32[]{:S(2)}, u32[]{:S(2)}) collective-permute-start(bf16[384,1024]{1,0:T(8,128)(2,1)} %collective-permute-done.refs_3_.refs_4_), channel_id=1, source_target_pairs={{1,0},{2,1},{3,2},{4,3},{5,4},{6,5},{7,6},{9,8},{10,9},{11,10},{12... | collective-permute-start | bytes 2359304 | tf_op jit(solution)/shard_map/ppermute | solution.py:91
  185.0 1.9 collective-permute-start.13
  187.0 4.5 %collective-permute-start.14 = (bf16[384,1024]{1,0:T(8,128)(2,1)}, bf16[384,1024]{1,0:T(8,128)(2,1)S(1)}, u32[]{:S(2)}, u32[]{:S(2)}) collective-permute-start(bf16[384,1024]{1,0:T(8,128)(2,1)} %collective-permute-done.12.refs_3_.refs_4_), channel_id=1, source_target_pairs={{1,0},{2,1},{3,2},{4,3},{5,4},{6,5},{7,6},{9,8},{10,9},{11,10},{12... | collective-permute-start | bytes 2359304 | tf_op jit(solution)/shard_map/ppermute | solution.py:91
  191.5 19.4 %collective-permute-done.15.refs_3_.refs_4_ = bf16[384,1024]{1,0:T(8,128)(2,1)} collective-permute-done((bf16[384,1024]{1,0:T(8,128)(2,1)S(1)}, bf16[384,1024]{1,0:T(8,128)(2,1)}, u32[]{:S(2)}, u32[]{:S(2)}) %collective-permute-start.15) | collective-permute-done | bytes 786464 | tf_op jit(solution)/shard_map/ppermute | solution.py:120
  210.9 1.9 collective-permute-start.16
  212.8 2.4 collective-permute-start.17
  215.9 3.2 %concatenate.16 = s32[6]{0:T(128)S(1)} concatenate(s32[1]{0:T(128)} %copy.10, s32[1]{0:T(128)} %collective-permute-done.7, s32[1]{0:T(128)} %collective-permute-done.8, s32[1]{0:T(128)} %collective-permute-done.9, s32[1]{0:T(128)} %collective-permute-done.10, s32[1]{0:T(128)} %collective-permute-done.11), dimensions={0} | concatenate | bytes 48 | tf_op jit(solution)/shard_map/concatenate | solution.py:108
  219.9 10.1 %shard_map.91 = bf16[384,512]{1,0:T(8,128)(2,1)} custom-call(bf16[384,1536]{1,0:T(8,128)(2,1)} %refs_0_.5, bf16[384,1536]{1,0:T(8,128)(2,1)} %refs_1_.5, bf16[384,1536]{1,0:T(8,128)(2,1)} %refs_2_.5, bf16[384,1024]{1,0:T(8,128)(2,1)} %collective-permute-done.refs_3_.refs_4_, bf16[384,1024]{1,0:T(8,128)(2,1)} %collective-permute-done.refs_3_.refs_4_, ...), custom_call_target="tpu_custom_call" | custom-call | tf_op jit(solution)/shard_map/pallas_call | solution.py:58
  231.0 10.1 %shard_map.92 = bf16[384,512]{1,0:T(8,128)(2,1)} custom-call(bf16[384,1536]{1,0:T(8,128)(2,1)} %refs_0_.5, bf16[384,1536]{1,0:T(8,128)(2,1)} %refs_1_.5, bf16[384,1536]{1,0:T(8,128)(2,1)} %refs_2_.5, bf16[384,1024]{1,0:T(8,128)(2,1)} %collective-permute-done.12.refs_3_.refs_4_, bf16[384,1024]{1,0:T(8,128)(2,1)} %collective-permute-done.12.refs_3_.refs_4_, ...), custom_call_target="tpu_custom_call" | custom-call | tf_op jit(solution)/shard_map/pallas_call | solution.py:58
  242.2 10.2 %shard_map.93 = bf16[384,512]{1,0:T(8,128)(2,1)} custom-call(bf16[384,1536]{1,0:T(8,128)(2,1)} %refs_0_.5, bf16[384,1536]{1,0:T(8,128)(2,1)} %refs_1_.5, bf16[384,1536]{1,0:T(8,128)(2,1)} %refs_2_.5, bf16[384,1024]{1,0:T(8,128)(2,1)} %collective-permute-done.15.refs_3_.refs_4_, bf16[384,1024]{1,0:T(8,128)(2,1)} %collective-permute-done.15.refs_3_.refs_4_, ...), custom_call_target="tpu_custom_call" | custom-call | tf_op jit(solution)/shard_map/pallas_call | solution.py:58
  252.5 1.1 broadcast_select_fusion.2
  253.7 8.7 %multiply_convert_fusion = bf16[384,3072]{1,0:T(8,128)(2,1)} fusion(bf16[1536,3072]{1,0:T(8,128)(2,1)} %all-gather.2.cloned.1.call-done, f32[3072]{0:T(1024)S(1)} %copy-done.15, bf16[384,512]{1,0:T(8,128)(2,1)S(1)} %get-tuple-element.31, bf16[384,512]{1,0:T(8,128)(2,1)S(1)} %get-tuple-element.30, bf16[384,512]{1,0:T(8,128)(2,1)S(1)} %get-tuple-element.29), kind=kOutput, calls=%fused_computation | convolution fusion | flops 3629776896 | bytes 12988416 | tf_op jit(solution)/shard_map/dot_general | solution.py:141
  (55 shorter events, 4.8 us)
Async XLA Ops:
  6.5 2.3 copy-start.1
  6.5 247.1 %all-gather.2.cloned.1.call-start = ((), (), s32[]{:S(2)}) async-start(), calls=%async_computation | async-start | bytes 10027008 | tf_op jit(solution)/shard_map/all_gather | solution.py:125
  9.9 37.4 %copy-start = (bf16[384,1536]{1,0:T(8,128)(2,1)S(1)}, bf16[384,1536]{1,0:T(8,128)(2,1)}, u32[]{:S(2)}) copy-start(bf16[384,1536]{1,0:T(8,128)(2,1)} %refs_1_.5) | copy-start | bytes 3538948
  10.0 37.3 %collective-permute-start = (bf16[384,1024]{1,0:T(8,128)(2,1)S(1)}, bf16[384,1024]{1,0:T(8,128)(2,1)}, u32[]{:S(2)}, u32[]{:S(2)}) collective-permute-start(bf16[384,1024]{1,0:T(8,128)(2,1)S(1)} %pad_maximum_fusion), channel_id=1, source_target_pairs={{0,8},{1,9},{2,10},{3,11},{4,12},{5,13},{6,14},{7,15},{8,0},{9,1},... | collective-permute-start | bytes 2359304 | tf_op jit(solution)/shard_map/ppermute | solution.py:120
  47.3 130.8 %collective-permute-start.1 = (bf16[384,1536]{1,0:T(8,128)(2,1)S(1)}, bf16[384,1536]{1,0:T(8,128)(2,1)S(1)}, u32[]{:S(2)}, u32[]{:S(2)}) collective-permute-start(bf16[384,1536]{1,0:T(8,128)(2,1)S(1)} %copy-done), channel_id=1, source_target_pairs={{0,1},{1,2},{2,3},{3,4},{4,5},{5,6},{6,7},{8,9},{9,10},{10,11},{11... | collective-permute-start | bytes 3538952 | tf_op jit(solution)/shard_map/ppermute | solution.py:91
  50.8 129.8 %copy-start.11 = (s32[12,2]{0,1:T(2,128)S(1)}, s32[12,2]{0,1:T(2,128)}, u32[]{:S(2)}) copy-start(s32[12,2]{0,1:T(2,128)} %param.13) | copy-start | bytes 292
  50.8 165.0 %copy-start.13 = (s32[6]{0:T(128)S(1)}, s32[6]{0:T(128)}, u32[]{:S(2)}) copy-start(s32[6]{0:T(128)} %constant.7.clone) | copy-start | bytes 76
  50.8 165.0 %copy-start.14 = (s32[6]{0:T(128)S(1)}, s32[6]{0:T(128)}, u32[]{:S(2)}) copy-start(s32[6]{0:T(128)} %constant.8.clone) | copy-start | bytes 76
  52.1 52.6 %collective-permute-start.12 = (bf16[384,1024]{1,0:T(8,128)(2,1)S(1)}, bf16[384,1024]{1,0:T(8,128)(2,1)}, u32[]{:S(2)}, u32[]{:S(2)}) collective-permute-start(bf16[384,1024]{1,0:T(8,128)(2,1)S(1)} %pad_maximum_fusion.1), channel_id=1, source_target_pairs={{0,8},{1,9},{2,10},{3,11},{4,12},{5,13},{6,14},{7,15},{8,0},{9,1},... | collective-permute-start | bytes 2359304 | tf_op jit(solution)/shard_map/ppermute | solution.py:120
  52.1 128.6 %collective-permute-start.2 = (bf16[384,1536]{1,0:T(8,128)(2,1)S(1)}, bf16[384,1536]{1,0:T(8,128)(2,1)S(1)}, u32[]{:S(2)}, u32[]{:S(2)}) collective-permute-start(bf16[384,1536]{1,0:T(8,128)(2,1)S(1)} %copy-done.1), channel_id=1, source_target_pairs={{0,1},{1,2},{2,3},{3,4},{4,5},{5,6},{6,7},{8,9},{9,10},{10,11},{11... | collective-permute-start | bytes 3538952 | tf_op jit(solution)/shard_map/ppermute | solution.py:91
  54.1 130.9 %collective-permute-start.4 = (bf16[384,1536]{1,0:T(8,128)(2,1)S(1)}, bf16[384,1536]{1,0:T(8,128)(2,1)S(1)}, u32[]{:S(2)}, u32[]{:S(2)}) collective-permute-start(bf16[384,1536]{1,0:T(8,128)(2,1)S(1)} %copy-done), channel_id=1, source_target_pairs={{1,0},{2,1},{3,2},{4,3},{5,4},{6,5},{7,6},{9,8},{10,9},{11,10},{12... | collective-permute-start | bytes 3538952 | tf_op jit(solution)/shard_map/ppermute | solution.py:91
  56.5 130.5 %collective-permute-start.5 = (bf16[384,1536]{1,0:T(8,128)(2,1)S(1)}, bf16[384,1536]{1,0:T(8,128)(2,1)S(1)}, u32[]{:S(2)}, u32[]{:S(2)}) collective-permute-start(bf16[384,1536]{1,0:T(8,128)(2,1)S(1)} %copy-done.1), channel_id=1, source_target_pairs={{1,0},{2,1},{3,2},{4,3},{5,4},{6,5},{7,6},{9,8},{10,9},{11,10},{12... | collective-permute-start | bytes 3538952 | tf_op jit(solution)/shard_map/ppermute | solution.py:91
  104.6 6.4 %collective-permute-start.10 = (s32[1]{0:T(128)}, s32[1]{0:T(128)}, u32[]{:S(2)}, u32[]{:S(2)}) collective-permute-start(s32[1]{0:T(128)} %param.12), channel_id=1, source_target_pairs={{1,0},{2,1},{3,2},{4,3},{5,4},{6,5},{7,6},{9,8},{10,9},{11,10},{12... | collective-permute-start | bytes 20 | tf_op jit(solution)/shard_map/ppermute | solution.py:96
  111.1 47.7 %collective-permute-start.11 = (s32[1]{0:T(128)}, s32[1]{0:T(128)}, u32[]{:S(2)}, u32[]{:S(2)}) collective-permute-start(s32[1]{0:T(128)} %param.12), channel_id=1, source_target_pairs={{1,8},{2,9},{3,10},{4,11},{5,12},{6,13},{7,14},{9,0},{10,1},{11,2}... | collective-permute-start | bytes 20 | tf_op jit(solution)/shard_map/ppermute | solution.py:96
  158.7 3.4 %collective-permute-start.7 = (s32[1]{0:T(128)}, s32[1]{0:T(128)}, u32[]{:S(2)}, u32[]{:S(2)}) collective-permute-start(s32[1]{0:T(128)} %param.12), channel_id=1, source_target_pairs={{0,8},{1,9},{2,10},{3,11},{4,12},{5,13},{6,14},{7,15},{8,0},{9,1},... | collective-permute-start | bytes 20 | tf_op jit(solution)/shard_map/ppermute | solution.py:96
  162.1 7.2 %collective-permute-start.8 = (s32[1]{0:T(128)}, s32[1]{0:T(128)}, u32[]{:S(2)}, u32[]{:S(2)}) collective-permute-start(s32[1]{0:T(128)} %param.12), channel_id=1, source_target_pairs={{0,1},{1,2},{2,3},{3,4},{4,5},{5,6},{6,7},{8,9},{9,10},{10,11},{11... | collective-permute-start | bytes 20 | tf_op jit(solution)/shard_map/ppermute | solution.py:96
  169.4 7.0 %collective-permute-start.9 = (s32[1]{0:T(128)}, s32[1]{0:T(128)}, u32[]{:S(2)}, u32[]{:S(2)}) collective-permute-start(s32[1]{0:T(128)} %param.12), channel_id=1, source_target_pairs={{0,9},{1,10},{2,11},{3,12},{4,13},{5,14},{6,15},{8,1},{9,2},{10,3}... | collective-permute-start | bytes 20 | tf_op jit(solution)/shard_map/ppermute | solution.py:96
  176.4 34.5 %collective-permute-start.15 = (bf16[384,1024]{1,0:T(8,128)(2,1)S(1)}, bf16[384,1024]{1,0:T(8,128)(2,1)}, u32[]{:S(2)}, u32[]{:S(2)}) collective-permute-start(bf16[384,1024]{1,0:T(8,128)(2,1)S(1)} %pad_maximum_fusion.2), channel_id=1, source_target_pairs={{0,8},{1,9},{2,10},{3,11},{4,12},{5,13},{6,14},{7,15},{8,0},{9,1},... | collective-permute-start | bytes 2359304 | tf_op jit(solution)/shard_map/ppermute | solution.py:120
  178.1 41.8 %copy-start.2 = (bf16[384,1536]{1,0:T(8,128)(2,1)}, bf16[384,1536]{1,0:T(8,128)(2,1)S(1)}, u32[]{:S(2)}) copy-start(bf16[384,1536]{1,0:T(8,128)(2,1)S(1)} %collective-permute-done.1.refs_5_) | copy-start | bytes 3538948
  178.1 34.8 %collective-permute-start.3 = (bf16[384,1024]{1,0:T(8,128)(2,1)}, bf16[384,1024]{1,0:T(8,128)(2,1)}, u32[]{:S(2)}, u32[]{:S(2)}) collective-permute-start(bf16[384,1024]{1,0:T(8,128)(2,1)} %collective-permute-done.refs_3_.refs_4_), channel_id=1, source_target_pairs={{0,1},{1,2},{2,3},{3,4},{4,5},{5,6},{6,7},{8,9},{9,10},{10,11},{11... | collective-permute-start | bytes 2359304 | tf_op jit(solution)/shard_map/ppermute | solution.py:91
  180.7 6.2 %copy-start.3 = (bf16[384,1536]{1,0:T(8,128)(2,1)}, bf16[384,1536]{1,0:T(8,128)(2,1)S(1)}, u32[]{:S(2)}) copy-start(bf16[384,1536]{1,0:T(8,128)(2,1)S(1)} %collective-permute-done.2.refs_6_) | copy-start | bytes 3538948
  180.7 39.2 %collective-permute-start.6 = (bf16[384,1024]{1,0:T(8,128)(2,1)}, bf16[384,1024]{1,0:T(8,128)(2,1)}, u32[]{:S(2)}, u32[]{:S(2)}) collective-permute-start(bf16[384,1024]{1,0:T(8,128)(2,1)} %collective-permute-done.refs_3_.refs_4_), channel_id=1, source_target_pairs={{1,0},{2,1},{3,2},{4,3},{5,4},{6,5},{7,6},{9,8},{10,9},{11,10},{12... | collective-permute-start | bytes 2359304 | tf_op jit(solution)/shard_map/ppermute | solution.py:91
  185.0 6.5 %copy-start.4 = (bf16[384,1536]{1,0:T(8,128)(2,1)}, bf16[384,1536]{1,0:T(8,128)(2,1)S(1)}, u32[]{:S(2)}) copy-start(bf16[384,1536]{1,0:T(8,128)(2,1)S(1)} %collective-permute-done.4.refs_9_) | copy-start | bytes 3538948
  185.0 45.0 %collective-permute-start.13 = (bf16[384,1024]{1,0:T(8,128)(2,1)}, bf16[384,1024]{1,0:T(8,128)(2,1)}, u32[]{:S(2)}, u32[]{:S(2)}) collective-permute-start(bf16[384,1024]{1,0:T(8,128)(2,1)} %collective-permute-done.12.refs_3_.refs_4_), channel_id=1, source_target_pairs={{0,1},{1,2},{2,3},{3,4},{4,5},{5,6},{6,7},{8,9},{9,10},{10,11},{11... | collective-permute-start | bytes 2359304 | tf_op jit(solution)/shard_map/ppermute | solution.py:91
  187.0 24.0 %copy-start.5 = (bf16[384,1536]{1,0:T(8,128)(2,1)}, bf16[384,1536]{1,0:T(8,128)(2,1)S(1)}, u32[]{:S(2)}) copy-start(bf16[384,1536]{1,0:T(8,128)(2,1)S(1)} %collective-permute-done.5.refs_10_) | copy-start | bytes 3538948
  187.0 43.1 %collective-permute-start.14 = (bf16[384,1024]{1,0:T(8,128)(2,1)}, bf16[384,1024]{1,0:T(8,128)(2,1)S(1)}, u32[]{:S(2)}, u32[]{:S(2)}) collective-permute-start(bf16[384,1024]{1,0:T(8,128)(2,1)} %collective-permute-done.12.refs_3_.refs_4_), channel_id=1, source_target_pairs={{1,0},{2,1},{3,2},{4,3},{5,4},{6,5},{7,6},{9,8},{10,9},{11,10},{12... | collective-permute-start | bytes 2359304 | tf_op jit(solution)/shard_map/ppermute | solution.py:91
  210.9 30.1 %collective-permute-start.16 = (bf16[384,1024]{1,0:T(8,128)(2,1)}, bf16[384,1024]{1,0:T(8,128)(2,1)S(1)}, u32[]{:S(2)}, u32[]{:S(2)}) collective-permute-start(bf16[384,1024]{1,0:T(8,128)(2,1)} %collective-permute-done.15.refs_3_.refs_4_), channel_id=1, source_target_pairs={{0,1},{1,2},{2,3},{3,4},{4,5},{5,6},{6,7},{8,9},{9,10},{10,11},{11... | collective-permute-start | bytes 2359304 | tf_op jit(solution)/shard_map/ppermute | solution.py:91
  212.8 28.2 %collective-permute-start.17 = (bf16[384,1024]{1,0:T(8,128)(2,1)}, bf16[384,1024]{1,0:T(8,128)(2,1)S(1)}, u32[]{:S(2)}, u32[]{:S(2)}) collective-permute-start(bf16[384,1024]{1,0:T(8,128)(2,1)} %collective-permute-done.15.refs_3_.refs_4_), channel_id=1, source_target_pairs={{1,0},{2,1},{3,2},{4,3},{5,4},{6,5},{7,6},{9,8},{10,9},{11,10},{12... | collective-permute-start | bytes 2359304 | tf_op jit(solution)/shard_map/ppermute | solution.py:91
  242.2 10.2 %copy-start.9 = (bf16[384,512]{1,0:T(8,128)(2,1)S(1)}, bf16[384,512]{1,0:T(8,128)(2,1)}, u32[]{:S(2)}) copy-start(bf16[384,512]{1,0:T(8,128)(2,1)} %shard_map.91) | copy-start | bytes 1179652
  242.2 10.2 %copy-start.10 = (bf16[384,512]{1,0:T(8,128)(2,1)S(1)}, bf16[384,512]{1,0:T(8,128)(2,1)}, u32[]{:S(2)}) copy-start(bf16[384,512]{1,0:T(8,128)(2,1)} %shard_map.92) | copy-start | bytes 1179652
  242.2 10.2 %copy-start.12 = (pred[384]{0:T(512)(128)(4,1)S(1)}, pred[384]{0:T(512)(128)(4,1)}, u32[]{:S(2)}) copy-start(pred[384]{0:T(512)(128)(4,1)} %iota_compare_fusion.1) | copy-start | bytes 1156
  252.5 1.2 copy-start.15
  (3 other events, 3.0 us)
Sparse Core Ops, SparseCore 0:
  47.4 105.2 all-gather.1

commit v4 on v3

--- a/solution.py
+++ b/solution.py
@@ -90,6 +90,9 @@
     to_left = [(i + 1, i) for i in range(devices) if i % TW < TW - 1]
     sideways = lambda x: (lax.ppermute(x, "seq", to_right), lax.ppermute(x, "seq", to_left))
 
+    column_groups = [[c + TW * r for r in range(grid_rows)] for c in range(TW)]
+    row_groups = [[c + TW * r for c in range(TW)] for r in range(grid_rows)]
+    weight_col = lax.all_gather(out_weight, "seq", axis=0, axis_index_groups=column_groups)
     verticals = vertical_parts(devices, grid_rows)
     left_of = lambda pairs: [(s, r + 1) for s, r in pairs if r % TW < TW - 1]
     right_of = lambda pairs: [(s, r - 1) for s, r in pairs if r % TW > 0]
@@ -121,8 +124,9 @@
         if got:
             previous = got[-1]
         if g == 0:
-            weight_part, _ = lax.optimization_barrier((out_weight, got[-1] if got else own))
-            weight_all = lax.all_gather(weight_part, "seq", axis=0, tiled=True)
+            weight_col, _ = lax.optimization_barrier((weight_col, got[-1] if got else own))
+            weight_grid = lax.all_gather(weight_col, "seq", axis=0, axis_index_groups=row_groups)
+            weight_all = jnp.swapaxes(weight_grid, 0, 1).reshape(-1, out_weight.shape[1])
         forwarded = [sideways(item) for item in got]
         base = g * group_heads
         slots = [(keys, values, base, base)]

time: 273 us -> 294 us (1.077)
  waiting for transfers between devices: 119 us -> 169 us
  starting transfers between devices: 82.5 us -> 48.5 us
  local copies, waits for them, and re-layouts: 8.7 us -> 16.9 us
    ppermute x5, waiting for transfers between devices: 18.8 us -> 67.2 us  [on_device(): fetch = lambda pairs: lax.ppermute(tile_lengths, 'seq', pairs)]
    ppermute x5, starting transfers between devices: 52.9 us -> 10.8 us  [on_device(): fetch = lambda pairs: lax.ppermute(tile_lengths, 'seq', pairs)]
    ppermute x5, starting transfers between devices: 11.2 us -> 25.9 us  [on_device(): lax.ppermute(x, 'seq', to_right)]
    transpose x0 -> x1, local copies, waits for them, and re-layouts: none -> 8.48 us  [on_device(): jnp.swapaxes(weight_grid, 0, 1).reshape(-1, out_weight.shape[1])]
    ppermute x5, starting transfers between devices: 16.5 us -> 11.1 us  [on_device(): lax.ppermute(x, 'seq', to_left)]
  transfers between devices with their start and end apart: 19 -> 20, of which waited for: 8 -> 8; matrix products, arithmetic and copies ran while one was open for 3% -> 4% of each run, Pallas kernels for 11% -> 10%
where the time goes in v4:
time: 294 us; the launch traced here: 293 us
  waiting for transfers between devices  169 us (57%)
  starting transfers between devices  48.5 us (16%)
  Pallas kernels  30.4 us (10%)
  local copies, waits for them, and re-layouts  16.9 us (6%)
  between operations  14.4 us (5%)
  matrix products  8.72 us (3%)
  other arithmetic  4.56 us (2%)
    ppermute x3, waiting for transfers between devices, on_device(): got = [lax.ppermute(own, 'seq', pairs) for pairs in verticals]  101 us
    ppermute x5, waiting for transfers between devices, on_device(): fetch = lambda pairs: lax.ppermute(tile_lengths, 'seq', pairs)  67.2 us
    pallas_call x3, Pallas kernels, group_attention(): pl.pallas_call(kernel, grid=(group_heads,), in_specs=in_specs, out_specs=...  30.4 us
    ppermute x5, starting transfers between devices, on_device(): lax.ppermute(x, 'seq', to_right)  25.9 us
    ppermute x5, starting transfers between devices, on_device(): lax.ppermute(x, 'seq', to_left)  11.1 us
    ppermute x5, starting transfers between devices, on_device(): fetch = lambda pairs: lax.ppermute(tile_lengths, 'seq', pairs)  10.8 us
    dot_general x1, matrix products, on_device(): jnp.dot(attended_all, weight_all, preferred_element_type=jnp.float32)  8.72 us
    transpose x1, local copies, waits for them, and re-layouts, on_device(): jnp.swapaxes(weight_grid, 0, 1).reshape(-1, out_weight.shape[1])  8.48 us
  transfers between devices with their start and end apart: 20, of which 8 were waited for; matrix products, arithmetic and copies ran while one was open for 4% of the time, Pallas kernels for 10%

profile of v4, /device:TPU:27, one launch (start us, length us, event | category | flops | bytes accessed | tf_op | source)
XLA Modules:
  0.0 292.8 jit_solution(3349170575652345571)
XLA Ops:
  7.3 2.3 fusion.6
  10.8 62.4 %collective-permute-done.refs_3_.refs_4_ = bf16[384,1024]{1,0:T(8,128)(2,1)} collective-permute-done((bf16[384,1024]{1,0:T(8,128)(2,1)S(1)}, bf16[384,1024]{1,0:T(8,128)(2,1)}, u32[]{:S(2)}, u32[]{:S(2)}) %collective-permute-start) | collective-permute-done | bytes 786464 | tf_op jit(solution)/shard_map/ppermute | solution.py:123
  73.2 3.5 %collective-permute-start.1 = (bf16[384,1536]{1,0:T(8,128)(2,1)S(1)}, bf16[384,1536]{1,0:T(8,128)(2,1)S(1)}, u32[]{:S(2)}, u32[]{:S(2)}) collective-permute-start(bf16[384,1536]{1,0:T(8,128)(2,1)S(1)} %copy-done), channel_id=1, source_target_pairs={{0,1},{1,2},{2,3},{3,4},{4,5},{5,6},{6,7},{8,9},{9,10},{10,11},{11... | collective-permute-start | bytes 3538952 | tf_op jit(solution)/shard_map/ppermute | solution.py:91
  76.8 1.2 pad_maximum_fusion.1
  78.1 1.9 collective-permute-start.2
  80.0 2.4 collective-permute-start.4
  82.4 2.9 %collective-permute-start.5 = (bf16[384,1536]{1,0:T(8,128)(2,1)S(1)}, bf16[384,1536]{1,0:T(8,128)(2,1)S(1)}, u32[]{:S(2)}, u32[]{:S(2)}) collective-permute-start(bf16[384,1536]{1,0:T(8,128)(2,1)S(1)} %copy-done.1), channel_id=1, source_target_pairs={{1,0},{2,1},{3,2},{4,3},{5,4},{6,5},{7,6},{9,8},{10,9},{11,10},{12... | collective-permute-start | bytes 3538952 | tf_op jit(solution)/shard_map/ppermute | solution.py:91
  85.4 1.2 pad_maximum_fusion.2
  86.6 25.1 %collective-permute-done.12.refs_3_.refs_4_ = bf16[384,1024]{1,0:T(8,128)(2,1)} collective-permute-done((bf16[384,1024]{1,0:T(8,128)(2,1)S(1)}, bf16[384,1024]{1,0:T(8,128)(2,1)}, u32[]{:S(2)}, u32[]{:S(2)}) %collective-permute-start.12) | collective-permute-done | bytes 786464 | tf_op jit(solution)/shard_map/ppermute | solution.py:123
  111.7 2.3 collective-permute-start.10
  114.0 55.8 %collective-permute-done.10 = s32[1]{0:T(128)} collective-permute-done((s32[1]{0:T(128)}, s32[1]{0:T(128)}, u32[]{:S(2)}, u32[]{:S(2)}) %collective-permute-start.10) | collective-permute-done | bytes 36 | tf_op jit(solution)/shard_map/ppermute | solution.py:99
  169.7 1.9 collective-permute-start.11
  171.7 5.0 %collective-permute-done.11 = s32[1]{0:T(128)} collective-permute-done((s32[1]{0:T(128)}, s32[1]{0:T(128)}, u32[]{:S(2)}, u32[]{:S(2)}) %collective-permute-start.11) | collective-permute-done | bytes 36 | tf_op jit(solution)/shard_map/ppermute | solution.py:99
  176.7 3.6 %collective-permute-done.7 = s32[1]{0:T(128)} collective-permute-done((s32[1]{0:T(128)}, s32[1]{0:T(128)}, u32[]{:S(2)}, u32[]{:S(2)}) %collective-permute-start.7) | collective-permute-done | bytes 36 | tf_op jit(solution)/shard_map/ppermute | solution.py:99
  180.2 1.9 collective-permute-start.8
  182.1 1.4 collective-permute-done.8
  183.5 4.6 %collective-permute-start.9 = (s32[1]{0:T(128)}, s32[1]{0:T(128)}, u32[]{:S(2)}, u32[]{:S(2)}) collective-permute-start(s32[1]{0:T(128)} %param.12), channel_id=1, source_target_pairs={{0,9},{1,10},{2,11},{3,12},{4,13},{5,14},{6,15},{8,1},{9,2},{10,3}... | collective-permute-start | bytes 20 | tf_op jit(solution)/shard_map/ppermute | solution.py:99
  188.2 1.5 collective-permute-done.9
  190.2 5.3 %collective-permute-start.3 = (bf16[384,1024]{1,0:T(8,128)(2,1)}, bf16[384,1024]{1,0:T(8,128)(2,1)}, u32[]{:S(2)}, u32[]{:S(2)}) collective-permute-start(bf16[384,1024]{1,0:T(8,128)(2,1)} %collective-permute-done.refs_3_.refs_4_), channel_id=1, source_target_pairs={{0,1},{1,2},{2,3},{3,4},{4,5},{5,6},{6,7},{8,9},{9,10},{10,11},{11... | collective-permute-start | bytes 2359304 | tf_op jit(solution)/shard_map/ppermute | solution.py:91
  196.3 1.9 collective-permute-start.6
  198.2 3.6 %collective-permute-start.13 = (bf16[384,1024]{1,0:T(8,128)(2,1)}, bf16[384,1024]{1,0:T(8,128)(2,1)S(1)}, u32[]{:S(2)}, u32[]{:S(2)}) collective-permute-start(bf16[384,1024]{1,0:T(8,128)(2,1)} %collective-permute-done.12.refs_3_.refs_4_), channel_id=1, source_target_pairs={{0,1},{1,2},{2,3},{3,4},{4,5},{5,6},{6,7},{8,9},{9,10},{10,11},{11... | collective-permute-start | bytes 2359304 | tf_op jit(solution)/shard_map/ppermute | solution.py:91
  201.9 1.9 collective-permute-start.14
  203.8 13.8 %collective-permute-done.15.refs_3_.refs_4_ = bf16[384,1024]{1,0:T(8,128)(2,1)} collective-permute-done((bf16[384,1024]{1,0:T(8,128)(2,1)S(1)}, bf16[384,1024]{1,0:T(8,128)(2,1)}, u32[]{:S(2)}, u32[]{:S(2)}) %collective-permute-start.15) | collective-permute-done | bytes 786464 | tf_op jit(solution)/shard_map/ppermute | solution.py:123
  217.7 11.5 %collective-permute-start.16 = (bf16[384,1024]{1,0:T(8,128)(2,1)}, bf16[384,1024]{1,0:T(8,128)(2,1)S(1)}, u32[]{:S(2)}, u32[]{:S(2)}) collective-permute-start(bf16[384,1024]{1,0:T(8,128)(2,1)} %collective-permute-done.15.refs_3_.refs_4_), channel_id=1, source_target_pairs={{0,1},{1,2},{2,3},{3,4},{4,5},{5,6},{6,7},{8,9},{9,10},{10,11},{11... | collective-permute-start | bytes 2359304 | tf_op jit(solution)/shard_map/ppermute | solution.py:91
  229.2 1.9 collective-permute-start.17
  231.2 3.3 %concatenate.16 = s32[6]{0:T(128)S(1)} concatenate(s32[1]{0:T(128)} %copy.12, s32[1]{0:T(128)} %collective-permute-done.7, s32[1]{0:T(128)} %collective-permute-done.8, s32[1]{0:T(128)} %collective-permute-done.9, s32[1]{0:T(128)} %collective-permute-done.10, s32[1]{0:T(128)} %collective-permute-done.11), dimensions={0} | concatenate | bytes 48 | tf_op jit(solution)/shard_map/concatenate | solution.py:111
  235.3 10.1 %shard_map.91 = bf16[384,512]{1,0:T(8,128)(2,1)} custom-call(bf16[384,1536]{1,0:T(8,128)(2,1)} %refs_0_.5, bf16[384,1536]{1,0:T(8,128)(2,1)} %refs_1_.5, bf16[384,1536]{1,0:T(8,128)(2,1)} %refs_2_.5, bf16[384,1024]{1,0:T(8,128)(2,1)} %collective-permute-done.refs_3_.refs_4_, bf16[384,1024]{1,0:T(8,128)(2,1)} %collective-permute-done.refs_3_.refs_4_, ...), custom_call_target="tpu_custom_call" | custom-call | tf_op jit(solution)/shard_map/pallas_call | solution.py:58
  246.3 10.1 %shard_map.92 = bf16[384,512]{1,0:T(8,128)(2,1)} custom-call(bf16[384,1536]{1,0:T(8,128)(2,1)} %refs_0_.5, bf16[384,1536]{1,0:T(8,128)(2,1)} %refs_1_.5, bf16[384,1536]{1,0:T(8,128)(2,1)} %refs_2_.5, bf16[384,1024]{1,0:T(8,128)(2,1)} %collective-permute-done.12.refs_3_.refs_4_, bf16[384,1024]{1,0:T(8,128)(2,1)} %collective-permute-done.12.refs_3_.refs_4_, ...), custom_call_target="tpu_custom_call" | custom-call | tf_op jit(solution)/shard_map/pallas_call | solution.py:58
  257.3 10.2 %shard_map.93 = bf16[384,512]{1,0:T(8,128)(2,1)} custom-call(bf16[384,1536]{1,0:T(8,128)(2,1)} %refs_0_.5, bf16[384,1536]{1,0:T(8,128)(2,1)} %refs_1_.5, bf16[384,1536]{1,0:T(8,128)(2,1)} %refs_2_.5, bf16[384,1024]{1,0:T(8,128)(2,1)} %collective-permute-done.15.refs_3_.refs_4_, bf16[384,1024]{1,0:T(8,128)(2,1)} %collective-permute-done.15.refs_3_.refs_4_, ...), custom_call_target="tpu_custom_call" | custom-call | tf_op jit(solution)/shard_map/pallas_call | solution.py:58
  267.5 1.1 broadcast_select_fusion.2
  268.7 8.5 %copy.11 = bf16[2,8,96,3072]{3,2,1,0:T(8,128)(2,1)} copy(bf16[2,8,96,3072]{3,2,0,1:T(8,128)(2,1)} %bitcast.20) | data formatting | bytes 18874368 | tf_op jit(solution)/shard_map/transpose | solution.py:129
  277.2 8.7 %multiply_convert_fusion = bf16[384,3072]{1,0:T(8,128)(2,1)} fusion(bf16[1536,3072]{1,0:T(8,128)(2,1)} %bitcast.21, f32[3072]{0:T(1024)S(1)} %copy-done.13, bf16[384,512]{1,0:T(8,128)(2,1)S(1)} %get-tuple-element.31, bf16[384,512]{1,0:T(8,128)(2,1)S(1)} %get-tuple-element.30, bf16[384,512]{1,0:T(8,128)(2,1)S(1)} %get-tuple-element.29), kind=kOutput, calls=%fused_computation | convolution fusion | flops 3629776896 | bytes 12988416 | tf_op jit(solution)/shard_map/dot_general | solution.py:145
  (55 shorter events, 5.4 us)
Async XLA Ops:
  6.5 3.0 %copy-start.1 = (bf16[384,1536]{1,0:T(8,128)(2,1)S(1)}, bf16[384,1536]{1,0:T(8,128)(2,1)}, u32[]{:S(2)}) copy-start(bf16[384,1536]{1,0:T(8,128)(2,1)} %refs_2_.5) | copy-start | bytes 3538948
  6.5 66.7 %all-gather.5.cloned.1.call-start = ((), (), s32[]{:S(2)}) async-start(), calls=%async_computation | async-start | bytes 1769472 | tf_op jit(solution)/shard_map/all_gather | solution.py:95
  7.3 261.4 %all-gather.7.cloned.1.call-start = ((), (), s32[]{:S(2)}) async-start(), calls=%async_computation.1 | async-start | bytes 10616832 | tf_op jit(solution)/shard_map/all_gather | solution.py:128
  10.5 62.7 %copy-start = (bf16[384,1536]{1,0:T(8,128)(2,1)S(1)}, bf16[384,1536]{1,0:T(8,128)(2,1)}, u32[]{:S(2)}) copy-start(bf16[384,1536]{1,0:T(8,128)(2,1)} %refs_1_.5) | copy-start | bytes 3538948
  10.7 62.6 %collective-permute-start = (bf16[384,1024]{1,0:T(8,128)(2,1)S(1)}, bf16[384,1024]{1,0:T(8,128)(2,1)}, u32[]{:S(2)}, u32[]{:S(2)}) collective-permute-start(bf16[384,1024]{1,0:T(8,128)(2,1)S(1)} %pad_maximum_fusion), channel_id=1, source_target_pairs={{0,8},{1,9},{2,10},{3,11},{4,12},{5,13},{6,14},{7,15},{8,0},{9,1},... | collective-permute-start | bytes 2359304 | tf_op jit(solution)/shard_map/ppermute | solution.py:123
  73.2 117.0 %collective-permute-start.1 = (bf16[384,1536]{1,0:T(8,128)(2,1)S(1)}, bf16[384,1536]{1,0:T(8,128)(2,1)S(1)}, u32[]{:S(2)}, u32[]{:S(2)}) collective-permute-start(bf16[384,1536]{1,0:T(8,128)(2,1)S(1)} %copy-done), channel_id=1, source_target_pairs={{0,1},{1,2},{2,3},{3,4},{4,5},{5,6},{6,7},{8,9},{9,10},{10,11},{11... | collective-permute-start | bytes 3538952 | tf_op jit(solution)/shard_map/ppermute | solution.py:91
  76.8 119.4 %copy-start.10 = (s32[12,2]{0,1:T(2,128)S(1)}, s32[12,2]{0,1:T(2,128)}, u32[]{:S(2)}) copy-start(s32[12,2]{0,1:T(2,128)} %param.13) | copy-start | bytes 292
  76.8 154.3 %copy-start.11 = (s32[6]{0:T(128)S(1)}, s32[6]{0:T(128)}, u32[]{:S(2)}) copy-start(s32[6]{0:T(128)} %constant.7.clone) | copy-start | bytes 76
  76.8 154.3 %copy-start.12 = (s32[6]{0:T(128)S(1)}, s32[6]{0:T(128)}, u32[]{:S(2)}) copy-start(s32[6]{0:T(128)} %constant.8.clone) | copy-start | bytes 76
  78.0 33.6 %collective-permute-start.12 = (bf16[384,1024]{1,0:T(8,128)(2,1)S(1)}, bf16[384,1024]{1,0:T(8,128)(2,1)}, u32[]{:S(2)}, u32[]{:S(2)}) collective-permute-start(bf16[384,1024]{1,0:T(8,128)(2,1)S(1)} %pad_maximum_fusion.1), channel_id=1, source_target_pairs={{0,8},{1,9},{2,10},{3,11},{4,12},{5,13},{6,14},{7,15},{8,0},{9,1},... | collective-permute-start | bytes 2359304 | tf_op jit(solution)/shard_map/ppermute | solution.py:123
  78.1 118.2 %collective-permute-start.2 = (bf16[384,1536]{1,0:T(8,128)(2,1)S(1)}, bf16[384,1536]{1,0:T(8,128)(2,1)S(1)}, u32[]{:S(2)}, u32[]{:S(2)}) collective-permute-start(bf16[384,1536]{1,0:T(8,128)(2,1)S(1)} %copy-done.1), channel_id=1, source_target_pairs={{0,1},{1,2},{2,3},{3,4},{4,5},{5,6},{6,7},{8,9},{9,10},{10,11},{11... | collective-permute-start | bytes 3538952 | tf_op jit(solution)/shard_map/ppermute | solution.py:91
  80.0 118.1 %collective-permute-start.4 = (bf16[384,1536]{1,0:T(8,128)(2,1)S(1)}, bf16[384,1536]{1,0:T(8,128)(2,1)S(1)}, u32[]{:S(2)}, u32[]{:S(2)}) collective-permute-start(bf16[384,1536]{1,0:T(8,128)(2,1)S(1)} %copy-done), channel_id=1, source_target_pairs={{1,0},{2,1},{3,2},{4,3},{5,4},{6,5},{7,6},{9,8},{10,9},{11,10},{12... | collective-permute-start | bytes 3538952 | tf_op jit(solution)/shard_map/ppermute | solution.py:91
  82.4 119.4 %collective-permute-start.5 = (bf16[384,1536]{1,0:T(8,128)(2,1)S(1)}, bf16[384,1536]{1,0:T(8,128)(2,1)S(1)}, u32[]{:S(2)}, u32[]{:S(2)}) collective-permute-start(bf16[384,1536]{1,0:T(8,128)(2,1)S(1)} %copy-done.1), channel_id=1, source_target_pairs={{1,0},{2,1},{3,2},{4,3},{5,4},{6,5},{7,6},{9,8},{10,9},{11,10},{12... | collective-permute-start | bytes 3538952 | tf_op jit(solution)/shard_map/ppermute | solution.py:91
  111.7 58.1 %collective-permute-start.10 = (s32[1]{0:T(128)}, s32[1]{0:T(128)}, u32[]{:S(2)}, u32[]{:S(2)}) collective-permute-start(s32[1]{0:T(128)} %param.12), channel_id=1, source_target_pairs={{1,0},{2,1},{3,2},{4,3},{5,4},{6,5},{7,6},{9,8},{10,9},{11,10},{12... | collective-permute-start | bytes 20 | tf_op jit(solution)/shard_map/ppermute | solution.py:99
  169.7 6.9 %collective-permute-start.11 = (s32[1]{0:T(128)}, s32[1]{0:T(128)}, u32[]{:S(2)}, u32[]{:S(2)}) collective-permute-start(s32[1]{0:T(128)} %param.12), channel_id=1, source_target_pairs={{1,8},{2,9},{3,10},{4,11},{5,12},{6,13},{7,14},{9,0},{10,1},{11,2}... | collective-permute-start | bytes 20 | tf_op jit(solution)/shard_map/ppermute | solution.py:99
  176.7 3.6 %collective-permute-start.7 = (s32[1]{0:T(128)}, s32[1]{0:T(128)}, u32[]{:S(2)}, u32[]{:S(2)}) collective-permute-start(s32[1]{0:T(128)} %param.12), channel_id=1, source_target_pairs={{0,8},{1,9},{2,10},{3,11},{4,12},{5,13},{6,14},{7,15},{8,0},{9,1},... | collective-permute-start | bytes 20 | tf_op jit(solution)/shard_map/ppermute | solution.py:99
  180.2 3.3 %collective-permute-start.8 = (s32[1]{0:T(128)}, s32[1]{0:T(128)}, u32[]{:S(2)}, u32[]{:S(2)}) collective-permute-start(s32[1]{0:T(128)} %param.12), channel_id=1, source_target_pairs={{0,1},{1,2},{2,3},{3,4},{4,5},{5,6},{6,7},{8,9},{9,10},{10,11},{11... | collective-permute-start | bytes 20 | tf_op jit(solution)/shard_map/ppermute | solution.py:99
  183.5 6.1 %collective-permute-start.9 = (s32[1]{0:T(128)}, s32[1]{0:T(128)}, u32[]{:S(2)}, u32[]{:S(2)}) collective-permute-start(s32[1]{0:T(128)} %param.12), channel_id=1, source_target_pairs={{0,9},{1,10},{2,11},{3,12},{4,13},{5,14},{6,15},{8,1},{9,2},{10,3}... | collective-permute-start | bytes 20 | tf_op jit(solution)/shard_map/ppermute | solution.py:99
  189.6 28.0 %collective-permute-start.15 = (bf16[384,1024]{1,0:T(8,128)(2,1)S(1)}, bf16[384,1024]{1,0:T(8,128)(2,1)}, u32[]{:S(2)}, u32[]{:S(2)}) collective-permute-start(bf16[384,1024]{1,0:T(8,128)(2,1)S(1)} %pad_maximum_fusion.2), channel_id=1, source_target_pairs={{0,8},{1,9},{2,10},{3,11},{4,12},{5,13},{6,14},{7,15},{8,0},{9,1},... | collective-permute-start | bytes 2359304 | tf_op jit(solution)/shard_map/ppermute | solution.py:123
  190.2 45.1 %copy-start.2 = (bf16[384,1536]{1,0:T(8,128)(2,1)}, bf16[384,1536]{1,0:T(8,128)(2,1)S(1)}, u32[]{:S(2)}) copy-start(bf16[384,1536]{1,0:T(8,128)(2,1)S(1)} %collective-permute-done.1.refs_5_) | copy-start | bytes 3538948
  190.2 39.0 %collective-permute-start.3 = (bf16[384,1024]{1,0:T(8,128)(2,1)}, bf16[384,1024]{1,0:T(8,128)(2,1)}, u32[]{:S(2)}, u32[]{:S(2)}) collective-permute-start(bf16[384,1024]{1,0:T(8,128)(2,1)} %collective-permute-done.refs_3_.refs_4_), channel_id=1, source_target_pairs={{0,1},{1,2},{2,3},{3,4},{4,5},{5,6},{6,7},{8,9},{9,10},{10,11},{11... | collective-permute-start | bytes 2359304 | tf_op jit(solution)/shard_map/ppermute | solution.py:91
  196.3 5.6 %copy-start.3 = (bf16[384,1536]{1,0:T(8,128)(2,1)}, bf16[384,1536]{1,0:T(8,128)(2,1)S(1)}, u32[]{:S(2)}) copy-start(bf16[384,1536]{1,0:T(8,128)(2,1)S(1)} %collective-permute-done.2.refs_6_) | copy-start | bytes 3538948
  196.3 39.1 %collective-permute-start.6 = (bf16[384,1024]{1,0:T(8,128)(2,1)}, bf16[384,1024]{1,0:T(8,128)(2,1)}, u32[]{:S(2)}, u32[]{:S(2)}) collective-permute-start(bf16[384,1024]{1,0:T(8,128)(2,1)} %collective-permute-done.refs_3_.refs_4_), channel_id=1, source_target_pairs={{1,0},{2,1},{3,2},{4,3},{5,4},{6,5},{7,6},{9,8},{10,9},{11,10},{12... | collective-permute-start | bytes 2359304 | tf_op jit(solution)/shard_map/ppermute | solution.py:91
  198.2 5.6 %copy-start.4 = (bf16[384,1536]{1,0:T(8,128)(2,1)}, bf16[384,1536]{1,0:T(8,128)(2,1)S(1)}, u32[]{:S(2)}) copy-start(bf16[384,1536]{1,0:T(8,128)(2,1)S(1)} %collective-permute-done.4.refs_9_) | copy-start | bytes 3538948
  198.2 47.2 %collective-permute-start.13 = (bf16[384,1024]{1,0:T(8,128)(2,1)}, bf16[384,1024]{1,0:T(8,128)(2,1)S(1)}, u32[]{:S(2)}, u32[]{:S(2)}) collective-permute-start(bf16[384,1024]{1,0:T(8,128)(2,1)} %collective-permute-done.12.refs_3_.refs_4_), channel_id=1, source_target_pairs={{0,1},{1,2},{2,3},{3,4},{4,5},{5,6},{6,7},{8,9},{9,10},{10,11},{11... | collective-permute-start | bytes 2359304 | tf_op jit(solution)/shard_map/ppermute | solution.py:91
  201.9 15.8 %copy-start.5 = (bf16[384,1536]{1,0:T(8,128)(2,1)}, bf16[384,1536]{1,0:T(8,128)(2,1)S(1)}, u32[]{:S(2)}) copy-start(bf16[384,1536]{1,0:T(8,128)(2,1)S(1)} %collective-permute-done.5.refs_10_) | copy-start | bytes 3538948
  201.9 43.6 %collective-permute-start.14 = (bf16[384,1024]{1,0:T(8,128)(2,1)}, bf16[384,1024]{1,0:T(8,128)(2,1)}, u32[]{:S(2)}, u32[]{:S(2)}) collective-permute-start(bf16[384,1024]{1,0:T(8,128)(2,1)} %collective-permute-done.12.refs_3_.refs_4_), channel_id=1, source_target_pairs={{1,0},{2,1},{3,2},{4,3},{5,4},{6,5},{7,6},{9,8},{10,9},{11,10},{12... | collective-permute-start | bytes 2359304 | tf_op jit(solution)/shard_map/ppermute | solution.py:91
  217.7 38.7 %collective-permute-start.16 = (bf16[384,1024]{1,0:T(8,128)(2,1)}, bf16[384,1024]{1,0:T(8,128)(2,1)S(1)}, u32[]{:S(2)}, u32[]{:S(2)}) collective-permute-start(bf16[384,1024]{1,0:T(8,128)(2,1)} %collective-permute-done.15.refs_3_.refs_4_), channel_id=1, source_target_pairs={{0,1},{1,2},{2,3},{3,4},{4,5},{5,6},{6,7},{8,9},{9,10},{10,11},{11... | collective-permute-start | bytes 2359304 | tf_op jit(solution)/shard_map/ppermute | solution.py:91
  229.2 27.3 %collective-permute-start.17 = (bf16[384,1024]{1,0:T(8,128)(2,1)}, bf16[384,1024]{1,0:T(8,128)(2,1)}, u32[]{:S(2)}, u32[]{:S(2)}) collective-permute-start(bf16[384,1024]{1,0:T(8,128)(2,1)} %collective-permute-done.15.refs_3_.refs_4_), channel_id=1, source_target_pairs={{1,0},{2,1},{3,2},{4,3},{5,4},{6,5},{7,6},{9,8},{10,9},{11,10},{12... | collective-permute-start | bytes 2359304 | tf_op jit(solution)/shard_map/ppermute | solution.py:91
  257.3 10.2 %copy-start.8 = (bf16[384,512]{1,0:T(8,128)(2,1)S(1)}, bf16[384,512]{1,0:T(8,128)(2,1)}, u32[]{:S(2)}) copy-start(bf16[384,512]{1,0:T(8,128)(2,1)} %shard_map.91) | copy-start | bytes 1179652
  257.3 10.2 %copy-start.9 = (bf16[384,512]{1,0:T(8,128)(2,1)S(1)}, bf16[384,512]{1,0:T(8,128)(2,1)}, u32[]{:S(2)}) copy-start(bf16[384,512]{1,0:T(8,128)(2,1)} %shard_map.92) | copy-start | bytes 1179652
  268.7 8.5 %copy-start.13 = (f32[3072]{0:T(1024)S(1)}, f32[3072]{0:T(1024)}, u32[]{:S(2)}) copy-start(f32[3072]{0:T(1024)} %param.15) | copy-start | bytes 36868
  (2 other events, 1.8 us)
Sparse Core Ops, SparseCore 0:
  8.9 60.3 all-gather.4
  73.4 92.5 all-gather.6

commit v5 on v3

--- a/solution.py
+++ b/solution.py
@@ -8,7 +8,7 @@
 
 
 TW = 8
-GROUPS = 3
+GROUPS = 2
 
 
 def group_attention(queries, slots, usable, head_base, group_heads, head_dim, score_scale):
@@ -90,6 +90,7 @@
     to_left = [(i + 1, i) for i in range(devices) if i % TW < TW - 1]
     sideways = lambda x: (lax.ppermute(x, "seq", to_right), lax.ppermute(x, "seq", to_left))
 
+    weight_all = lax.all_gather(out_weight, "seq", axis=0, tiled=True)
     verticals = vertical_parts(devices, grid_rows)
     left_of = lambda pairs: [(s, r + 1) for s, r in pairs if r % TW < TW - 1]
     right_of = lambda pairs: [(s, r - 1) for s, r in pairs if r % TW > 0]
@@ -120,9 +121,6 @@
         got = [lax.ppermute(own, "seq", pairs) for pairs in verticals]
         if got:
             previous = got[-1]
-        if g == 0:
-            weight_part, _ = lax.optimization_barrier((out_weight, got[-1] if got else own))
-            weight_all = lax.all_gather(weight_part, "seq", axis=0, tiled=True)
         forwarded = [sideways(item) for item in got]
         base = g * group_heads
         slots = [(keys, values, base, base)]

time: 273 us -> 291 us (1.066)
  waiting for transfers between devices: 119 us -> 184 us
  starting transfers between devices: 82.5 us -> 43 us
    ppermute x5, waiting for transfers between devices: 18.8 us -> 53.9 us  [on_device(): fetch = lambda pairs: lax.ppermute(tile_lengths, 'seq', pairs)]
    ppermute x5 -> x4, waiting for transfers between devices: 0.01 us -> 34.8 us  [on_device(): lax.ppermute(x, 'seq', to_left)]
    ppermute x5, starting transfers between devices: 52.9 us -> 18.1 us  [on_device(): fetch = lambda pairs: lax.ppermute(tile_lengths, 'seq', pairs)]
    ppermute x3 -> x2, waiting for transfers between devices: 101 us -> 94.1 us  [on_device(): got = [lax.ppermute(own, 'seq', pairs) for pairs in verticals]]
    ppermute x5 -> x4, starting transfers between devices: 16.5 us -> 14 us  [on_device(): lax.ppermute(x, 'seq', to_left)]
    pallas_call x3 -> x2, Pallas kernels: 30.4 us -> 28.3 us  [group_attention(): pl.pallas_call(kernel, grid=(group_heads,), in_specs=in_specs, out_specs=...]
    ppermute x5 -> x4, starting transfers between devices: 11.2 us -> 10.7 us  [on_device(): lax.ppermute(x, 'seq', to_right)]
  transfers between devices with their start and end apart: 19 -> 16, of which waited for: 8 -> 8; matrix products, arithmetic and copies ran while one was open for 3% -> 2% of each run, Pallas kernels for 11% -> 10%
where the time goes in v5:
time: 291 us; the launch traced here: 288 us
  waiting for transfers between devices  184 us (63%)
  starting transfers between devices  43 us (15%)
  Pallas kernels  28.3 us (10%)
  between operations  14.4 us (5%)
  matrix products  8.82 us (3%)
  local copies, waits for them, and re-layouts  8.19 us (3%)
    ppermute x2, waiting for transfers between devices, on_device(): got = [lax.ppermute(own, 'seq', pairs) for pairs in verticals]  94.1 us
    ppermute x5, waiting for transfers between devices, on_device(): fetch = lambda pairs: lax.ppermute(tile_lengths, 'seq', pairs)  53.9 us
    ppermute x4, waiting for transfers between devices, on_device(): lax.ppermute(x, 'seq', to_left)  34.8 us
    pallas_call x2, Pallas kernels, group_attention(): pl.pallas_call(kernel, grid=(group_heads,), in_specs=in_specs, out_specs=...  28.3 us
    ppermute x5, starting transfers between devices, on_device(): fetch = lambda pairs: lax.ppermute(tile_lengths, 'seq', pairs)  18.1 us
    ppermute x4, starting transfers between devices, on_device(): lax.ppermute(x, 'seq', to_left)  14 us
    ppermute x4, starting transfers between devices, on_device(): lax.ppermute(x, 'seq', to_right)  10.7 us
    dot_general x1, matrix products, on_device(): jnp.dot(attended_all, weight_all, preferred_element_type=jnp.float32)  8.82 us
  transfers between devices with their start and end apart: 16, of which 8 were waited for; matrix products, arithmetic and copies ran while one was open for 2% of the time, Pallas kernels for 10%

profile of v5, /device:TPU:27, one launch (start us, length us, event | category | flops | bytes accessed | tf_op | source)
XLA Modules:
  0.0 288.4 jit_solution(13846643900277384372)
XLA Ops:
  6.5 0.7 all-gather.2.cloned.1.call-update
  7.3 1.4 fusion.4
  8.7 0.2 copy-done.1
  9.2 1.1 copy-done
  10.2 3.7 %collective-permute-start.1 = (bf16[384,1536]{1,0:T(8,128)(2,1)S(1)}, bf16[384,1536]{1,0:T(8,128)(2,1)S(1)}, u32[]{:S(2)}, u32[]{:S(2)}) collective-permute-start(bf16[384,1536]{1,0:T(8,128)(2,1)S(1)} %copy-done), channel_id=1, source_target_pairs={{0,1},{1,2},{2,3},{3,4},{4,5},{5,6},{6,7},{8,9},{9,10},{10,11},{11... | collective-permute-start | bytes 3538952 | tf_op jit(solution)/shard_map/ppermute | solution.py:91
  13.9 1.9 collective-permute-start.2
  16.0 94.1 %collective-permute-done.refs_3_.refs_4_ = bf16[384,1536]{1,0:T(8,128)(2,1)} collective-permute-done((bf16[384,1536]{1,0:T(8,128)(2,1)S(1)}, bf16[384,1536]{1,0:T(8,128)(2,1)}, u32[]{:S(2)}, u32[]{:S(2)}) %collective-permute-start) | collective-permute-done | bytes 1179680 | tf_op jit(solution)/shard_map/ppermute | solution.py:121
  110.1 3.3 %collective-permute-start.4 = (bf16[384,1536]{1,0:T(8,128)(2,1)S(1)}, bf16[384,1536]{1,0:T(8,128)(2,1)S(1)}, u32[]{:S(2)}, u32[]{:S(2)}) collective-permute-start(bf16[384,1536]{1,0:T(8,128)(2,1)S(1)} %copy-done), channel_id=1, source_target_pairs={{1,0},{2,1},{3,2},{4,3},{5,4},{6,5},{7,6},{9,8},{10,9},{11,10},{12... | collective-permute-start | bytes 3538952 | tf_op jit(solution)/shard_map/ppermute | solution.py:91
  113.4 1.9 collective-permute-start.10
  115.3 12.7 %collective-permute-done.10 = s32[1]{0:T(128)} collective-permute-done((s32[1]{0:T(128)}, s32[1]{0:T(128)}, u32[]{:S(2)}, u32[]{:S(2)}) %collective-permute-start.10) | collective-permute-done | bytes 36 | tf_op jit(solution)/shard_map/ppermute | solution.py:97
  128.0 9.0 %collective-permute-start.11 = (s32[1]{0:T(128)}, s32[1]{0:T(128)}, u32[]{:S(2)}, u32[]{:S(2)}) collective-permute-start(s32[1]{0:T(128)} %param.12), channel_id=1, source_target_pairs={{1,8},{2,9},{3,10},{4,11},{5,12},{6,13},{7,14},{9,0},{10,1},{11,2}... | collective-permute-start | bytes 20 | tf_op jit(solution)/shard_map/ppermute | solution.py:97
  137.0 34.5 %collective-permute-done.11 = s32[1]{0:T(128)} collective-permute-done((s32[1]{0:T(128)}, s32[1]{0:T(128)}, u32[]{:S(2)}, u32[]{:S(2)}) %collective-permute-start.11) | collective-permute-done | bytes 36 | tf_op jit(solution)/shard_map/ppermute | solution.py:97
  171.5 3.4 %collective-permute-done.7 = s32[1]{0:T(128)} collective-permute-done((s32[1]{0:T(128)}, s32[1]{0:T(128)}, u32[]{:S(2)}, u32[]{:S(2)}) %collective-permute-start.7) | collective-permute-done | bytes 36 | tf_op jit(solution)/shard_map/ppermute | solution.py:97
  174.9 3.7 %collective-permute-start.8 = (s32[1]{0:T(128)}, s32[1]{0:T(128)}, u32[]{:S(2)}, u32[]{:S(2)}) collective-permute-start(s32[1]{0:T(128)} %param.12), channel_id=1, source_target_pairs={{0,1},{1,2},{2,3},{3,4},{4,5},{5,6},{6,7},{8,9},{9,10},{10,11},{11... | collective-permute-start | bytes 20 | tf_op jit(solution)/shard_map/ppermute | solution.py:97
  178.5 0.8 collective-permute-done.8
  179.4 3.6 %collective-permute-start.9 = (s32[1]{0:T(128)}, s32[1]{0:T(128)}, u32[]{:S(2)}, u32[]{:S(2)}) collective-permute-start(s32[1]{0:T(128)} %param.12), channel_id=1, source_target_pairs={{0,9},{1,10},{2,11},{3,12},{4,13},{5,14},{6,15},{8,1},{9,2},{10,3}... | collective-permute-start | bytes 20 | tf_op jit(solution)/shard_map/ppermute | solution.py:97
  182.9 2.4 collective-permute-done.9
  185.4 5.6 %collective-permute-start.5 = (bf16[384,1536]{1,0:T(8,128)(2,1)S(1)}, bf16[384,1536]{1,0:T(8,128)(2,1)}, u32[]{:S(2)}, u32[]{:S(2)}) collective-permute-start(bf16[384,1536]{1,0:T(8,128)(2,1)S(1)} %copy-done.1), channel_id=1, source_target_pairs={{1,0},{2,1},{3,2},{4,3},{5,4},{6,5},{7,6},{9,8},{10,9},{11,10},{12... | collective-permute-start | bytes 3538952 | tf_op jit(solution)/shard_map/ppermute | solution.py:91
  191.0 1.9 collective-permute-start.3
  192.9 2.4 collective-permute-start.6
  195.3 3.2 %collective-permute-start.13 = (bf16[384,1536]{1,0:T(8,128)(2,1)}, bf16[384,1536]{1,0:T(8,128)(2,1)}, u32[]{:S(2)}, u32[]{:S(2)}) collective-permute-start(bf16[384,1536]{1,0:T(8,128)(2,1)} %collective-permute-done.12.refs_3_.refs_4_), channel_id=1, source_target_pairs={{0,1},{1,2},{2,3},{3,4},{4,5},{5,6},{6,7},{8,9},{9,10},{10,11},{11... | collective-permute-start | bytes 3538952 | tf_op jit(solution)/shard_map/ppermute | solution.py:91
  198.5 1.0 copy-done.4
  199.6 2.8 collective-permute-start.14
  203.2 3.3 %concatenate.13 = s32[6]{0:T(128)S(1)} concatenate(s32[1]{0:T(128)} %copy.10, s32[1]{0:T(128)} %collective-permute-done.7, s32[1]{0:T(128)} %collective-permute-done.8, s32[1]{0:T(128)} %collective-permute-done.9, s32[1]{0:T(128)} %collective-permute-done.10, s32[1]{0:T(128)} %collective-permute-done.11), dimensions={0} | concatenate | bytes 48 | tf_op jit(solution)/shard_map/concatenate | solution.py:109
  206.6 0.7 and_convert_fusion.1
  207.3 22.2 %collective-permute-done.5.refs_10_ = bf16[384,1536]{1,0:T(8,128)(2,1)} collective-permute-done((bf16[384,1536]{1,0:T(8,128)(2,1)S(1)}, bf16[384,1536]{1,0:T(8,128)(2,1)}, u32[]{:S(2)}, u32[]{:S(2)}) %collective-permute-start.5) | collective-permute-done | bytes 1179680 | tf_op jit(solution)/shard_map/ppermute | solution.py:91
  229.5 12.6 %collective-permute-done.6.refs_11_.refs_12_ = bf16[384,1536]{1,0:T(8,128)(2,1)} collective-permute-done((bf16[384,1536]{1,0:T(8,128)(2,1)}, bf16[384,1536]{1,0:T(8,128)(2,1)}, u32[]{:S(2)}, u32[]{:S(2)}) %collective-permute-start.6) | collective-permute-done | bytes 1179680 | tf_op jit(solution)/shard_map/ppermute | solution.py:91
  242.2 14.1 %shard_map.91 = bf16[384,768]{1,0:T(8,128)(2,1)} custom-call(bf16[384,1536]{1,0:T(8,128)(2,1)} %refs_0_.3, bf16[384,1536]{1,0:T(8,128)(2,1)} %refs_1_.3, bf16[384,1536]{1,0:T(8,128)(2,1)} %refs_2_.3, bf16[384,1536]{1,0:T(8,128)(2,1)} %collective-permute-done.refs_3_.refs_4_, bf16[384,1536]{1,0:T(8,128)(2,1)} %collective-permute-done.refs_3_.refs_4_, ...), custom_call_target="tpu_custom_call" | custom-call | tf_op jit(solution)/shard_map/pallas_call | solution.py:58
  256.3 1.0 copy-done.5
  257.3 14.2 %shard_map.92 = bf16[384,768]{1,0:T(8,128)(2,1)} custom-call(bf16[384,1536]{1,0:T(8,128)(2,1)} %refs_0_.3, bf16[384,1536]{1,0:T(8,128)(2,1)} %refs_1_.3, bf16[384,1536]{1,0:T(8,128)(2,1)} %refs_2_.3, bf16[384,1536]{1,0:T(8,128)(2,1)} %collective-permute-done.12.refs_3_.refs_4_, bf16[384,1536]{1,0:T(8,128)(2,1)} %collective-permute-done.12.refs_3_.refs_4_, ...), custom_call_target="tpu_custom_call" | custom-call | tf_op jit(solution)/shard_map/pallas_call | solution.py:58
  271.5 1.2 broadcast_select_fusion.1
  272.8 8.8 %multiply_convert_fusion = bf16[384,3072]{1,0:T(8,128)(2,1)} fusion(bf16[1536,3072]{1,0:T(8,128)(2,1)} %all-gather.2.cloned.1.call-done, f32[3072]{0:T(1024)S(1)} %copy-done.10, bf16[384,768]{1,0:T(8,128)(2,1)S(1)} %get-tuple-element.20, bf16[384,768]{1,0:T(8,128)(2,1)S(1)} %get-tuple-element.19), kind=kOutput, calls=%fused_computation | convolution fusion | flops 3628597248 | bytes 12988416 | tf_op jit(solution)/shard_map/dot_general | solution.py:139
  (37 shorter events, 0.7 us)
Async XLA Ops:
  6.5 266.2 %all-gather.2.cloned.1.call-start = ((), (), s32[]{:S(2)}) async-start(), calls=%async_computation | async-start | bytes 10027008 | tf_op jit(solution)/shard_map/all_gather | solution.py:93
  7.3 1.6 copy-start.1
  9.0 1.3 copy-start
  9.1 101.0 %collective-permute-start = (bf16[384,1536]{1,0:T(8,128)(2,1)S(1)}, bf16[384,1536]{1,0:T(8,128)(2,1)}, u32[]{:S(2)}, u32[]{:S(2)}) collective-permute-start(bf16[384,1536]{1,0:T(8,128)(2,1)S(1)} %pad_maximum_fusion), channel_id=1, source_target_pairs={{0,8},{1,9},{2,10},{3,11},{4,12},{5,13},{6,14},{7,15},{8,0},{9,1},... | collective-permute-start | bytes 3538952 | tf_op jit(solution)/shard_map/ppermute | solution.py:121
  10.2 180.7 %collective-permute-start.1 = (bf16[384,1536]{1,0:T(8,128)(2,1)S(1)}, bf16[384,1536]{1,0:T(8,128)(2,1)S(1)}, u32[]{:S(2)}, u32[]{:S(2)}) collective-permute-start(bf16[384,1536]{1,0:T(8,128)(2,1)S(1)} %copy-done), channel_id=1, source_target_pairs={{0,1},{1,2},{2,3},{3,4},{4,5},{5,6},{6,7},{8,9},{9,10},{10,11},{11... | collective-permute-start | bytes 3538952 | tf_op jit(solution)/shard_map/ppermute | solution.py:91
  13.9 179.0 %collective-permute-start.2 = (bf16[384,1536]{1,0:T(8,128)(2,1)S(1)}, bf16[384,1536]{1,0:T(8,128)(2,1)S(1)}, u32[]{:S(2)}, u32[]{:S(2)}) collective-permute-start(bf16[384,1536]{1,0:T(8,128)(2,1)S(1)} %copy-done.1), channel_id=1, source_target_pairs={{0,1},{1,2},{2,3},{3,4},{4,5},{5,6},{6,7},{8,9},{9,10},{10,11},{11... | collective-permute-start | bytes 3538952 | tf_op jit(solution)/shard_map/ppermute | solution.py:91
  15.9 187.2 %copy-start.7 = (s32[12,2]{0,1:T(2,128)S(1)}, s32[12,2]{0,1:T(2,128)}, u32[]{:S(2)}) copy-start(s32[12,2]{0,1:T(2,128)} %param.13) | copy-start | bytes 292
  15.9 187.2 %copy-start.8 = (s32[6]{0:T(128)S(1)}, s32[6]{0:T(128)}, u32[]{:S(2)}) copy-start(s32[6]{0:T(128)} %constant.7.clone) | copy-start | bytes 76
  15.9 187.2 %copy-start.9 = (s32[6]{0:T(128)S(1)}, s32[6]{0:T(128)}, u32[]{:S(2)}) copy-start(s32[6]{0:T(128)} %constant.8.clone) | copy-start | bytes 76
  110.1 85.2 %collective-permute-start.12 = (bf16[384,1536]{1,0:T(8,128)(2,1)S(1)}, bf16[384,1536]{1,0:T(8,128)(2,1)}, u32[]{:S(2)}, u32[]{:S(2)}) collective-permute-start(bf16[384,1536]{1,0:T(8,128)(2,1)S(1)} %pad_maximum_fusion.1), channel_id=1, source_target_pairs={{0,8},{1,9},{2,10},{3,11},{4,12},{5,13},{6,14},{7,15},{8,0},{9,1},... | collective-permute-start | bytes 3538952 | tf_op jit(solution)/shard_map/ppermute | solution.py:121
  110.1 88.4 %collective-permute-start.4 = (bf16[384,1536]{1,0:T(8,128)(2,1)S(1)}, bf16[384,1536]{1,0:T(8,128)(2,1)S(1)}, u32[]{:S(2)}, u32[]{:S(2)}) collective-permute-start(bf16[384,1536]{1,0:T(8,128)(2,1)S(1)} %copy-done), channel_id=1, source_target_pairs={{1,0},{2,1},{3,2},{4,3},{5,4},{6,5},{7,6},{9,8},{10,9},{11,10},{12... | collective-permute-start | bytes 3538952 | tf_op jit(solution)/shard_map/ppermute | solution.py:91
  113.4 14.7 %collective-permute-start.10 = (s32[1]{0:T(128)}, s32[1]{0:T(128)}, u32[]{:S(2)}, u32[]{:S(2)}) collective-permute-start(s32[1]{0:T(128)} %param.12), channel_id=1, source_target_pairs={{1,0},{2,1},{3,2},{4,3},{5,4},{6,5},{7,6},{9,8},{10,9},{11,10},{12... | collective-permute-start | bytes 20 | tf_op jit(solution)/shard_map/ppermute | solution.py:97
  128.0 43.4 %collective-permute-start.11 = (s32[1]{0:T(128)}, s32[1]{0:T(128)}, u32[]{:S(2)}, u32[]{:S(2)}) collective-permute-start(s32[1]{0:T(128)} %param.12), channel_id=1, source_target_pairs={{1,8},{2,9},{3,10},{4,11},{5,12},{6,13},{7,14},{9,0},{10,1},{11,2}... | collective-permute-start | bytes 20 | tf_op jit(solution)/shard_map/ppermute | solution.py:97
  171.5 3.4 %collective-permute-start.7 = (s32[1]{0:T(128)}, s32[1]{0:T(128)}, u32[]{:S(2)}, u32[]{:S(2)}) collective-permute-start(s32[1]{0:T(128)} %param.12), channel_id=1, source_target_pairs={{0,8},{1,9},{2,10},{3,11},{4,12},{5,13},{6,14},{7,15},{8,0},{9,1},... | collective-permute-start | bytes 20 | tf_op jit(solution)/shard_map/ppermute | solution.py:97
  174.9 4.5 %collective-permute-start.8 = (s32[1]{0:T(128)}, s32[1]{0:T(128)}, u32[]{:S(2)}, u32[]{:S(2)}) collective-permute-start(s32[1]{0:T(128)} %param.12), channel_id=1, source_target_pairs={{0,1},{1,2},{2,3},{3,4},{4,5},{5,6},{6,7},{8,9},{9,10},{10,11},{11... | collective-permute-start | bytes 20 | tf_op jit(solution)/shard_map/ppermute | solution.py:97
  179.4 6.0 %collective-permute-start.9 = (s32[1]{0:T(128)}, s32[1]{0:T(128)}, u32[]{:S(2)}, u32[]{:S(2)}) collective-permute-start(s32[1]{0:T(128)} %param.12), channel_id=1, source_target_pairs={{0,9},{1,10},{2,11},{3,12},{4,13},{5,14},{6,15},{8,1},{9,2},{10,3}... | collective-permute-start | bytes 20 | tf_op jit(solution)/shard_map/ppermute | solution.py:97
  185.4 44.1 %collective-permute-start.5 = (bf16[384,1536]{1,0:T(8,128)(2,1)S(1)}, bf16[384,1536]{1,0:T(8,128)(2,1)}, u32[]{:S(2)}, u32[]{:S(2)}) collective-permute-start(bf16[384,1536]{1,0:T(8,128)(2,1)S(1)} %copy-done.1), channel_id=1, source_target_pairs={{1,0},{2,1},{3,2},{4,3},{5,4},{6,5},{7,6},{9,8},{10,9},{11,10},{12... | collective-permute-start | bytes 3538952 | tf_op jit(solution)/shard_map/ppermute | solution.py:91
  191.0 51.2 %copy-start.2 = (bf16[384,1536]{1,0:T(8,128)(2,1)}, bf16[384,1536]{1,0:T(8,128)(2,1)S(1)}, u32[]{:S(2)}) copy-start(bf16[384,1536]{1,0:T(8,128)(2,1)S(1)} %collective-permute-done.1.refs_5_) | copy-start | bytes 3538948
  191.0 38.6 %collective-permute-start.3 = (bf16[384,1536]{1,0:T(8,128)(2,1)}, bf16[384,1536]{1,0:T(8,128)(2,1)}, u32[]{:S(2)}, u32[]{:S(2)}) collective-permute-start(bf16[384,1536]{1,0:T(8,128)(2,1)} %collective-permute-done.refs_3_.refs_4_), channel_id=1, source_target_pairs={{0,1},{1,2},{2,3},{3,4},{4,5},{5,6},{6,7},{8,9},{9,10},{10,11},{11... | collective-permute-start | bytes 3538952 | tf_op jit(solution)/shard_map/ppermute | solution.py:91
  192.9 5.6 %copy-start.3 = (bf16[384,1536]{1,0:T(8,128)(2,1)}, bf16[384,1536]{1,0:T(8,128)(2,1)S(1)}, u32[]{:S(2)}) copy-start(bf16[384,1536]{1,0:T(8,128)(2,1)S(1)} %collective-permute-done.2.refs_6_) | copy-start | bytes 3538948
  192.9 49.2 %collective-permute-start.6 = (bf16[384,1536]{1,0:T(8,128)(2,1)}, bf16[384,1536]{1,0:T(8,128)(2,1)}, u32[]{:S(2)}, u32[]{:S(2)}) collective-permute-start(bf16[384,1536]{1,0:T(8,128)(2,1)} %collective-permute-done.refs_3_.refs_4_), channel_id=1, source_target_pairs={{1,0},{2,1},{3,2},{4,3},{5,4},{6,5},{7,6},{9,8},{10,9},{11,10},{12... | collective-permute-start | bytes 3538952 | tf_op jit(solution)/shard_map/ppermute | solution.py:91
  195.3 60.9 %collective-permute-start.13 = (bf16[384,1536]{1,0:T(8,128)(2,1)}, bf16[384,1536]{1,0:T(8,128)(2,1)}, u32[]{:S(2)}, u32[]{:S(2)}) collective-permute-start(bf16[384,1536]{1,0:T(8,128)(2,1)} %collective-permute-done.12.refs_3_.refs_4_), channel_id=1, source_target_pairs={{0,1},{1,2},{2,3},{3,4},{4,5},{5,6},{6,7},{8,9},{9,10},{10,11},{11... | collective-permute-start | bytes 3538952 | tf_op jit(solution)/shard_map/ppermute | solution.py:91
  198.5 1.0 copy-start.4
  199.6 56.7 %collective-permute-start.14 = (bf16[384,1536]{1,0:T(8,128)(2,1)}, bf16[384,1536]{1,0:T(8,128)(2,1)S(1)}, u32[]{:S(2)}, u32[]{:S(2)}) collective-permute-start(bf16[384,1536]{1,0:T(8,128)(2,1)} %collective-permute-done.12.refs_3_.refs_4_), channel_id=1, source_target_pairs={{1,0},{2,1},{3,2},{4,3},{5,4},{6,5},{7,6},{9,8},{10,9},{11,10},{12... | collective-permute-start | bytes 3538952 | tf_op jit(solution)/shard_map/ppermute | solution.py:91
  256.3 1.0 copy-start.5
  257.3 14.2 %copy-start.6 = (bf16[384,768]{1,0:T(8,128)(2,1)S(1)}, bf16[384,768]{1,0:T(8,128)(2,1)}, u32[]{:S(2)}) copy-start(bf16[384,768]{1,0:T(8,128)(2,1)} %shard_map.91) | copy-start | bytes 1769476
  271.5 1.3 copy-start.10
Sparse Core Ops, SparseCore 0:
  9.6 148.2 all-gather.1

commit v6 on v5

--- a/solution.py
+++ b/solution.py
@@ -8,7 +8,7 @@
 
 
 TW = 8
-GROUPS = 2
+GROUPS = 3
 
 
 def group_attention(queries, slots, usable, head_base, group_heads, head_dim, score_scale):
@@ -90,7 +90,10 @@
     to_left = [(i + 1, i) for i in range(devices) if i % TW < TW - 1]
     sideways = lambda x: (lax.ppermute(x, "seq", to_right), lax.ppermute(x, "seq", to_left))
 
-    weight_all = lax.all_gather(out_weight, "seq", axis=0, tiled=True)
+    parity_groups = [list(range(p, devices, 2)) for p in range(2)]
+    weight_same = lax.all_gather(
+        out_weight, "seq", axis=0, tiled=True, axis_index_groups=parity_groups
+    )
     verticals = vertical_parts(devices, grid_rows)
     left_of = lambda pairs: [(s, r + 1) for s, r in pairs if r % TW < TW - 1]
     right_of = lambda pairs: [(s, r - 1) for s, r in pairs if r % TW > 0]
@@ -121,6 +124,9 @@
         got = [lax.ppermute(own, "seq", pairs) for pairs in verticals]
         if got:
             previous = got[-1]
+        if g == min(1, groups - 1):
+            weight_same, _ = lax.optimization_barrier((weight_same, got[-1] if got else own))
+            weight_other = lax.ppermute(weight_same, "seq", [(i, i ^ 1) for i in range(devices)])
         forwarded = [sideways(item) for item in got]
         base = g * group_heads
         slots = [(keys, values, base, base)]
@@ -136,7 +142,14 @@
         outputs.append(jnp.where(query_real[:, None], attended, 0))
 
     attended_all = jnp.concatenate(outputs, axis=1)
-    projected = jnp.dot(attended_all, weight_all, preferred_element_type=jnp.float32)
+    shard_rows = out_weight.shape[0]
+    split = attended_all.reshape(tile_rows, devices // 2, 2, shard_rows)
+    parity = lax.axis_index("seq") % 2
+    same = jnp.where(parity == 0, split[:, :, 0], split[:, :, 1]).reshape(tile_rows, -1)
+    other = jnp.where(parity == 0, split[:, :, 1], split[:, :, 0]).reshape(tile_rows, -1)
+    projected = jnp.dot(same, weight_same, preferred_element_type=jnp.float32) + jnp.dot(
+        other, weight_other, preferred_element_type=jnp.float32
+    )
     return (projected * gate[None, :]).astype(jnp.bfloat16)
 
 

time: 291 us -> 306 us (1.052)
  starting transfers between devices: 43 us -> 53.9 us
    ppermute x2 -> x3, waiting for transfers between devices: 94.1 us -> 129 us  [on_device(): got = [lax.ppermute(own, 'seq', pairs) for pairs in verticals]]
    ppermute x4 -> x5, waiting for transfers between devices: 34.8 us -> 11.4 us  [on_device(): lax.ppermute(x, 'seq', to_left)]
    ppermute x4 -> x5, starting transfers between devices: 10.7 us -> 22.5 us  [on_device(): lax.ppermute(x, 'seq', to_right)]
    ppermute x5, waiting for transfers between devices: 53.9 us -> 42.4 us  [on_device(): fetch = lambda pairs: lax.ppermute(tile_lengths, 'seq', pairs)]
    ppermute x5, starting transfers between devices: 18.1 us -> 13 us  [on_device(): fetch = lambda pairs: lax.ppermute(tile_lengths, 'seq', pairs)]
    ppermute x4 -> x5, starting transfers between devices: 14 us -> 17 us  [on_device(): lax.ppermute(x, 'seq', to_left)]
    pallas_call x2 -> x3, Pallas kernels: 28.3 us -> 30.4 us  [group_attention(): pl.pallas_call(kernel, grid=(group_heads,), in_specs=in_specs, out_specs=...]
    dot_general x1 -> x2, matrix products: 8.82 us -> 8 us  [the longest x1 4.52 us: on_device(): jnp.dot(other, weight_other, preferred_element_type=jnp.float32)]
  transfers between devices with their start and end apart: 16 -> 20, of which waited for: 8 -> 10; matrix products, arithmetic and copies ran while one was open for 2% -> 4% of each run, Pallas kernels for 10% -> 10%
where the time goes in v6:
time: 306 us; the launch traced here: 305 us
  waiting for transfers between devices  185 us (60%)
  starting transfers between devices  53.9 us (18%)
  Pallas kernels  30.4 us (10%)
  between operations  14.4 us (5%)
  local copies, waits for them, and re-layouts  8.12 us (3%)
  matrix products  8 us (3%)
  other arithmetic  4.51 us (1%)
    ppermute x3, waiting for transfers between devices, on_device(): got = [lax.ppermute(own, 'seq', pairs) for pairs in verticals]  129 us
    ppermute x5, waiting for transfers between devices, on_device(): fetch = lambda pairs: lax.ppermute(tile_lengths, 'seq', pairs)  42.4 us
    pallas_call x3, Pallas kernels, group_attention(): pl.pallas_call(kernel, grid=(group_heads,), in_specs=in_specs, out_specs=...  30.4 us
    ppermute x5, starting transfers between devices, on_device(): lax.ppermute(x, 'seq', to_right)  22.5 us
    ppermute x5, starting transfers between devices, on_device(): lax.ppermute(x, 'seq', to_left)  17 us
    ppermute x5, starting transfers between devices, on_device(): fetch = lambda pairs: lax.ppermute(tile_lengths, 'seq', pairs)  13 us
    ppermute x5, waiting for transfers between devices, on_device(): lax.ppermute(x, 'seq', to_left)  11.4 us
  transfers between devices with their start and end apart: 20, of which 10 were waited for; matrix products, arithmetic and copies ran while one was open for 4% of the time, Pallas kernels for 10%

profile of v6, /device:TPU:27, one launch (start us, length us, event | category | flops | bytes accessed | tf_op | source)
XLA Modules:
  0.0 304.8 jit_solution(15540444717430557872)
XLA Ops:
  7.3 2.1 fusion
  10.5 56.0 %collective-permute-done.refs_3_.refs_4_ = bf16[384,1024]{1,0:T(8,128)(2,1)} collective-permute-done((bf16[384,1024]{1,0:T(8,128)(2,1)S(1)}, bf16[384,1024]{1,0:T(8,128)(2,1)}, u32[]{:S(2)}, u32[]{:S(2)}) %collective-permute-start) | collective-permute-done | bytes 786464 | tf_op jit(solution)/shard_map/ppermute | solution.py:124
  66.5 70.4 %collective-permute-done.12.refs_3_.refs_4_ = bf16[384,1024]{1,0:T(8,128)(2,1)S(1)} collective-permute-done((bf16[384,1024]{1,0:T(8,128)(2,1)S(1)}, bf16[384,1024]{1,0:T(8,128)(2,1)S(1)}, u32[]{:S(2)}, u32[]{:S(2)}) %collective-permute-start.12) | collective-permute-done | bytes 786464 | tf_op jit(solution)/shard_map/ppermute | solution.py:124
  136.9 2.1 all-gather.2.cloned.1.call-done
  139.5 3.0 collective-permute-start.1
  142.5 2.4 collective-permute-start.2
  144.9 1.9 collective-permute-start.4
  146.9 3.5 %collective-permute-start.10 = (s32[1]{0:T(128)}, s32[1]{0:T(128)}, u32[]{:S(2)}, u32[]{:S(2)}) collective-permute-start(s32[1]{0:T(128)} %param.12), channel_id=1, source_target_pairs={{1,0},{2,1},{3,2},{4,3},{5,4},{6,5},{7,6},{9,8},{10,9},{11,10},{12... | collective-permute-start | bytes 20 | tf_op jit(solution)/shard_map/ppermute | solution.py:100
  150.3 32.2 %collective-permute-done.10 = s32[1]{0:T(128)} collective-permute-done((s32[1]{0:T(128)}, s32[1]{0:T(128)}, u32[]{:S(2)}, u32[]{:S(2)}) %collective-permute-start.10) | collective-permute-done | bytes 36 | tf_op jit(solution)/shard_map/ppermute | solution.py:100
  182.6 1.9 collective-permute-start.11
  184.5 5.0 %collective-permute-done.11 = s32[1]{0:T(128)} collective-permute-done((s32[1]{0:T(128)}, s32[1]{0:T(128)}, u32[]{:S(2)}, u32[]{:S(2)}) %collective-permute-start.11) | collective-permute-done | bytes 36 | tf_op jit(solution)/shard_map/ppermute | solution.py:100
  190.6 2.5 collective-permute-done.7
  193.1 1.9 collective-permute-start.8
  195.0 1.4 collective-permute-done.8
  196.4 4.6 %collective-permute-start.9 = (s32[1]{0:T(128)}, s32[1]{0:T(128)}, u32[]{:S(2)}, u32[]{:S(2)}) collective-permute-start(s32[1]{0:T(128)} %param.12), channel_id=1, source_target_pairs={{0,9},{1,10},{2,11},{3,12},{4,13},{5,14},{6,15},{8,1},{9,2},{10,3}... | collective-permute-start | bytes 20 | tf_op jit(solution)/shard_map/ppermute | solution.py:100
  201.0 1.3 collective-permute-done.9
  202.3 5.3 %collective-permute-start.5 = (bf16[384,1536]{1,0:T(8,128)(2,1)S(1)}, bf16[384,1536]{1,0:T(8,128)(2,1)}, u32[]{:S(2)}, u32[]{:S(2)}) collective-permute-start(bf16[384,1536]{1,0:T(8,128)(2,1)S(1)} %copy-done.1), channel_id=1, source_target_pairs={{1,0},{2,1},{3,2},{4,3},{5,4},{6,5},{7,6},{9,8},{10,9},{11,10},{12... | collective-permute-start | bytes 3538952 | tf_op jit(solution)/shard_map/ppermute | solution.py:91
  207.6 2.1 pad_maximum_fusion.3
  209.7 1.9 collective-permute-start.3
  212.6 2.4 collective-permute-start.6
  215.8 11.4 %collective-permute-done.5.refs_10_ = bf16[384,1536]{1,0:T(8,128)(2,1)} collective-permute-done((bf16[384,1536]{1,0:T(8,128)(2,1)S(1)}, bf16[384,1536]{1,0:T(8,128)(2,1)}, u32[]{:S(2)}, u32[]{:S(2)}) %collective-permute-start.5) | collective-permute-done | bytes 1179680 | tf_op jit(solution)/shard_map/ppermute | solution.py:91
  227.2 1.9 collective-permute-start.13
  229.1 5.3 %collective-permute-start.14 = (bf16[384,1024]{1,0:T(8,128)(2,1)}, bf16[384,1024]{1,0:T(8,128)(2,1)}, u32[]{:S(2)}, u32[]{:S(2)}) collective-permute-start(bf16[384,1024]{1,0:T(8,128)(2,1)} %copy-done.5), channel_id=1, source_target_pairs={{1,0},{2,1},{3,2},{4,3},{5,4},{6,5},{7,6},{9,8},{10,9},{11,10},{12... | collective-permute-start | bytes 2359304 | tf_op jit(solution)/shard_map/ppermute | solution.py:91
  234.4 2.4 collective-permute-done.15.refs_3_.refs_4_
  236.8 13.3 %collective-permute-start.16 = (bf16[384,1024]{1,0:T(8,128)(2,1)}, bf16[384,1024]{1,0:T(8,128)(2,1)S(1)}, u32[]{:S(2)}, u32[]{:S(2)}) collective-permute-start(bf16[384,1024]{1,0:T(8,128)(2,1)} %collective-permute-done.15.refs_3_.refs_4_), channel_id=1, source_target_pairs={{0,1},{1,2},{2,3},{3,4},{4,5},{5,6},{6,7},{8,9},{9,10},{10,11},{11... | collective-permute-start | bytes 2359304 | tf_op jit(solution)/shard_map/ppermute | solution.py:91
  250.2 2.1 collective-permute-start.17
  252.4 3.1 %concatenate.16 = s32[6]{0:T(128)S(1)} concatenate(s32[1]{0:T(128)} %copy.11, s32[1]{0:T(128)} %collective-permute-done.7, s32[1]{0:T(128)} %collective-permute-done.8, s32[1]{0:T(128)} %collective-permute-done.9, s32[1]{0:T(128)} %collective-permute-done.10, s32[1]{0:T(128)} %collective-permute-done.11), dimensions={0} | concatenate | bytes 48 | tf_op jit(solution)/shard_map/concatenate | solution.py:112
  256.4 10.1 %shard_map.91 = bf16[384,512]{1,0:T(8,128)(2,1)} custom-call(bf16[384,1536]{1,0:T(8,128)(2,1)} %refs_0_.5, bf16[384,1536]{1,0:T(8,128)(2,1)} %refs_1_.5, bf16[384,1536]{1,0:T(8,128)(2,1)} %refs_2_.5, bf16[384,1024]{1,0:T(8,128)(2,1)} %collective-permute-done.refs_3_.refs_4_, bf16[384,1024]{1,0:T(8,128)(2,1)} %collective-permute-done.refs_3_.refs_4_, ...), custom_call_target="tpu_custom_call" | custom-call | tf_op jit(solution)/shard_map/pallas_call | solution.py:58
  266.5 10.1 %shard_map.92 = bf16[384,512]{1,0:T(8,128)(2,1)} custom-call(bf16[384,1536]{1,0:T(8,128)(2,1)} %refs_0_.5, bf16[384,1536]{1,0:T(8,128)(2,1)} %refs_1_.5, bf16[384,1536]{1,0:T(8,128)(2,1)} %refs_2_.5, bf16[384,1024]{1,0:T(8,128)(2,1)} %copy-done.5, bf16[384,1024]{1,0:T(8,128)(2,1)} %copy-done.5, bf16[384,1536]{1,0:T(8,128)(2,1)} %copy-done.2, ...), custom_call_target="tpu_custom_call" | custom-call | tf_op jit(solution)/shard_map/pallas_call | solution.py:58
  277.5 10.2 %shard_map.93 = bf16[384,512]{1,0:T(8,128)(2,1)} custom-call(bf16[384,1536]{1,0:T(8,128)(2,1)} %refs_0_.5, bf16[384,1536]{1,0:T(8,128)(2,1)} %refs_1_.5, bf16[384,1536]{1,0:T(8,128)(2,1)} %refs_2_.5, bf16[384,1024]{1,0:T(8,128)(2,1)} %collective-permute-done.15.refs_3_.refs_4_, bf16[384,1024]{1,0:T(8,128)(2,1)} %collective-permute-done.15.refs_3_.refs_4_, ...), custom_call_target="tpu_custom_call" | custom-call | tf_op jit(solution)/shard_map/pallas_call | solution.py:58
  289.9 4.5 %fusion.2 = f32[384,3072]{1,0:T(8,128)S(1)} fusion(bf16[384,768]{0,1:T(8,128)(2,1)S(1)} %bitcast.24, bf16[768,3072]{1,0:T(8,128)(2,1)} %collective-permute-done.18), kind=kOutput, calls=%fused_computation.26 | convolution fusion | flops 1811939328 | bytes 10027008 | tf_op jit(solution)/shard_map/dot_general | solution.py:150
  294.4 3.5 %multiply_convert_fusion = bf16[384,3072]{1,0:T(8,128)(2,1)} fusion(f32[384,3072]{1,0:T(8,128)S(1)} %fusion.2, bf16[384,768]{0,1:T(8,128)(2,1)S(1)} %bitcast.25, bf16[768,3072]{1,0:T(8,128)(2,1)S(1)} %bitcast.23, f32[3072]{0:T(1024)S(1)} %copy-done.10), kind=kOutput, calls=%fused_computation | convolution fusion | flops 1815478272 | bytes 12398592 | tf_op jit(solution)/shard_map/dot_general | solution.py:150
  (62 shorter events, 8.5 us)
Async XLA Ops:
  6.5 2.8 copy-start.1
  6.5 132.5 %all-gather.2.cloned.1.call-start = ((), (), s32[]{:S(2)}) async-start(), calls=%async_computation | async-start | bytes 5308416 | tf_op jit(solution)/shard_map/all_gather | solution.py:94
  10.2 129.3 %copy-start = (bf16[384,1536]{1,0:T(8,128)(2,1)S(1)}, bf16[384,1536]{1,0:T(8,128)(2,1)}, u32[]{:S(2)}) copy-start(bf16[384,1536]{1,0:T(8,128)(2,1)} %refs_1_.5) | copy-start | bytes 3538948
  10.3 56.2 %collective-permute-start = (bf16[384,1024]{1,0:T(8,128)(2,1)S(1)}, bf16[384,1024]{1,0:T(8,128)(2,1)}, u32[]{:S(2)}, u32[]{:S(2)}) collective-permute-start(bf16[384,1024]{1,0:T(8,128)(2,1)S(1)} %pad_maximum_fusion.1), channel_id=1, source_target_pairs={{0,8},{1,9},{2,10},{3,11},{4,12},{5,13},{6,14},{7,15},{8,0},{9,1},... | collective-permute-start | bytes 2359304 | tf_op jit(solution)/shard_map/ppermute | solution.py:124
  10.4 205.3 %copy-start.11 = (s32[12,2]{0,1:T(2,128)S(1)}, s32[12,2]{0,1:T(2,128)}, u32[]{:S(2)}) copy-start(s32[12,2]{0,1:T(2,128)} %param.13) | copy-start | bytes 292
  10.4 241.9 %copy-start.12 = (s32[6]{0:T(128)S(1)}, s32[6]{0:T(128)}, u32[]{:S(2)}) copy-start(s32[6]{0:T(128)} %constant.24.clone) | copy-start | bytes 76
  10.4 241.9 %copy-start.13 = (s32[6]{0:T(128)S(1)}, s32[6]{0:T(128)}, u32[]{:S(2)}) copy-start(s32[6]{0:T(128)} %constant.25.clone) | copy-start | bytes 76
  66.5 70.4 %collective-permute-start.12 = (bf16[384,1024]{1,0:T(8,128)(2,1)S(1)}, bf16[384,1024]{1,0:T(8,128)(2,1)S(1)}, u32[]{:S(2)}, u32[]{:S(2)}) collective-permute-start(bf16[384,1024]{1,0:T(8,128)(2,1)S(1)} %pad_maximum_fusion.2), channel_id=1, source_target_pairs={{0,8},{1,9},{2,10},{3,11},{4,12},{5,13},{6,14},{7,15},{8,0},{9,1},... | collective-permute-start | bytes 2359304 | tf_op jit(solution)/shard_map/ppermute | solution.py:124
  139.0 150.8 %collective-permute-start.18 = (bf16[768,3072]{1,0:T(8,128)(2,1)}, bf16[768,3072]{1,0:T(8,128)(2,1)}, u32[]{:S(2)}, u32[]{:S(2)}) collective-permute-start(bf16[768,3072]{1,0:T(8,128)(2,1)} %all-gather.2.cloned.1.call-done), channel_id=1, source_target_pairs={{0,1},{1,0},{2,3},{3,2},{4,5},{5,4},{6,7},{7,6},{8,9},{9,8},{10,11... | collective-permute-start | bytes 14155784 | tf_op jit(solution)/shard_map/ppermute | solution.py:129
  139.5 70.2 %collective-permute-start.1 = (bf16[384,1536]{1,0:T(8,128)(2,1)S(1)}, bf16[384,1536]{1,0:T(8,128)(2,1)S(1)}, u32[]{:S(2)}, u32[]{:S(2)}) collective-permute-start(bf16[384,1536]{1,0:T(8,128)(2,1)S(1)} %copy-done), channel_id=1, source_target_pairs={{0,1},{1,2},{2,3},{3,4},{4,5},{5,6},{6,7},{8,9},{9,10},{10,11},{11... | collective-permute-start | bytes 3538952 | tf_op jit(solution)/shard_map/ppermute | solution.py:91
  142.5 69.1 %collective-permute-start.2 = (bf16[384,1536]{1,0:T(8,128)(2,1)S(1)}, bf16[384,1536]{1,0:T(8,128)(2,1)S(1)}, u32[]{:S(2)}, u32[]{:S(2)}) collective-permute-start(bf16[384,1536]{1,0:T(8,128)(2,1)S(1)} %copy-done.1), channel_id=1, source_target_pairs={{0,1},{1,2},{2,3},{3,4},{4,5},{5,6},{6,7},{8,9},{9,10},{10,11},{11... | collective-permute-start | bytes 3538952 | tf_op jit(solution)/shard_map/ppermute | solution.py:91
  144.9 67.4 %collective-permute-start.4 = (bf16[384,1536]{1,0:T(8,128)(2,1)S(1)}, bf16[384,1536]{1,0:T(8,128)(2,1)S(1)}, u32[]{:S(2)}, u32[]{:S(2)}) collective-permute-start(bf16[384,1536]{1,0:T(8,128)(2,1)S(1)} %copy-done), channel_id=1, source_target_pairs={{1,0},{2,1},{3,2},{4,3},{5,4},{6,5},{7,6},{9,8},{10,9},{11,10},{12... | collective-permute-start | bytes 3538952 | tf_op jit(solution)/shard_map/ppermute | solution.py:91
  146.9 35.7 %collective-permute-start.10 = (s32[1]{0:T(128)}, s32[1]{0:T(128)}, u32[]{:S(2)}, u32[]{:S(2)}) collective-permute-start(s32[1]{0:T(128)} %param.12), channel_id=1, source_target_pairs={{1,0},{2,1},{3,2},{4,3},{5,4},{6,5},{7,6},{9,8},{10,9},{11,10},{12... | collective-permute-start | bytes 20 | tf_op jit(solution)/shard_map/ppermute | solution.py:100
  182.6 6.9 %collective-permute-start.11 = (s32[1]{0:T(128)}, s32[1]{0:T(128)}, u32[]{:S(2)}, u32[]{:S(2)}) collective-permute-start(s32[1]{0:T(128)} %param.12), channel_id=1, source_target_pairs={{1,8},{2,9},{3,10},{4,11},{5,12},{6,13},{7,14},{9,0},{10,1},{11,2}... | collective-permute-start | bytes 20 | tf_op jit(solution)/shard_map/ppermute | solution.py:100
  189.5 3.6 %collective-permute-start.7 = (s32[1]{0:T(128)}, s32[1]{0:T(128)}, u32[]{:S(2)}, u32[]{:S(2)}) collective-permute-start(s32[1]{0:T(128)} %param.12), channel_id=1, source_target_pairs={{0,8},{1,9},{2,10},{3,11},{4,12},{5,13},{6,14},{7,15},{8,0},{9,1},... | collective-permute-start | bytes 20 | tf_op jit(solution)/shard_map/ppermute | solution.py:100
  193.1 3.3 %collective-permute-start.8 = (s32[1]{0:T(128)}, s32[1]{0:T(128)}, u32[]{:S(2)}, u32[]{:S(2)}) collective-permute-start(s32[1]{0:T(128)} %param.12), channel_id=1, source_target_pairs={{0,1},{1,2},{2,3},{3,4},{4,5},{5,6},{6,7},{8,9},{9,10},{10,11},{11... | collective-permute-start | bytes 20 | tf_op jit(solution)/shard_map/ppermute | solution.py:100
  196.4 6.0 %collective-permute-start.9 = (s32[1]{0:T(128)}, s32[1]{0:T(128)}, u32[]{:S(2)}, u32[]{:S(2)}) collective-permute-start(s32[1]{0:T(128)} %param.12), channel_id=1, source_target_pairs={{0,9},{1,10},{2,11},{3,12},{4,13},{5,14},{6,15},{8,1},{9,2},{10,3}... | collective-permute-start | bytes 20 | tf_op jit(solution)/shard_map/ppermute | solution.py:100
  202.3 24.9 %collective-permute-start.5 = (bf16[384,1536]{1,0:T(8,128)(2,1)S(1)}, bf16[384,1536]{1,0:T(8,128)(2,1)}, u32[]{:S(2)}, u32[]{:S(2)}) collective-permute-start(bf16[384,1536]{1,0:T(8,128)(2,1)S(1)} %copy-done.1), channel_id=1, source_target_pairs={{1,0},{2,1},{3,2},{4,3},{5,4},{6,5},{7,6},{9,8},{10,9},{11,10},{12... | collective-permute-start | bytes 3538952 | tf_op jit(solution)/shard_map/ppermute | solution.py:91
  209.7 46.7 %copy-start.2 = (bf16[384,1536]{1,0:T(8,128)(2,1)}, bf16[384,1536]{1,0:T(8,128)(2,1)S(1)}, u32[]{:S(2)}) copy-start(bf16[384,1536]{1,0:T(8,128)(2,1)S(1)} %collective-permute-done.1.refs_5_) | copy-start | bytes 3538948
  209.7 19.4 %collective-permute-start.3 = (bf16[384,1024]{1,0:T(8,128)(2,1)}, bf16[384,1024]{1,0:T(8,128)(2,1)}, u32[]{:S(2)}, u32[]{:S(2)}) collective-permute-start(bf16[384,1024]{1,0:T(8,128)(2,1)} %collective-permute-done.refs_3_.refs_4_), channel_id=1, source_target_pairs={{0,1},{1,2},{2,3},{3,4},{4,5},{5,6},{6,7},{8,9},{9,10},{10,11},{11... | collective-permute-start | bytes 2359304 | tf_op jit(solution)/shard_map/ppermute | solution.py:91
  211.6 25.2 %collective-permute-start.15 = (bf16[384,1024]{1,0:T(8,128)(2,1)}, bf16[384,1024]{1,0:T(8,128)(2,1)}, u32[]{:S(2)}, u32[]{:S(2)}) collective-permute-start(bf16[384,1024]{1,0:T(8,128)(2,1)} %pad_maximum_fusion.3), channel_id=1, source_target_pairs={{0,8},{1,9},{2,10},{3,11},{4,12},{5,13},{6,14},{7,15},{8,0},{9,1},... | collective-permute-start | bytes 2359304 | tf_op jit(solution)/shard_map/ppermute | solution.py:124
  212.6 37.5 %collective-permute-start.6 = (bf16[384,1024]{1,0:T(8,128)(2,1)}, bf16[384,1024]{1,0:T(8,128)(2,1)S(1)}, u32[]{:S(2)}, u32[]{:S(2)}) collective-permute-start(bf16[384,1024]{1,0:T(8,128)(2,1)} %collective-permute-done.refs_3_.refs_4_), channel_id=1, source_target_pairs={{1,0},{2,1},{3,2},{4,3},{5,4},{6,5},{7,6},{9,8},{10,9},{11,10},{12... | collective-permute-start | bytes 2359304 | tf_op jit(solution)/shard_map/ppermute | solution.py:91
  227.2 39.3 %collective-permute-start.13 = (bf16[384,1024]{1,0:T(8,128)(2,1)}, bf16[384,1024]{1,0:T(8,128)(2,1)}, u32[]{:S(2)}, u32[]{:S(2)}) collective-permute-start(bf16[384,1024]{1,0:T(8,128)(2,1)} %copy-done.5), channel_id=1, source_target_pairs={{0,1},{1,2},{2,3},{3,4},{4,5},{5,6},{6,7},{8,9},{9,10},{10,11},{11... | collective-permute-start | bytes 2359304 | tf_op jit(solution)/shard_map/ppermute | solution.py:91
  229.1 37.4 %collective-permute-start.14 = (bf16[384,1024]{1,0:T(8,128)(2,1)}, bf16[384,1024]{1,0:T(8,128)(2,1)}, u32[]{:S(2)}, u32[]{:S(2)}) collective-permute-start(bf16[384,1024]{1,0:T(8,128)(2,1)} %copy-done.5), channel_id=1, source_target_pairs={{1,0},{2,1},{3,2},{4,3},{5,4},{6,5},{7,6},{9,8},{10,9},{11,10},{12... | collective-permute-start | bytes 2359304 | tf_op jit(solution)/shard_map/ppermute | solution.py:91
  236.8 39.8 %collective-permute-start.16 = (bf16[384,1024]{1,0:T(8,128)(2,1)}, bf16[384,1024]{1,0:T(8,128)(2,1)S(1)}, u32[]{:S(2)}, u32[]{:S(2)}) collective-permute-start(bf16[384,1024]{1,0:T(8,128)(2,1)} %collective-permute-done.15.refs_3_.refs_4_), channel_id=1, source_target_pairs={{0,1},{1,2},{2,3},{3,4},{4,5},{5,6},{6,7},{8,9},{9,10},{10,11},{11... | collective-permute-start | bytes 2359304 | tf_op jit(solution)/shard_map/ppermute | solution.py:91
  250.2 6.2 %copy-start.6 = (bf16[384,1024]{1,0:T(8,128)(2,1)}, bf16[384,1024]{1,0:T(8,128)(2,1)S(1)}, u32[]{:S(2)}) copy-start(bf16[384,1024]{1,0:T(8,128)(2,1)S(1)} %collective-permute-done.6.refs_11_.refs_12_) | copy-start | bytes 2359300
  250.2 26.4 %collective-permute-start.17 = (bf16[384,1024]{1,0:T(8,128)(2,1)}, bf16[384,1024]{1,0:T(8,128)(2,1)}, u32[]{:S(2)}, u32[]{:S(2)}) collective-permute-start(bf16[384,1024]{1,0:T(8,128)(2,1)} %collective-permute-done.15.refs_3_.refs_4_), channel_id=1, source_target_pairs={{1,0},{2,1},{3,2},{4,3},{5,4},{6,5},{7,6},{9,8},{10,9},{11,10},{12... | collective-permute-start | bytes 2359304 | tf_op jit(solution)/shard_map/ppermute | solution.py:91
  277.5 10.2 %copy-start.8 = (bf16[384,512]{1,0:T(8,128)(2,1)S(1)}, bf16[384,512]{1,0:T(8,128)(2,1)}, u32[]{:S(2)}) copy-start(bf16[384,512]{1,0:T(8,128)(2,1)} %shard_map.91) | copy-start | bytes 1179652
  277.5 10.2 %copy-start.9 = (bf16[384,512]{1,0:T(8,128)(2,1)S(1)}, bf16[384,512]{1,0:T(8,128)(2,1)}, u32[]{:S(2)}) copy-start(bf16[384,512]{1,0:T(8,128)(2,1)} %shard_map.92) | copy-start | bytes 1179652
  289.8 4.6 %slice-start = ((s8[4718592]{0:T(1024)(128)(4,1)}), s8[4194304]{0:T(1024)(128)(4,1)S(1)}, s32[]{:S(2)}) async-start(s8[4718592]{0:T(1024)(128)(4,1)} %bitcast.22), calls=%async_computation.1 | async-start | bytes 8388608
  289.9 4.6 %slice-start.1 = ((s8[4718592]{0:T(1024)(128)(4,1)}), s8[524288]{0:T(1024)(128)(4,1)S(1)}, s32[]{:S(2)}) async-start(s8[4718592]{0:T(1024)(128)(4,1)} %bitcast.22), calls=%async_computation.2 | async-start | bytes 1048576
  289.9 4.6 %copy-start.10 = (f32[3072]{0:T(1024)S(1)}, f32[3072]{0:T(1024)}, u32[]{:S(2)}) copy-start(f32[3072]{0:T(1024)} %param.15) | copy-start | bytes 36868
  (4 other events, 6.4 us)
Sparse Core Ops, SparseCore 0:
  9.5 129.4 all-gather.1

commit v7 on v5

--- a/solution.py
+++ b/solution.py
@@ -8,7 +8,7 @@
 
 
 TW = 8
-GROUPS = 2
+GROUPS = 3
 
 
 def group_attention(queries, slots, usable, head_base, group_heads, head_dim, score_scale):
@@ -133,10 +133,14 @@
         window = (far_rows[None, :] <= reach[:, 0:1]) & (far_cols[None, :] <= reach[:, 1:2])
         usable = key_real[None, :, :] & window[:, :, None]
         attended = group_attention(queries, slots, usable, base, group_heads, head_dim, score_scale)
-        outputs.append(jnp.where(query_real[:, None], attended, 0))
+        attended = jnp.where(query_real[:, None], attended, 0)
+        rows_g = lax.slice_in_dim(weight_all, g * group_width, (g + 1) * group_width, axis=0)
+        part = jnp.dot(attended, rows_g, preferred_element_type=jnp.float32)
+        outputs.append(part)
 
-    attended_all = jnp.concatenate(outputs, axis=1)
-    projected = jnp.dot(attended_all, weight_all, preferred_element_type=jnp.float32)
+    projected = outputs[0]
+    for part in outputs[1:]:
+        projected = projected + part
     return (projected * gate[None, :]).astype(jnp.bfloat16)
 
 

time: 291 us -> 262 us (0.900)
  waiting for transfers between devices: 184 us -> 149 us
    ppermute x2 -> x3, waiting for transfers between devices: 94.1 us -> 137 us  [on_device(): got = [lax.ppermute(own, 'seq', pairs) for pairs in verticals]]
    ppermute x5, waiting for transfers between devices: 53.9 us -> 11.5 us  [on_device(): fetch = lambda pairs: lax.ppermute(tile_lengths, 'seq', pairs)]
    ppermute x4 -> x5, waiting for transfers between devices: 34.8 us -> 0.01 us  [on_device(): lax.ppermute(x, 'seq', to_left)]
    ppermute x4 -> x5, starting transfers between devices: 10.7 us -> 14.8 us  [on_device(): lax.ppermute(x, 'seq', to_right)]
    ppermute x5, starting transfers between devices: 18.1 us -> 14.2 us  [on_device(): fetch = lambda pairs: lax.ppermute(tile_lengths, 'seq', pairs)]
    dot_general x1 -> x3, matrix products: 8.82 us -> 11.6 us  [on_device(): part = jnp.dot(attended, rows_g, preferred_element_type=jnp.float32)]
    pallas_call x2 -> x3, Pallas kernels: 28.3 us -> 30.4 us  [group_attention(): pl.pallas_call(kernel, grid=(group_heads,), in_specs=in_specs, out_specs=...]
    ppermute x4 -> x5, starting transfers between devices: 14 us -> 13.9 us  [on_device(): lax.ppermute(x, 'seq', to_left)]
  transfers between devices with their start and end apart: 16 -> 19, of which waited for: 8 -> 8; matrix products, arithmetic and copies ran while one was open for 2% -> 2% of each run, Pallas kernels for 10% -> 12%
where the time goes in v7:
time: 262 us; the launch traced here: 259 us
  waiting for transfers between devices  149 us (57%)
  starting transfers between devices  45 us (17%)
  Pallas kernels  30.4 us (12%)
  between operations  14.5 us (6%)
  matrix products  11.6 us (4%)
  local copies, waits for them, and re-layouts  6.57 us (3%)
    ppermute x3, waiting for transfers between devices, on_device(): got = [lax.ppermute(own, 'seq', pairs) for pairs in verticals]  137 us
    pallas_call x3, Pallas kernels, group_attention(): pl.pallas_call(kernel, grid=(group_heads,), in_specs=in_specs, out_specs=...  30.4 us
    ppermute x5, starting transfers between devices, on_device(): lax.ppermute(x, 'seq', to_right)  14.8 us
    ppermute x5, starting transfers between devices, on_device(): fetch = lambda pairs: lax.ppermute(tile_lengths, 'seq', pairs)  14.2 us
    ppermute x5, starting transfers between devices, on_device(): lax.ppermute(x, 'seq', to_left)  13.9 us
    dot_general x3, matrix products, on_device(): part = jnp.dot(attended, rows_g, preferred_element_type=jnp.float32)  11.6 us
    ppermute x5, waiting for transfers between devices, on_device(): fetch = lambda pairs: lax.ppermute(tile_lengths, 'seq', pairs)  11.5 us
  transfers between devices with their start and end apart: 19, of which 8 were waited for; matrix products, arithmetic and copies ran while one was open for 2% of the time, Pallas kernels for 12%

profile of v7, /device:TPU:27, one launch (start us, length us, event | category | flops | bytes accessed | tf_op | source)
XLA Modules:
  0.0 258.7 jit_solution(700422214277575263)
XLA Ops:
  7.3 1.4 fusion.20
  9.1 2.9 %collective-permute-start.4 = (bf16[384,1536]{1,0:T(8,128)(2,1)S(1)}, bf16[384,1536]{1,0:T(8,128)(2,1)S(1)}, u32[]{:S(2)}, u32[]{:S(2)}) collective-permute-start(bf16[384,1536]{1,0:T(8,128)(2,1)S(1)} %copy-done), channel_id=1, source_target_pairs={{1,0},{2,1},{3,2},{4,3},{5,4},{6,5},{7,6},{9,8},{10,9},{11,10},{12... | collective-permute-start | bytes 3538952 | tf_op jit(solution)/shard_map/ppermute | solution.py:91
  12.1 53.0 %collective-permute-done.refs_3_.refs_4_ = bf16[384,1024]{1,0:T(8,128)(2,1)S(1)} collective-permute-done((bf16[384,1024]{1,0:T(8,128)(2,1)S(1)}, bf16[384,1024]{1,0:T(8,128)(2,1)S(1)}, u32[]{:S(2)}, u32[]{:S(2)}) %collective-permute-start) | collective-permute-done | bytes 786464 | tf_op jit(solution)/shard_map/ppermute | solution.py:121
  65.1 3.5 %collective-permute-start.1 = (bf16[384,1536]{1,0:T(8,128)(2,1)S(1)}, bf16[384,1536]{1,0:T(8,128)(2,1)S(1)}, u32[]{:S(2)}, u32[]{:S(2)}) collective-permute-start(bf16[384,1536]{1,0:T(8,128)(2,1)S(1)} %copy-done), channel_id=1, source_target_pairs={{0,1},{1,2},{2,3},{3,4},{4,5},{5,6},{6,7},{8,9},{9,10},{10,11},{11... | collective-permute-start | bytes 3538952 | tf_op jit(solution)/shard_map/ppermute | solution.py:91
  68.6 1.9 collective-permute-start.5
  70.6 3.6 %collective-permute-start.2 = (bf16[384,1536]{1,0:T(8,128)(2,1)S(1)}, bf16[384,1536]{1,0:T(8,128)(2,1)S(1)}, u32[]{:S(2)}, u32[]{:S(2)}) collective-permute-start(bf16[384,1536]{1,0:T(8,128)(2,1)S(1)} %copy-done.1), channel_id=1, source_target_pairs={{0,1},{1,2},{2,3},{3,4},{4,5},{5,6},{6,7},{8,9},{9,10},{10,11},{11... | collective-permute-start | bytes 3538952 | tf_op jit(solution)/shard_map/ppermute | solution.py:91
  74.3 61.0 %collective-permute-done.12.refs_3_.refs_4_ = bf16[384,1024]{1,0:T(8,128)(2,1)} collective-permute-done((bf16[384,1024]{1,0:T(8,128)(2,1)S(1)}, bf16[384,1024]{1,0:T(8,128)(2,1)}, u32[]{:S(2)}, u32[]{:S(2)}) %collective-permute-start.12) | collective-permute-done | bytes 786464 | tf_op jit(solution)/shard_map/ppermute | solution.py:121
  135.4 2.7 %collective-permute-start.10 = (s32[1]{0:T(128)}, s32[1]{0:T(128)}, u32[]{:S(2)}, u32[]{:S(2)}) collective-permute-start(s32[1]{0:T(128)} %param.12), channel_id=1, source_target_pairs={{1,0},{2,1},{3,2},{4,3},{5,4},{6,5},{7,6},{9,8},{10,9},{11,10},{12... | collective-permute-start | bytes 20 | tf_op jit(solution)/shard_map/ppermute | solution.py:97
  138.0 2.8 %collective-permute-done.10 = s32[1]{0:T(128)} collective-permute-done((s32[1]{0:T(128)}, s32[1]{0:T(128)}, u32[]{:S(2)}, u32[]{:S(2)}) %collective-permute-start.10) | collective-permute-done | bytes 36 | tf_op jit(solution)/shard_map/ppermute | solution.py:97
  140.8 1.9 collective-permute-start.9
  142.7 4.1 %collective-permute-done.9 = s32[1]{0:T(128)} collective-permute-done((s32[1]{0:T(128)}, s32[1]{0:T(128)}, u32[]{:S(2)}, u32[]{:S(2)}) %collective-permute-start.9) | collective-permute-done | bytes 36 | tf_op jit(solution)/shard_map/ppermute | solution.py:97
  146.8 2.3 collective-permute-start.8
  149.2 0.9 collective-permute-done.8
  150.6 2.9 %collective-permute-done.7 = s32[1]{0:T(128)} collective-permute-done((s32[1]{0:T(128)}, s32[1]{0:T(128)}, u32[]{:S(2)}, u32[]{:S(2)}) %collective-permute-start.7) | collective-permute-done | bytes 36 | tf_op jit(solution)/shard_map/ppermute | solution.py:97
  153.5 6.7 %collective-permute-start.11 = (s32[1]{0:T(128)}, s32[1]{0:T(128)}, u32[]{:S(2)}, u32[]{:S(2)}) collective-permute-start(s32[1]{0:T(128)} %param.12), channel_id=1, source_target_pairs={{1,8},{2,9},{3,10},{4,11},{5,12},{6,13},{7,14},{9,0},{10,1},{11,2}... | collective-permute-start | bytes 20 | tf_op jit(solution)/shard_map/ppermute | solution.py:97
  161.0 1.9 collective-permute-start.15
  163.0 3.6 %collective-permute-start.6 = (bf16[384,1024]{1,0:T(8,128)(2,1)S(1)}, bf16[384,1024]{1,0:T(8,128)(2,1)S(1)}, u32[]{:S(2)}, u32[]{:S(2)}) collective-permute-start(bf16[384,1024]{1,0:T(8,128)(2,1)S(1)} %collective-permute-done.refs_3_.refs_4_), channel_id=1, source_target_pairs={{1,0},{2,1},{3,2},{4,3},{5,4},{6,5},{7,6},{9,8},{10,9},{11,10},{12... | collective-permute-start | bytes 2359304 | tf_op jit(solution)/shard_map/ppermute | solution.py:91
  167.3 1.9 collective-permute-start.3
  169.3 3.1 %collective-permute-start.14 = (bf16[384,1024]{1,0:T(8,128)(2,1)}, bf16[384,1024]{1,0:T(8,128)(2,1)}, u32[]{:S(2)}, u32[]{:S(2)}) collective-permute-start(bf16[384,1024]{1,0:T(8,128)(2,1)} %collective-permute-done.12.refs_3_.refs_4_), channel_id=1, source_target_pairs={{1,0},{2,1},{3,2},{4,3},{5,4},{6,5},{7,6},{9,8},{10,9},{11,10},{12... | collective-permute-start | bytes 2359304 | tf_op jit(solution)/shard_map/ppermute | solution.py:91
  172.5 2.4 collective-permute-start.13
  174.9 23.1 %collective-permute-done.15.refs_3_.refs_4_ = bf16[384,1024]{1,0:T(8,128)(2,1)} collective-permute-done((bf16[384,1024]{1,0:T(8,128)(2,1)S(1)}, bf16[384,1024]{1,0:T(8,128)(2,1)}, u32[]{:S(2)}, u32[]{:S(2)}) %collective-permute-start.15) | collective-permute-done | bytes 786464 | tf_op jit(solution)/shard_map/ppermute | solution.py:121
  198.1 2.4 collective-permute-start.17
  200.5 0.9 copy-done.7
  201.4 3.3 %collective-permute-start.16 = (bf16[384,1024]{1,0:T(8,128)(2,1)}, bf16[384,1024]{1,0:T(8,128)(2,1)}, u32[]{:S(2)}, u32[]{:S(2)}) collective-permute-start(bf16[384,1024]{1,0:T(8,128)(2,1)} %collective-permute-done.15.refs_3_.refs_4_), channel_id=1, source_target_pairs={{0,1},{1,2},{2,3},{3,4},{4,5},{5,6},{6,7},{8,9},{9,10},{10,11},{11... | collective-permute-start | bytes 2359304 | tf_op jit(solution)/shard_map/ppermute | solution.py:91
  204.8 3.1 %concatenate.13 = s32[6]{0:T(128)S(1)} concatenate(s32[1]{0:T(128)} %copy.10, s32[1]{0:T(128)} %collective-permute-done.7, s32[1]{0:T(128)} %collective-permute-done.8, s32[1]{0:T(128)} %collective-permute-done.9, s32[1]{0:T(128)} %collective-permute-done.10, s32[1]{0:T(128)} %collective-permute-done.11), dimensions={0} | concatenate | bytes 48 | tf_op jit(solution)/shard_map/concatenate | solution.py:109
  208.8 10.1 %shard_map.91 = bf16[384,512]{1,0:T(8,128)(2,1)} custom-call(bf16[384,1536]{1,0:T(8,128)(2,1)} %refs_0_.5, bf16[384,1536]{1,0:T(8,128)(2,1)} %refs_1_.5, bf16[384,1536]{1,0:T(8,128)(2,1)} %refs_2_.5, bf16[384,1024]{1,0:T(8,128)(2,1)} %copy-done.6, bf16[384,1024]{1,0:T(8,128)(2,1)} %copy-done.6, bf16[384,1536]{1,0:T(8,128)(2,1)} %copy-done.3, ...), custom_call_target="tpu_custom_call" | custom-call | tf_op jit(solution)/shard_map/pallas_call | solution.py:58
  218.9 10.1 %shard_map.92 = bf16[384,512]{1,0:T(8,128)(2,1)} custom-call(bf16[384,1536]{1,0:T(8,128)(2,1)} %refs_0_.5, bf16[384,1536]{1,0:T(8,128)(2,1)} %refs_1_.5, bf16[384,1536]{1,0:T(8,128)(2,1)} %refs_2_.5, bf16[384,1024]{1,0:T(8,128)(2,1)} %collective-permute-done.12.refs_3_.refs_4_, bf16[384,1024]{1,0:T(8,128)(2,1)} %collective-permute-done.12.refs_3_.refs_4_, ...), custom_call_target="tpu_custom_call" | custom-call | tf_op jit(solution)/shard_map/pallas_call | solution.py:58
  229.0 0.9 copy-done.8
  229.9 10.2 %shard_map.93 = bf16[384,512]{1,0:T(8,128)(2,1)} custom-call(bf16[384,1536]{1,0:T(8,128)(2,1)} %refs_0_.5, bf16[384,1536]{1,0:T(8,128)(2,1)} %refs_1_.5, bf16[384,1536]{1,0:T(8,128)(2,1)} %refs_2_.5, bf16[384,1024]{1,0:T(8,128)(2,1)} %collective-permute-done.15.refs_3_.refs_4_, bf16[384,1024]{1,0:T(8,128)(2,1)} %collective-permute-done.15.refs_3_.refs_4_, ...), custom_call_target="tpu_custom_call" | custom-call | tf_op jit(solution)/shard_map/pallas_call | solution.py:58
  240.2 3.4 %fusion.6 = f32[384,3072]{1,0:T(8,128)S(1)} fusion(bf16[1536,3072]{1,0:T(8,128)(2,1)} %all-gather.2.cloned.1.call-done, bf16[384,512]{1,0:T(8,128)(2,1)S(1)} %copy-done.9, pred[384]{0:T(512)(128)(4,1)S(1)} %iota_compare_fusion.1), kind=kOutput, calls=%fused_computation.5 | convolution fusion | flops 1208156160 | bytes 8257920 | tf_op jit(solution)/shard_map/dot_general | solution.py:138
  243.6 3.4 %fusion.4 = f32[384,3072]{1,0:T(8,128)S(1)} fusion(bf16[1536,3072]{1,0:T(8,128)(2,1)} %all-gather.2.cloned.1.call-done, bf16[384,512]{1,0:T(8,128)(2,1)S(1)} %copy-done.10, pred[384]{0:T(512)(128)(4,1)S(1)} %iota_compare_fusion.1), kind=kOutput, calls=%fused_computation.3 | convolution fusion | flops 1208156160 | bytes 8257920 | tf_op jit(solution)/shard_map/dot_general | solution.py:138
  247.0 4.9 %multiply_convert_fusion = bf16[384,3072]{1,0:T(8,128)(2,1)} fusion(f32[384,3072]{1,0:T(8,128)S(1)} %fusion.6, f32[384,3072]{1,0:T(8,128)S(1)} %fusion.4, bf16[1536,3072]{1,0:T(8,128)(2,1)} %all-gather.2.cloned.1.call-done, f32[3072]{0:T(1024)S(1)} %copy-done.12, bf16[384,512]{1,0:T(8,128)(2,1)S(1)} %copy-done.11, pred[384]{0:T(512)(128)(4,1)S(1)} %iota_compare_fusion.1), kind=kOutput, calls=%fused_computation | convolution fusion | flops 1212874752 | bytes 15348096 | tf_op jit(solution)/shard_map/dot_general | solution.py:138
  (56 shorter events, 3.7 us)
Async XLA Ops:
  6.5 2.2 copy-start.1
  6.5 233.6 %all-gather.2.cloned.1.call-start = ((), (), s32[]{:S(2)}) async-start(), calls=%async_computation | async-start | bytes 10027008 | tf_op jit(solution)/shard_map/all_gather | solution.py:93
  8.7 158.5 %copy-start.13 = (s32[12,2]{0,1:T(2,128)S(1)}, s32[12,2]{0,1:T(2,128)}, u32[]{:S(2)}) copy-start(s32[12,2]{0,1:T(2,128)} %param.13) | copy-start | bytes 292
  8.7 196.0 %copy-start.14 = (s32[6]{0:T(128)S(1)}, s32[6]{0:T(128)}, u32[]{:S(2)}) copy-start(s32[6]{0:T(128)} %constant.8.clone) | copy-start | bytes 76
  8.7 196.0 %copy-start.15 = (s32[6]{0:T(128)S(1)}, s32[6]{0:T(128)}, u32[]{:S(2)}) copy-start(s32[6]{0:T(128)} %constant.7.clone) | copy-start | bytes 76
  9.0 56.1 %collective-permute-start = (bf16[384,1024]{1,0:T(8,128)(2,1)S(1)}, bf16[384,1024]{1,0:T(8,128)(2,1)S(1)}, u32[]{:S(2)}, u32[]{:S(2)}) collective-permute-start(bf16[384,1024]{1,0:T(8,128)(2,1)S(1)} %pad_maximum_fusion), channel_id=1, source_target_pairs={{0,8},{1,9},{2,10},{3,11},{4,12},{5,13},{6,14},{7,15},{8,0},{9,1},... | collective-permute-start | bytes 2359304 | tf_op jit(solution)/shard_map/ppermute | solution.py:121
  9.1 153.9 %collective-permute-start.4 = (bf16[384,1536]{1,0:T(8,128)(2,1)S(1)}, bf16[384,1536]{1,0:T(8,128)(2,1)S(1)}, u32[]{:S(2)}, u32[]{:S(2)}) collective-permute-start(bf16[384,1536]{1,0:T(8,128)(2,1)S(1)} %copy-done), channel_id=1, source_target_pairs={{1,0},{2,1},{3,2},{4,3},{5,4},{6,5},{7,6},{9,8},{10,9},{11,10},{12... | collective-permute-start | bytes 3538952 | tf_op jit(solution)/shard_map/ppermute | solution.py:91
  65.1 143.7 %copy-start.6 = (bf16[384,1024]{1,0:T(8,128)(2,1)}, bf16[384,1024]{1,0:T(8,128)(2,1)S(1)}, u32[]{:S(2)}) copy-start(bf16[384,1024]{1,0:T(8,128)(2,1)S(1)} %collective-permute-done.refs_3_.refs_4_) | copy-start | bytes 2359300
  65.1 70.2 %collective-permute-start.12 = (bf16[384,1024]{1,0:T(8,128)(2,1)S(1)}, bf16[384,1024]{1,0:T(8,128)(2,1)}, u32[]{:S(2)}, u32[]{:S(2)}) collective-permute-start(bf16[384,1024]{1,0:T(8,128)(2,1)S(1)} %pad_maximum_fusion.1), channel_id=1, source_target_pairs={{0,8},{1,9},{2,10},{3,11},{4,12},{5,13},{6,14},{7,15},{8,0},{9,1},... | collective-permute-start | bytes 2359304 | tf_op jit(solution)/shard_map/ppermute | solution.py:121
  65.1 102.2 %collective-permute-start.1 = (bf16[384,1536]{1,0:T(8,128)(2,1)S(1)}, bf16[384,1536]{1,0:T(8,128)(2,1)S(1)}, u32[]{:S(2)}, u32[]{:S(2)}) collective-permute-start(bf16[384,1536]{1,0:T(8,128)(2,1)S(1)} %copy-done), channel_id=1, source_target_pairs={{0,1},{1,2},{2,3},{3,4},{4,5},{5,6},{6,7},{8,9},{9,10},{10,11},{11... | collective-permute-start | bytes 3538952 | tf_op jit(solution)/shard_map/ppermute | solution.py:91
  68.6 100.6 %collective-permute-start.5 = (bf16[384,1536]{1,0:T(8,128)(2,1)S(1)}, bf16[384,1536]{1,0:T(8,128)(2,1)S(1)}, u32[]{:S(2)}, u32[]{:S(2)}) collective-permute-start(bf16[384,1536]{1,0:T(8,128)(2,1)S(1)} %copy-done.1), channel_id=1, source_target_pairs={{1,0},{2,1},{3,2},{4,3},{5,4},{6,5},{7,6},{9,8},{10,9},{11,10},{12... | collective-permute-start | bytes 3538952 | tf_op jit(solution)/shard_map/ppermute | solution.py:91
  70.6 101.9 %collective-permute-start.2 = (bf16[384,1536]{1,0:T(8,128)(2,1)S(1)}, bf16[384,1536]{1,0:T(8,128)(2,1)S(1)}, u32[]{:S(2)}, u32[]{:S(2)}) collective-permute-start(bf16[384,1536]{1,0:T(8,128)(2,1)S(1)} %copy-done.1), channel_id=1, source_target_pairs={{0,1},{1,2},{2,3},{3,4},{4,5},{5,6},{6,7},{8,9},{9,10},{10,11},{11... | collective-permute-start | bytes 3538952 | tf_op jit(solution)/shard_map/ppermute | solution.py:91
  135.4 5.4 %collective-permute-start.10 = (s32[1]{0:T(128)}, s32[1]{0:T(128)}, u32[]{:S(2)}, u32[]{:S(2)}) collective-permute-start(s32[1]{0:T(128)} %param.12), channel_id=1, source_target_pairs={{1,0},{2,1},{3,2},{4,3},{5,4},{6,5},{7,6},{9,8},{10,9},{11,10},{12... | collective-permute-start | bytes 20 | tf_op jit(solution)/shard_map/ppermute | solution.py:97
  140.8 6.0 %collective-permute-start.9 = (s32[1]{0:T(128)}, s32[1]{0:T(128)}, u32[]{:S(2)}, u32[]{:S(2)}) collective-permute-start(s32[1]{0:T(128)} %param.12), channel_id=1, source_target_pairs={{0,9},{1,10},{2,11},{3,12},{4,13},{5,14},{6,15},{8,1},{9,2},{10,3}... | collective-permute-start | bytes 20 | tf_op jit(solution)/shard_map/ppermute | solution.py:97
  146.8 3.2 %collective-permute-start.8 = (s32[1]{0:T(128)}, s32[1]{0:T(128)}, u32[]{:S(2)}, u32[]{:S(2)}) collective-permute-start(s32[1]{0:T(128)} %param.12), channel_id=1, source_target_pairs={{0,1},{1,2},{2,3},{3,4},{4,5},{5,6},{6,7},{8,9},{9,10},{10,11},{11... | collective-permute-start | bytes 20 | tf_op jit(solution)/shard_map/ppermute | solution.py:97
  150.1 3.4 %collective-permute-start.7 = (s32[1]{0:T(128)}, s32[1]{0:T(128)}, u32[]{:S(2)}, u32[]{:S(2)}) collective-permute-start(s32[1]{0:T(128)} %param.12), channel_id=1, source_target_pairs={{0,8},{1,9},{2,10},{3,11},{4,12},{5,13},{6,14},{7,15},{8,0},{9,1},... | collective-permute-start | bytes 20 | tf_op jit(solution)/shard_map/ppermute | solution.py:97
  153.5 7.6 %collective-permute-start.11 = (s32[1]{0:T(128)}, s32[1]{0:T(128)}, u32[]{:S(2)}, u32[]{:S(2)}) collective-permute-start(s32[1]{0:T(128)} %param.12), channel_id=1, source_target_pairs={{1,8},{2,9},{3,10},{4,11},{5,12},{6,13},{7,14},{9,0},{10,1},{11,2}... | collective-permute-start | bytes 20 | tf_op jit(solution)/shard_map/ppermute | solution.py:97
  161.0 37.0 %collective-permute-start.15 = (bf16[384,1024]{1,0:T(8,128)(2,1)S(1)}, bf16[384,1024]{1,0:T(8,128)(2,1)}, u32[]{:S(2)}, u32[]{:S(2)}) collective-permute-start(bf16[384,1024]{1,0:T(8,128)(2,1)S(1)} %pad_maximum_fusion.2), channel_id=1, source_target_pairs={{0,8},{1,9},{2,10},{3,11},{4,12},{5,13},{6,14},{7,15},{8,0},{9,1},... | collective-permute-start | bytes 2359304 | tf_op jit(solution)/shard_map/ppermute | solution.py:121
  163.0 45.8 %copy-start.2 = (bf16[384,1536]{1,0:T(8,128)(2,1)}, bf16[384,1536]{1,0:T(8,128)(2,1)S(1)}, u32[]{:S(2)}) copy-start(bf16[384,1536]{1,0:T(8,128)(2,1)S(1)} %collective-permute-done.4.refs_9_) | copy-start | bytes 3538948
  163.0 37.5 %collective-permute-start.6 = (bf16[384,1024]{1,0:T(8,128)(2,1)S(1)}, bf16[384,1024]{1,0:T(8,128)(2,1)S(1)}, u32[]{:S(2)}, u32[]{:S(2)}) collective-permute-start(bf16[384,1024]{1,0:T(8,128)(2,1)S(1)} %collective-permute-done.refs_3_.refs_4_), channel_id=1, source_target_pairs={{1,0},{2,1},{3,2},{4,3},{5,4},{6,5},{7,6},{9,8},{10,9},{11,10},{12... | collective-permute-start | bytes 2359304 | tf_op jit(solution)/shard_map/ppermute | solution.py:91
  167.3 5.1 %copy-start.3 = (bf16[384,1536]{1,0:T(8,128)(2,1)}, bf16[384,1536]{1,0:T(8,128)(2,1)S(1)}, u32[]{:S(2)}) copy-start(bf16[384,1536]{1,0:T(8,128)(2,1)S(1)} %collective-permute-done.1.refs_5_) | copy-start | bytes 3538948
  167.3 41.4 %collective-permute-start.3 = (bf16[384,1024]{1,0:T(8,128)(2,1)S(1)}, bf16[384,1024]{1,0:T(8,128)(2,1)}, u32[]{:S(2)}, u32[]{:S(2)}) collective-permute-start(bf16[384,1024]{1,0:T(8,128)(2,1)S(1)} %collective-permute-done.refs_3_.refs_4_), channel_id=1, source_target_pairs={{0,1},{1,2},{2,3},{3,4},{4,5},{5,6},{6,7},{8,9},{9,10},{10,11},{11... | collective-permute-start | bytes 2359304 | tf_op jit(solution)/shard_map/ppermute | solution.py:91
  169.3 5.6 %copy-start.4 = (bf16[384,1536]{1,0:T(8,128)(2,1)}, bf16[384,1536]{1,0:T(8,128)(2,1)S(1)}, u32[]{:S(2)}) copy-start(bf16[384,1536]{1,0:T(8,128)(2,1)S(1)} %collective-permute-done.5.refs_10_) | copy-start | bytes 3538948
  169.3 49.6 %collective-permute-start.14 = (bf16[384,1024]{1,0:T(8,128)(2,1)}, bf16[384,1024]{1,0:T(8,128)(2,1)}, u32[]{:S(2)}, u32[]{:S(2)}) collective-permute-start(bf16[384,1024]{1,0:T(8,128)(2,1)} %collective-permute-done.12.refs_3_.refs_4_), channel_id=1, source_target_pairs={{1,0},{2,1},{3,2},{4,3},{5,4},{6,5},{7,6},{9,8},{10,9},{11,10},{12... | collective-permute-start | bytes 2359304 | tf_op jit(solution)/shard_map/ppermute | solution.py:91
  172.5 25.6 %copy-start.5 = (bf16[384,1536]{1,0:T(8,128)(2,1)}, bf16[384,1536]{1,0:T(8,128)(2,1)S(1)}, u32[]{:S(2)}) copy-start(bf16[384,1536]{1,0:T(8,128)(2,1)S(1)} %collective-permute-done.2.refs_6_) | copy-start | bytes 3538948
  172.5 46.4 %collective-permute-start.13 = (bf16[384,1024]{1,0:T(8,128)(2,1)}, bf16[384,1024]{1,0:T(8,128)(2,1)}, u32[]{:S(2)}, u32[]{:S(2)}) collective-permute-start(bf16[384,1024]{1,0:T(8,128)(2,1)} %collective-permute-done.12.refs_3_.refs_4_), channel_id=1, source_target_pairs={{0,1},{1,2},{2,3},{3,4},{4,5},{5,6},{6,7},{8,9},{9,10},{10,11},{11... | collective-permute-start | bytes 2359304 | tf_op jit(solution)/shard_map/ppermute | solution.py:91
  198.1 31.0 %collective-permute-start.17 = (bf16[384,1024]{1,0:T(8,128)(2,1)}, bf16[384,1024]{1,0:T(8,128)(2,1)S(1)}, u32[]{:S(2)}, u32[]{:S(2)}) collective-permute-start(bf16[384,1024]{1,0:T(8,128)(2,1)} %collective-permute-done.15.refs_3_.refs_4_), channel_id=1, source_target_pairs={{1,0},{2,1},{3,2},{4,3},{5,4},{6,5},{7,6},{9,8},{10,9},{11,10},{12... | collective-permute-start | bytes 2359304 | tf_op jit(solution)/shard_map/ppermute | solution.py:91
  201.4 27.7 %collective-permute-start.16 = (bf16[384,1024]{1,0:T(8,128)(2,1)}, bf16[384,1024]{1,0:T(8,128)(2,1)}, u32[]{:S(2)}, u32[]{:S(2)}) collective-permute-start(bf16[384,1024]{1,0:T(8,128)(2,1)} %collective-permute-done.15.refs_3_.refs_4_), channel_id=1, source_target_pairs={{0,1},{1,2},{2,3},{3,4},{4,5},{5,6},{6,7},{8,9},{9,10},{10,11},{11... | collective-permute-start | bytes 2359304 | tf_op jit(solution)/shard_map/ppermute | solution.py:91
  229.9 10.2 %copy-start.9 = (bf16[384,512]{1,0:T(8,128)(2,1)S(1)}, bf16[384,512]{1,0:T(8,128)(2,1)}, u32[]{:S(2)}) copy-start(bf16[384,512]{1,0:T(8,128)(2,1)} %shard_map.91) | copy-start | bytes 1179652
  240.1 3.4 %copy-start.10 = (bf16[384,512]{1,0:T(8,128)(2,1)S(1)}, bf16[384,512]{1,0:T(8,128)(2,1)}, u32[]{:S(2)}) copy-start(bf16[384,512]{1,0:T(8,128)(2,1)} %shard_map.92) | copy-start | bytes 1179652
  243.5 3.4 %copy-start.11 = (bf16[384,512]{1,0:T(8,128)(2,1)S(1)}, bf16[384,512]{1,0:T(8,128)(2,1)}, u32[]{:S(2)}) copy-start(bf16[384,512]{1,0:T(8,128)(2,1)} %shard_map.93) | copy-start | bytes 1179652
  243.6 3.4 %copy-start.12 = (f32[3072]{0:T(1024)S(1)}, f32[3072]{0:T(1024)}, u32[]{:S(2)}) copy-start(f32[3072]{0:T(1024)} %param.15) | copy-start | bytes 36868
  (3 other events, 3.6 us)
Sparse Core Ops, SparseCore 0:
  9.6 129.6 all-gather.1

commit v8 on v5

--- a/solution.py
+++ b/solution.py
@@ -8,7 +8,7 @@
 
 
 TW = 8
-GROUPS = 2
+SIZES = (5, 4, 3)
 
 
 def group_attention(queries, slots, usable, head_base, group_heads, head_dim, score_scale):
@@ -82,9 +82,8 @@
     head_count = head_windows.shape[0]
     head_dim = feat_width // head_count
     score_scale = 1.0 / math.sqrt(head_dim)
-    groups = GROUPS if head_count % GROUPS == 0 else 1
-    group_heads = head_count // groups
-    group_width = group_heads * head_dim
+    sizes = SIZES if sum(SIZES) == head_count else (head_count,)
+    starts = [sum(sizes[:g]) for g in range(len(sizes))]
 
     to_right = [(i, i + 1) for i in range(devices) if i % TW < TW - 1]
     to_left = [(i + 1, i) for i in range(devices) if i % TW < TW - 1]
@@ -99,7 +98,7 @@
     column_lens = jnp.concatenate([tile_lengths] + vert_lens)
     left_lens = jnp.concatenate([fetch(to_right)] + [fetch(left_of(p)) for p in verticals])
     right_lens = jnp.concatenate([fetch(to_left)] + [fetch(right_of(p)) for p in verticals])
-    (left_k, left_v), (right_k, right_v) = sideways((keys, values))
+    left_kv, right_kv = sideways(jnp.concatenate([keys, values], axis=1))
 
     positions = jnp.arange(tile_rows, dtype=jnp.int32)
     query_real = positions < tile_lengths[0]
@@ -110,11 +109,12 @@
     key_real = positions[None, :] < length_stack[:, None]
 
     def chunk(x, g):
-        return lax.slice_in_dim(x, g * group_width, (g + 1) * group_width, axis=1)
+        return lax.slice_in_dim(x, starts[g] * head_dim, (starts[g] + sizes[g]) * head_dim, axis=1)
 
     outputs = []
     previous = None
-    for g in range(groups):
+    for g in range(len(sizes)):
+        group_heads = sizes[g]
         own = jnp.concatenate([chunk(keys, g), chunk(values, g)], axis=1)
         if previous is not None:
             own, _ = lax.optimization_barrier((own, previous))
@@ -122,12 +122,12 @@
         if got:
             previous = got[-1]
         forwarded = [sideways(item) for item in got]
-        base = g * group_heads
+        base = starts[g]
         slots = [(keys, values, base, base)]
         slots += [(item, item, 0, group_heads) for item in got]
-        slots += [(left_k, left_v, base, base)]
+        slots += [(left_kv, left_kv, base, head_count + base)]
         slots += [(item[0], item[0], 0, group_heads) for item in forwarded]
-        slots += [(right_k, right_v, base, base)]
+        slots += [(right_kv, right_kv, base, head_count + base)]
         slots += [(item[1], item[1], 0, group_heads) for item in forwarded]
         reach = lax.slice_in_dim(head_windows, base, base + group_heads, axis=0)
         window = (far_rows[None, :] <= reach[:, 0:1]) & (far_cols[None, :] <= reach[:, 1:2])

time: 291 us -> 248 us (0.85)
  waiting for transfers between devices: 184 us -> 139 us
  other arithmetic: 2.28 us -> 7.72 us
  starting transfers between devices: 43 us -> 39.3 us
    ppermute x2 -> x3, waiting for transfers between devices: 94.1 us -> 68.3 us  [on_device(): got = [lax.ppermute(own, 'seq', pairs) for pairs in verticals]]
    ppermute x4, waiting for transfers between devices: 34.8 us -> 13.8 us  [on_device(): lax.ppermute(x, 'seq', to_left)]
    ppermute x4, starting transfers between devices: 14 us -> 7.87 us  [on_device(): lax.ppermute(x, 'seq', to_left)]
    ppermute x5, starting transfers between devices: 18.1 us -> 14.2 us  [on_device(): fetch = lambda pairs: lax.ppermute(tile_lengths, 'seq', pairs)]
    ppermute x4, waiting for transfers between devices: 0.01 us -> 3.56 us  [on_device(): lax.ppermute(x, 'seq', to_right)]
    ppermute x2 -> x3, starting transfers between devices: 0.12 us -> 3.34 us  [on_device(): got = [lax.ppermute(own, 'seq', pairs) for pairs in verticals]]
    ppermute x4, starting transfers between devices: 10.7 us -> 13.9 us  [on_device(): lax.ppermute(x, 'seq', to_right)]
    pallas_call x2 -> x3, Pallas kernels: 28.3 us -> 30.5 us  [group_attention(): pl.pallas_call(kernel, grid=(group_heads,), in_specs=in_specs, out_specs=...]
  transfers between devices with their start and end apart: 16 -> 17, of which waited for: 8 -> 6; matrix products, arithmetic and copies ran while one was open for 2% -> 5% of each run, Pallas kernels for 10% -> 12%
where the time goes in v8:
time: 248 us; the launch traced here: 245 us
  waiting for transfers between devices  139 us (56%)
  starting transfers between devices  39.3 us (16%)
  Pallas kernels  30.5 us (12%)
  between operations  14.4 us (6%)
  matrix products  8.93 us (4%)
  other arithmetic  7.72 us (3%)
  local copies, waits for them, and re-layouts  5.62 us (2%)
    ppermute x3, waiting for transfers between devices, on_device(): got = [lax.ppermute(own, 'seq', pairs) for pairs in verticals]  68.3 us
    ppermute x5, waiting for transfers between devices, on_device(): fetch = lambda pairs: lax.ppermute(tile_lengths, 'seq', pairs)  52.4 us
    pallas_call x3, Pallas kernels, group_attention(): pl.pallas_call(kernel, grid=(group_heads,), in_specs=in_specs, out_specs=...  30.5 us
    ppermute x5, starting transfers between devices, on_device(): fetch = lambda pairs: lax.ppermute(tile_lengths, 'seq', pairs)  14.2 us
    ppermute x4, starting transfers between devices, on_device(): lax.ppermute(x, 'seq', to_right)  13.9 us
    ppermute x4, waiting for transfers between devices, on_device(): lax.ppermute(x, 'seq', to_left)  13.8 us
    dot_general x1, matrix products, on_device(): jnp.dot(attended_all, weight_all, preferred_element_type=jnp.float32)  8.93 us
    ppermute x4, starting transfers between devices, on_device(): lax.ppermute(x, 'seq', to_left)  7.87 us
  transfers between devices with their start and end apart: 17, of which 6 were waited for; matrix products, arithmetic and copies ran while one was open for 5% of the time, Pallas kernels for 12%

profile of v8, /device:TPU:27, one launch (start us, length us, event | category | flops | bytes accessed | tf_op | source)
XLA Modules:
  0.0 245.2 jit_solution(9613023068407610694)
XLA Ops:
  7.4 4.0 %collective-permute-start.6 = (s32[1]{0:T(128)}, s32[1]{0:T(128)}, u32[]{:S(2)}, u32[]{:S(2)}) collective-permute-start(s32[1]{0:T(128)} %param.12), channel_id=1, source_target_pairs={{0,1},{1,2},{2,3},{3,4},{4,5},{5,6},{6,7},{8,9},{9,10},{10,11},{11... | collective-permute-start | bytes 20 | tf_op jit(solution)/shard_map/ppermute | solution.py:96
  11.5 2.4 collective-permute-start
  13.9 1.1 constant_dynamic-update-slice_fusion.1
  15.0 1.1 constant_dynamic-update-slice_fusion
  16.1 2.3 collective-permute-start.1
  18.4 2.1 collective-permute-start.3
  20.6 1.0 pad_maximum_fusion.1
  21.7 66.3 %collective-permute-done.refs_3_.refs_4_ = bf16[384,1280]{1,0:T(8,128)(2,1)} collective-permute-done((bf16[384,1280]{1,0:T(8,128)(2,1)S(1)}, bf16[384,1280]{1,0:T(8,128)(2,1)}, u32[]{:S(2)}, u32[]{:S(2)}) %collective-permute-start) | collective-permute-done | bytes 983072 | tf_op jit(solution)/shard_map/ppermute | solution.py:121
  88.1 0.9 pad_maximum_fusion.2
  89.6 1.9 collective-permute-start.7
  91.6 4.7 %collective-permute-start.8 = (s32[1]{0:T(128)}, s32[1]{0:T(128)}, u32[]{:S(2)}, u32[]{:S(2)}) collective-permute-start(s32[1]{0:T(128)} %param.12), channel_id=1, source_target_pairs={{1,0},{2,1},{3,2},{4,3},{5,4},{6,5},{7,6},{9,8},{10,9},{11,10},{12... | collective-permute-start | bytes 20 | tf_op jit(solution)/shard_map/ppermute | solution.py:96
  96.2 51.1 %collective-permute-done.7 = s32[1]{0:T(128)} collective-permute-done((s32[1]{0:T(128)}, s32[1]{0:T(128)}, u32[]{:S(2)}, u32[]{:S(2)}) %collective-permute-start.7) | collective-permute-done | bytes 36 | tf_op jit(solution)/shard_map/ppermute | solution.py:96
  147.3 3.5 %collective-permute-start.9 = (s32[1]{0:T(128)}, s32[1]{0:T(128)}, u32[]{:S(2)}, u32[]{:S(2)}) collective-permute-start(s32[1]{0:T(128)} %param.12), channel_id=1, source_target_pairs={{1,8},{2,9},{3,10},{4,11},{5,12},{6,13},{7,14},{9,0},{10,1},{11,2}... | collective-permute-start | bytes 20 | tf_op jit(solution)/shard_map/ppermute | solution.py:96
  150.8 1.9 collective-permute-start.2
  152.7 1.3 collective-permute-done.9
  154.1 1.9 collective-permute-start.4
  156.3 3.2 %concatenate.20 = s32[6]{0:T(128)S(1)} concatenate(s32[1]{0:T(128)} %copy.11, s32[1]{0:T(128)} %collective-permute-done.5, s32[1]{0:T(128)} %collective-permute-done.6, s32[1]{0:T(128)} %collective-permute-done.7, s32[1]{0:T(128)} %collective-permute-done.8, s32[1]{0:T(128)} %collective-permute-done.9), dimensions={0} | concatenate | bytes 48 | tf_op jit(solution)/shard_map/concatenate | solution.py:108
  159.5 1.0 collective-permute-start.13
  160.5 3.6 %collective-permute-done.2.refs_7_.refs_8_ = bf16[384,1280]{1,0:T(8,128)(2,1)S(1)} collective-permute-done((bf16[384,1280]{1,0:T(8,128)(2,1)}, bf16[384,1280]{1,0:T(8,128)(2,1)S(1)}, u32[]{:S(2)}, u32[]{:S(2)}) %collective-permute-start.2) | collective-permute-done | bytes 983072 | tf_op jit(solution)/shard_map/ppermute | solution.py:90
  164.1 4.3 %collective-permute-start.11 = (bf16[384,1024]{1,0:T(8,128)(2,1)}, bf16[384,1024]{1,0:T(8,128)(2,1)}, u32[]{:S(2)}, u32[]{:S(2)}) collective-permute-start(bf16[384,1024]{1,0:T(8,128)(2,1)} %collective-permute-done.10.refs_3_.refs_4_), channel_id=1, source_target_pairs={{0,1},{1,2},{2,3},{3,4},{4,5},{5,6},{6,7},{8,9},{9,10},{10,11},{11... | collective-permute-start | bytes 2359304 | tf_op jit(solution)/shard_map/ppermute | solution.py:90
  168.4 13.8 %collective-permute-done.4.refs_11_.refs_12_ = bf16[384,1280]{1,0:T(8,128)(2,1)} collective-permute-done((bf16[384,1280]{1,0:T(8,128)(2,1)}, bf16[384,1280]{1,0:T(8,128)(2,1)}, u32[]{:S(2)}, u32[]{:S(2)}) %collective-permute-start.4) | collective-permute-done | bytes 983072 | tf_op jit(solution)/shard_map/ppermute | solution.py:90
  182.1 1.9 collective-permute-start.12
  185.4 2.0 collective-permute-done.13.refs_3_.refs_4_
  187.4 5.4 %collective-permute-start.14 = (bf16[384,768]{1,0:T(8,128)(2,1)}, bf16[384,768]{1,0:T(8,128)(2,1)}, u32[]{:S(2)}, u32[]{:S(2)}) collective-permute-start(bf16[384,768]{1,0:T(8,128)(2,1)} %collective-permute-done.13.refs_3_.refs_4_), channel_id=1, source_target_pairs={{0,1},{1,2},{2,3},{3,4},{4,5},{5,6},{6,7},{8,9},{9,10},{10,11},{11... | collective-permute-start | bytes 1769480 | tf_op jit(solution)/shard_map/ppermute | solution.py:90
  192.8 1.9 collective-permute-start.15
  195.4 12.2 %shard_map.91 = bf16[384,640]{1,0:T(8,128)(2,1)} custom-call(bf16[384,1536]{1,0:T(8,128)(2,1)} %refs_0_.5, bf16[384,1536]{1,0:T(8,128)(2,1)} %refs_1_.5, bf16[384,1536]{1,0:T(8,128)(2,1)} %refs_2_.5, bf16[384,1280]{1,0:T(8,128)(2,1)} %collective-permute-done.refs_3_.refs_4_, bf16[384,1280]{1,0:T(8,128)(2,1)} %collective-permute-done.refs_3_.refs_4_, ...), custom_call_target="tpu_custom_call" | custom-call | tf_op jit(solution)/shard_map/pallas_call | solution.py:58
  207.6 1.2 broadcast_select_fusion
  208.8 10.2 %shard_map.92 = bf16[384,512]{1,0:T(8,128)(2,1)} custom-call(bf16[384,1536]{1,0:T(8,128)(2,1)} %refs_0_.5, bf16[384,1536]{1,0:T(8,128)(2,1)} %refs_1_.5, bf16[384,1536]{1,0:T(8,128)(2,1)} %refs_2_.5, bf16[384,1024]{1,0:T(8,128)(2,1)} %collective-permute-done.10.refs_3_.refs_4_, bf16[384,1024]{1,0:T(8,128)(2,1)} %collective-permute-done.10.refs_3_.refs_4_, ...), custom_call_target="tpu_custom_call" | custom-call | tf_op jit(solution)/shard_map/pallas_call | solution.py:58
  219.0 1.1 broadcast_select_fusion.1
  220.1 8.1 %shard_map.93 = bf16[384,384]{1,0:T(8,128)(2,1)} custom-call(bf16[384,1536]{1,0:T(8,128)(2,1)} %refs_0_.5, bf16[384,1536]{1,0:T(8,128)(2,1)} %refs_1_.5, bf16[384,1536]{1,0:T(8,128)(2,1)} %refs_2_.5, bf16[384,768]{1,0:T(8,128)(2,1)} %collective-permute-done.13.refs_3_.refs_4_, bf16[384,768]{1,0:T(8,128)(2,1)} %collective-permute-done.13.refs_3_.refs_4_, ...), custom_call_target="tpu_custom_call" | custom-call | tf_op jit(solution)/shard_map/pallas_call | solution.py:58
  228.3 1.1 broadcast_select_fusion.2
  229.4 8.9 %multiply_convert_fusion = bf16[384,3072]{1,0:T(8,128)(2,1)} fusion(bf16[1536,3072]{1,0:T(8,128)(2,1)} %all-gather.2.cloned.1.call-done, f32[3072]{0:T(1024)S(1)} %copy-done.7, bf16[384,384]{1,0:T(8,128)(2,1)S(1)} %broadcast_select_fusion.2, bf16[384,512]{1,0:T(8,128)(2,1)S(1)} %broadcast_select_fusion.1, bf16[384,640]{1,0:T(8,128)(2,1)S(1)} %broadcast_select_fusion), kind=kOutput, calls=%fused_computation | convolution fusion | flops 3629776896 | bytes 12988416 | tf_op jit(solution)/shard_map/dot_general | solution.py:139
  (55 shorter events, 3.5 us)
Async XLA Ops:
  6.5 4.8 %slice-start = ((bf16[384,1536]{1,0:T(8,128)(2,1)}), bf16[384,640]{1,0:T(8,128)(2,1)S(1)}, s32[]{:S(2)}) async-start(bf16[384,1536]{1,0:T(8,128)(2,1)} %refs_1_.5), calls=%async_computation.1 | async-start | bytes 983040 | tf_op jit(solution)/shard_map/slice | solution.py:112
  6.5 7.3 %copy-start.1 = (bf16[384,1536]{1,0:T(8,128)(2,1)S(1)}, bf16[384,1536]{1,0:T(8,128)(2,1)}, u32[]{:S(2)}) copy-start(bf16[384,1536]{1,0:T(8,128)(2,1)} %refs_1_.5) | copy-start | bytes 3538948
  6.5 4.8 %slice-start.3 = ((bf16[384,1536]{1,0:T(8,128)(2,1)}), bf16[384,640]{1,0:T(8,128)(2,1)S(1)}, s32[]{:S(2)}) async-start(bf16[384,1536]{1,0:T(8,128)(2,1)} %refs_2_.5), calls=%async_computation.4 | async-start | bytes 983040 | tf_op jit(solution)/shard_map/slice | solution.py:112
  6.5 222.9 %all-gather.2.cloned.1.call-start = ((), (), s32[]{:S(2)}) async-start(), calls=%async_computation | async-start | bytes 10027008 | tf_op jit(solution)/shard_map/all_gather | solution.py:92
  7.3 82.4 %collective-permute-start.5 = (s32[1]{0:T(128)}, s32[1]{0:T(128)}, u32[]{:S(2)}, u32[]{:S(2)}) collective-permute-start(s32[1]{0:T(128)} %param.12), channel_id=1, source_target_pairs={{0,8},{1,9},{2,10},{3,11},{4,12},{5,13},{6,14},{7,15},{8,0},{9,1},... | collective-permute-start | bytes 20 | tf_op jit(solution)/shard_map/ppermute | solution.py:96
  7.4 84.2 %collective-permute-start.6 = (s32[1]{0:T(128)}, s32[1]{0:T(128)}, u32[]{:S(2)}, u32[]{:S(2)}) collective-permute-start(s32[1]{0:T(128)} %param.12), channel_id=1, source_target_pairs={{0,1},{1,2},{2,3},{3,4},{4,5},{5,6},{6,7},{8,9},{9,10},{10,11},{11... | collective-permute-start | bytes 20 | tf_op jit(solution)/shard_map/ppermute | solution.py:96
  11.4 3.6 %copy-start.2 = (bf16[384,1536]{1,0:T(8,128)(2,1)S(1)}, bf16[384,1536]{1,0:T(8,128)(2,1)}, u32[]{:S(2)}) copy-start(bf16[384,1536]{1,0:T(8,128)(2,1)} %refs_2_.5) | copy-start | bytes 3538948
  11.5 76.6 %collective-permute-start = (bf16[384,1280]{1,0:T(8,128)(2,1)S(1)}, bf16[384,1280]{1,0:T(8,128)(2,1)}, u32[]{:S(2)}, u32[]{:S(2)}) collective-permute-start(bf16[384,1280]{1,0:T(8,128)(2,1)S(1)} %pad_maximum_fusion), channel_id=1, source_target_pairs={{0,8},{1,9},{2,10},{3,11},{4,12},{5,13},{6,14},{7,15},{8,0},{9,1},... | collective-permute-start | bytes 2949128 | tf_op jit(solution)/shard_map/ppermute | solution.py:121
  15.0 5.6 %copy-start.4 = (s32[12,2]{0,1:T(2,128)S(1)}, s32[12,2]{0,1:T(2,128)}, u32[]{:S(2)}) copy-start(s32[12,2]{0,1:T(2,128)} %param.13) | copy-start | bytes 292
  15.0 5.7 %slice-start.1 = ((bf16[384,1536]{1,0:T(8,128)(2,1)}), bf16[384,512]{1,0:T(8,128)(2,1)S(1)}, s32[]{:S(2)}) async-start(bf16[384,1536]{1,0:T(8,128)(2,1)} %refs_1_.5), calls=%async_computation.2 | async-start | bytes 786432 | tf_op jit(solution)/shard_map/slice | solution.py:112
  15.0 5.7 %slice-start.4 = ((bf16[384,1536]{1,0:T(8,128)(2,1)}), bf16[384,512]{1,0:T(8,128)(2,1)S(1)}, s32[]{:S(2)}) async-start(bf16[384,1536]{1,0:T(8,128)(2,1)} %refs_2_.5), calls=%async_computation.5 | async-start | bytes 786432 | tf_op jit(solution)/shard_map/slice | solution.py:112
  16.1 72.0 %slice-start.2 = ((bf16[384,1536]{1,0:T(8,128)(2,1)}), bf16[384,384]{1,0:T(8,128)(2,1)S(1)}, s32[]{:S(2)}) async-start(bf16[384,1536]{1,0:T(8,128)(2,1)} %refs_1_.5), calls=%async_computation.3 | async-start | bytes 589824 | tf_op jit(solution)/shard_map/slice | solution.py:112
  16.1 72.0 %slice-start.5 = ((bf16[384,1536]{1,0:T(8,128)(2,1)}), bf16[384,384]{1,0:T(8,128)(2,1)S(1)}, s32[]{:S(2)}) async-start(bf16[384,1536]{1,0:T(8,128)(2,1)} %refs_2_.5), calls=%async_computation.6 | async-start | bytes 589824 | tf_op jit(solution)/shard_map/slice | solution.py:112
  16.1 176.7 %collective-permute-start.1 = (bf16[384,3072]{1,0:T(8,128)(2,1)}, bf16[384,3072]{1,0:T(8,128)(2,1)S(1)}, u32[]{:S(2)}, u32[]{:S(2)}) collective-permute-start(bf16[384,3072]{1,0:T(8,128)(2,1)} %constant_dynamic-update-slice_fusion), channel_id=1, source_target_pairs={{0,1},{1,2},{2,3},{3,4},{4,5},{5,6},{6,7},{8,9},{9,10},{10,11},{11... | collective-permute-start | bytes 7077896 | tf_op jit(solution)/shard_map/ppermute | solution.py:90
  18.4 177.0 %collective-permute-start.3 = (bf16[384,3072]{1,0:T(8,128)(2,1)}, bf16[384,3072]{1,0:T(8,128)(2,1)}, u32[]{:S(2)}, u32[]{:S(2)}) collective-permute-start(bf16[384,3072]{1,0:T(8,128)(2,1)} %constant_dynamic-update-slice_fusion), channel_id=1, source_target_pairs={{1,0},{2,1},{3,2},{4,3},{5,4},{6,5},{7,6},{9,8},{10,9},{11,10},{12... | collective-permute-start | bytes 7077896 | tf_op jit(solution)/shard_map/ppermute | solution.py:90
  20.5 135.5 %copy-start.5 = (s32[6]{0:T(128)S(1)}, s32[6]{0:T(128)}, u32[]{:S(2)}) copy-start(s32[6]{0:T(128)} %constant.7.clone) | copy-start | bytes 76
  20.5 135.5 %copy-start.6 = (s32[6]{0:T(128)S(1)}, s32[6]{0:T(128)}, u32[]{:S(2)}) copy-start(s32[6]{0:T(128)} %constant.8.clone) | copy-start | bytes 76
  88.1 71.4 %collective-permute-start.10 = (bf16[384,1024]{1,0:T(8,128)(2,1)}, bf16[384,1024]{1,0:T(8,128)(2,1)}, u32[]{:S(2)}, u32[]{:S(2)}) collective-permute-start(bf16[384,1024]{1,0:T(8,128)(2,1)} %pad_maximum_fusion.1), channel_id=1, source_target_pairs={{0,8},{1,9},{2,10},{3,11},{4,12},{5,13},{6,14},{7,15},{8,0},{9,1},... | collective-permute-start | bytes 2359304 | tf_op jit(solution)/shard_map/ppermute | solution.py:121
  89.6 57.7 %collective-permute-start.7 = (s32[1]{0:T(128)}, s32[1]{0:T(128)}, u32[]{:S(2)}, u32[]{:S(2)}) collective-permute-start(s32[1]{0:T(128)} %param.12), channel_id=1, source_target_pairs={{0,9},{1,10},{2,11},{3,12},{4,13},{5,14},{6,15},{8,1},{9,2},{10,3}... | collective-permute-start | bytes 20 | tf_op jit(solution)/shard_map/ppermute | solution.py:96
  91.6 59.2 %collective-permute-start.8 = (s32[1]{0:T(128)}, s32[1]{0:T(128)}, u32[]{:S(2)}, u32[]{:S(2)}) collective-permute-start(s32[1]{0:T(128)} %param.12), channel_id=1, source_target_pairs={{1,0},{2,1},{3,2},{4,3},{5,4},{6,5},{7,6},{9,8},{10,9},{11,10},{12... | collective-permute-start | bytes 20 | tf_op jit(solution)/shard_map/ppermute | solution.py:96
  147.3 6.8 %collective-permute-start.9 = (s32[1]{0:T(128)}, s32[1]{0:T(128)}, u32[]{:S(2)}, u32[]{:S(2)}) collective-permute-start(s32[1]{0:T(128)} %param.12), channel_id=1, source_target_pairs={{1,8},{2,9},{3,10},{4,11},{5,12},{6,13},{7,14},{9,0},{10,1},{11,2}... | collective-permute-start | bytes 20 | tf_op jit(solution)/shard_map/ppermute | solution.py:96
  150.8 13.3 %collective-permute-start.2 = (bf16[384,1280]{1,0:T(8,128)(2,1)}, bf16[384,1280]{1,0:T(8,128)(2,1)S(1)}, u32[]{:S(2)}, u32[]{:S(2)}) collective-permute-start(bf16[384,1280]{1,0:T(8,128)(2,1)} %collective-permute-done.refs_3_.refs_4_), channel_id=1, source_target_pairs={{0,1},{1,2},{2,3},{3,4},{4,5},{5,6},{6,7},{8,9},{9,10},{10,11},{11... | collective-permute-start | bytes 2949128 | tf_op jit(solution)/shard_map/ppermute | solution.py:90
  154.1 28.0 %collective-permute-start.4 = (bf16[384,1280]{1,0:T(8,128)(2,1)}, bf16[384,1280]{1,0:T(8,128)(2,1)}, u32[]{:S(2)}, u32[]{:S(2)}) collective-permute-start(bf16[384,1280]{1,0:T(8,128)(2,1)} %collective-permute-done.refs_3_.refs_4_), channel_id=1, source_target_pairs={{1,0},{2,1},{3,2},{4,3},{5,4},{6,5},{7,6},{9,8},{10,9},{11,10},{12... | collective-permute-start | bytes 2949128 | tf_op jit(solution)/shard_map/ppermute | solution.py:90
  159.5 27.9 %collective-permute-start.13 = (bf16[384,768]{1,0:T(8,128)(2,1)}, bf16[384,768]{1,0:T(8,128)(2,1)}, u32[]{:S(2)}, u32[]{:S(2)}) collective-permute-start(bf16[384,768]{1,0:T(8,128)(2,1)} %pad_maximum_fusion.2), channel_id=1, source_target_pairs={{0,8},{1,9},{2,10},{3,11},{4,12},{5,13},{6,14},{7,15},{8,0},{9,1},... | collective-permute-start | bytes 1769480 | tf_op jit(solution)/shard_map/ppermute | solution.py:121
  164.1 31.3 %copy-start.3 = (bf16[384,1280]{1,0:T(8,128)(2,1)}, bf16[384,1280]{1,0:T(8,128)(2,1)S(1)}, u32[]{:S(2)}) copy-start(bf16[384,1280]{1,0:T(8,128)(2,1)S(1)} %collective-permute-done.2.refs_7_.refs_8_) | copy-start | bytes 2949124
  164.1 44.7 %collective-permute-start.11 = (bf16[384,1024]{1,0:T(8,128)(2,1)}, bf16[384,1024]{1,0:T(8,128)(2,1)}, u32[]{:S(2)}, u32[]{:S(2)}) collective-permute-start(bf16[384,1024]{1,0:T(8,128)(2,1)} %collective-permute-done.10.refs_3_.refs_4_), channel_id=1, source_target_pairs={{0,1},{1,2},{2,3},{3,4},{4,5},{5,6},{6,7},{8,9},{9,10},{10,11},{11... | collective-permute-start | bytes 2359304 | tf_op jit(solution)/shard_map/ppermute | solution.py:90
  182.1 26.7 %collective-permute-start.12 = (bf16[384,1024]{1,0:T(8,128)(2,1)}, bf16[384,1024]{1,0:T(8,128)(2,1)}, u32[]{:S(2)}, u32[]{:S(2)}) collective-permute-start(bf16[384,1024]{1,0:T(8,128)(2,1)} %collective-permute-done.10.refs_3_.refs_4_), channel_id=1, source_target_pairs={{1,0},{2,1},{3,2},{4,3},{5,4},{6,5},{7,6},{9,8},{10,9},{11,10},{12... | collective-permute-start | bytes 2359304 | tf_op jit(solution)/shard_map/ppermute | solution.py:90
  187.4 32.7 %collective-permute-start.14 = (bf16[384,768]{1,0:T(8,128)(2,1)}, bf16[384,768]{1,0:T(8,128)(2,1)}, u32[]{:S(2)}, u32[]{:S(2)}) collective-permute-start(bf16[384,768]{1,0:T(8,128)(2,1)} %collective-permute-done.13.refs_3_.refs_4_), channel_id=1, source_target_pairs={{0,1},{1,2},{2,3},{3,4},{4,5},{5,6},{6,7},{8,9},{9,10},{10,11},{11... | collective-permute-start | bytes 1769480 | tf_op jit(solution)/shard_map/ppermute | solution.py:90
  192.8 2.6 %copy-start = (bf16[384,3072]{1,0:T(8,128)(2,1)}, bf16[384,3072]{1,0:T(8,128)(2,1)S(1)}, u32[]{:S(2)}) copy-start(bf16[384,3072]{1,0:T(8,128)(2,1)S(1)} %collective-permute-done.1.refs_5_.refs_6_) | copy-start | bytes 7077892
  192.8 27.4 %collective-permute-start.15 = (bf16[384,768]{1,0:T(8,128)(2,1)}, bf16[384,768]{1,0:T(8,128)(2,1)}, u32[]{:S(2)}, u32[]{:S(2)}) collective-permute-start(bf16[384,768]{1,0:T(8,128)(2,1)} %collective-permute-done.13.refs_3_.refs_4_), channel_id=1, source_target_pairs={{1,0},{2,1},{3,2},{4,3},{5,4},{6,5},{7,6},{9,8},{10,9},{11,10},{12... | collective-permute-start | bytes 1769480 | tf_op jit(solution)/shard_map/ppermute | solution.py:90
  220.1 9.3 %copy-start.7 = (f32[3072]{0:T(1024)S(1)}, f32[3072]{0:T(1024)}, u32[]{:S(2)}) copy-start(f32[3072]{0:T(1024)} %param.15) | copy-start | bytes 36868
Sparse Core Ops, SparseCore 0:
  9.6 137.3 all-gather.1

commit v9 on v8

--- a/solution.py
+++ b/solution.py
@@ -8,7 +8,7 @@
 
 
 TW = 8
-SIZES = (5, 4, 3)
+SIZES = (4, 5, 3)
 
 
 def group_attention(queries, slots, usable, head_base, group_heads, head_dim, score_scale):
@@ -98,7 +98,7 @@
     column_lens = jnp.concatenate([tile_lengths] + vert_lens)
     left_lens = jnp.concatenate([fetch(to_right)] + [fetch(left_of(p)) for p in verticals])
     right_lens = jnp.concatenate([fetch(to_left)] + [fetch(right_of(p)) for p in verticals])
-    left_kv, right_kv = sideways(jnp.concatenate([keys, values], axis=1))
+    (left_k, left_v), (right_k, right_v) = sideways((keys, values))
 
     positions = jnp.arange(tile_rows, dtype=jnp.int32)
     query_real = positions < tile_lengths[0]
@@ -125,9 +125,9 @@
         base = starts[g]
         slots = [(keys, values, base, base)]
         slots += [(item, item, 0, group_heads) for item in got]
-        slots += [(left_kv, left_kv, base, head_count + base)]
+        slots += [(left_k, left_v, base, base)]
         slots += [(item[0], item[0], 0, group_heads) for item in forwarded]
-        slots += [(right_kv, right_kv, base, head_count + base)]
+        slots += [(right_k, right_v, base, base)]
         slots += [(item[1], item[1], 0, group_heads) for item in forwarded]
         reach = lax.slice_in_dim(head_windows, base, base + group_heads, axis=0)
         window = (far_rows[None, :] <= reach[:, 0:1]) & (far_cols[None, :] <= reach[:, 1:2])

time: 248 us -> 279 us (1.12)
  starting transfers between devices: 39.3 us -> 85.1 us
  waiting for transfers between devices: 139 us -> 123 us
    ppermute x5, starting transfers between devices: 14.2 us -> 57.2 us  [on_device(): fetch = lambda pairs: lax.ppermute(tile_lengths, 'seq', pairs)]
    ppermute x3, waiting for transfers between devices: 68.3 us -> 104 us  [on_device(): got = [lax.ppermute(own, 'seq', pairs) for pairs in verticals]]
    ppermute x5, waiting for transfers between devices: 52.4 us -> 18 us  [on_device(): fetch = lambda pairs: lax.ppermute(tile_lengths, 'seq', pairs)]
    ppermute x4 -> x5, waiting for transfers between devices: 13.8 us -> 0.01 us  [on_device(): lax.ppermute(x, 'seq', to_left)]
    ppermute x4 -> x5, starting transfers between devices: 7.87 us -> 14 us  [on_device(): lax.ppermute(x, 'seq', to_left)]
    ppermute x4 -> x5, waiting for transfers between devices: 3.56 us -> 0.01 us  [on_device(): lax.ppermute(x, 'seq', to_right)]
    unnamed x17 -> x20, local copies, waits for them, and re-layouts: 1.13 us -> 4.31 us
    ppermute x4 -> x5, starting transfers between devices: 13.9 us -> 12.6 us  [on_device(): lax.ppermute(x, 'seq', to_right)]
  transfers between devices with their start and end apart: 17 -> 19, of which waited for: 6 -> 8; matrix products, arithmetic and copies ran while one was open for 5% -> 4% of each run, Pallas kernels for 12% -> 11%
where the time goes in v9:
time: 279 us; the launch traced here: 276 us
  waiting for transfers between devices  123 us (44%)
  starting transfers between devices  85.1 us (31%)
  Pallas kernels  30.4 us (11%)
  between operations  14.4 us (5%)
  matrix products  8.95 us (3%)
  local copies, waits for them, and re-layouts  8.17 us (3%)
  other arithmetic  6.76 us (2%)
    ppermute x3, waiting for transfers between devices, on_device(): got = [lax.ppermute(own, 'seq', pairs) for pairs in verticals]  104 us
    ppermute x5, starting transfers between devices, on_device(): fetch = lambda pairs: lax.ppermute(tile_lengths, 'seq', pairs)  57.2 us
    pallas_call x3, Pallas kernels, group_attention(): pl.pallas_call(kernel, grid=(group_heads,), in_specs=in_specs, out_specs=...  30.4 us
    ppermute x5, waiting for transfers between devices, on_device(): fetch = lambda pairs: lax.ppermute(tile_lengths, 'seq', pairs)  18 us
    ppermute x5, starting transfers between devices, on_device(): lax.ppermute(x, 'seq', to_left)  14 us
    ppermute x5, starting transfers between devices, on_device(): lax.ppermute(x, 'seq', to_right)  12.6 us
    dot_general x1, matrix products, on_device(): jnp.dot(attended_all, weight_all, preferred_element_type=jnp.float32)  8.95 us
  transfers between devices with their start and end apart: 19, of which 8 were waited for; matrix products, arithmetic and copies ran while one was open for 4% of the time, Pallas kernels for 11%

profile of v9, /device:TPU:27, one launch (start us, length us, event | category | flops | bytes accessed | tf_op | source)
XLA Modules:
  0.0 276.4 jit_solution(14409545478633655445)
XLA Ops:
  8.6 3.7 %collective-permute-start.1 = (bf16[384,1536]{1,0:T(8,128)(2,1)S(1)}, bf16[384,1536]{1,0:T(8,128)(2,1)}, u32[]{:S(2)}, u32[]{:S(2)}) collective-permute-start(bf16[384,1536]{1,0:T(8,128)(2,1)S(1)} %copy-done), channel_id=1, source_target_pairs={{0,1},{1,2},{2,3},{3,4},{4,5},{5,6},{6,7},{8,9},{9,10},{10,11},{11... | collective-permute-start | bytes 3538952 | tf_op jit(solution)/shard_map/ppermute | solution.py:90
  12.3 1.9 collective-permute-start.2
  14.2 2.4 collective-permute-start.4
  16.7 2.9 %collective-permute-start.5 = (bf16[384,1536]{1,0:T(8,128)(2,1)S(1)}, bf16[384,1536]{1,0:T(8,128)(2,1)}, u32[]{:S(2)}, u32[]{:S(2)}) collective-permute-start(bf16[384,1536]{1,0:T(8,128)(2,1)S(1)} %copy-done.1), channel_id=1, source_target_pairs={{1,0},{2,1},{3,2},{4,3},{5,4},{6,5},{7,6},{9,8},{10,9},{11,10},{12... | collective-permute-start | bytes 3538952 | tf_op jit(solution)/shard_map/ppermute | solution.py:90
  20.7 43.3 %collective-permute-done.refs_3_.refs_4_ = bf16[384,1024]{1,0:T(8,128)(2,1)} collective-permute-done((bf16[384,1024]{1,0:T(8,128)(2,1)S(1)}, bf16[384,1024]{1,0:T(8,128)(2,1)}, u32[]{:S(2)}, u32[]{:S(2)}) %collective-permute-start) | collective-permute-done | bytes 786464 | tf_op jit(solution)/shard_map/ppermute | solution.py:121
  64.0 2.4 collective-permute-start.10
  66.4 3.0 %collective-permute-done.10 = s32[1]{0:T(128)} collective-permute-done((s32[1]{0:T(128)}, s32[1]{0:T(128)}, u32[]{:S(2)}, u32[]{:S(2)}) %collective-permute-start.10) | collective-permute-done | bytes 36 | tf_op jit(solution)/shard_map/ppermute | solution.py:96
  69.4 50.9 %collective-permute-start.11 = (s32[1]{0:T(128)}, s32[1]{0:T(128)}, u32[]{:S(2)}, u32[]{:S(2)}) collective-permute-start(s32[1]{0:T(128)} %param.12), channel_id=1, source_target_pairs={{1,8},{2,9},{3,10},{4,11},{5,12},{6,13},{7,14},{9,0},{10,1},{11,2}... | collective-permute-start | bytes 20 | tf_op jit(solution)/shard_map/ppermute | solution.py:96
  121.2 3.6 %collective-permute-done.7 = s32[1]{0:T(128)} collective-permute-done((s32[1]{0:T(128)}, s32[1]{0:T(128)}, u32[]{:S(2)}, u32[]{:S(2)}) %collective-permute-start.7) | collective-permute-done | bytes 36 | tf_op jit(solution)/shard_map/ppermute | solution.py:96
  124.7 1.9 collective-permute-start.8
  126.7 5.0 %collective-permute-done.8 = s32[1]{0:T(128)} collective-permute-done((s32[1]{0:T(128)}, s32[1]{0:T(128)}, u32[]{:S(2)}, u32[]{:S(2)}) %collective-permute-start.8) | collective-permute-done | bytes 36 | tf_op jit(solution)/shard_map/ppermute | solution.py:96
  131.7 1.9 collective-permute-start.9
  133.6 5.6 %collective-permute-done.9 = s32[1]{0:T(128)} collective-permute-done((s32[1]{0:T(128)}, s32[1]{0:T(128)}, u32[]{:S(2)}, u32[]{:S(2)}) %collective-permute-start.9) | collective-permute-done | bytes 36 | tf_op jit(solution)/shard_map/ppermute | solution.py:96
  139.2 1.2 collective-permute-start.12
  141.5 40.0 %collective-permute-done.12.refs_3_.refs_4_ = bf16[384,1280]{1,0:T(8,128)(2,1)} collective-permute-done((bf16[384,1280]{1,0:T(8,128)(2,1)S(1)}, bf16[384,1280]{1,0:T(8,128)(2,1)}, u32[]{:S(2)}, u32[]{:S(2)}) %collective-permute-start.12) | collective-permute-done | bytes 983072 | tf_op jit(solution)/shard_map/ppermute | solution.py:121
  181.5 1.9 collective-permute-start.3
  183.4 3.2 %concatenate.16 = s32[6]{0:T(128)S(1)} concatenate(s32[1]{0:T(128)} %copy.10, s32[1]{0:T(128)} %collective-permute-done.7, s32[1]{0:T(128)} %collective-permute-done.8, s32[1]{0:T(128)} %collective-permute-done.9, s32[1]{0:T(128)} %collective-permute-done.10, s32[1]{0:T(128)} %collective-permute-done.11), dimensions={0} | concatenate | bytes 48 | tf_op jit(solution)/shard_map/concatenate | solution.py:108
  186.6 2.4 collective-permute-start.6
  189.1 3.2 %collective-permute-start.13 = (bf16[384,1280]{1,0:T(8,128)(2,1)}, bf16[384,1280]{1,0:T(8,128)(2,1)S(1)}, u32[]{:S(2)}, u32[]{:S(2)}) collective-permute-start(bf16[384,1280]{1,0:T(8,128)(2,1)} %collective-permute-done.12.refs_3_.refs_4_), channel_id=1, source_target_pairs={{0,1},{1,2},{2,3},{3,4},{4,5},{5,6},{6,7},{8,9},{9,10},{10,11},{11... | collective-permute-start | bytes 2949128 | tf_op jit(solution)/shard_map/ppermute | solution.py:90
  192.3 3.3 %collective-permute-start.14 = (bf16[384,1280]{1,0:T(8,128)(2,1)}, bf16[384,1280]{1,0:T(8,128)(2,1)S(1)}, u32[]{:S(2)}, u32[]{:S(2)}) collective-permute-start(bf16[384,1280]{1,0:T(8,128)(2,1)} %collective-permute-done.12.refs_3_.refs_4_), channel_id=1, source_target_pairs={{1,0},{2,1},{3,2},{4,3},{5,4},{6,5},{7,6},{9,8},{10,9},{11,10},{12... | collective-permute-start | bytes 2949128 | tf_op jit(solution)/shard_map/ppermute | solution.py:90
  197.1 20.6 %collective-permute-done.15.refs_3_.refs_4_ = bf16[384,768]{1,0:T(8,128)(2,1)} collective-permute-done((bf16[384,768]{1,0:T(8,128)(2,1)}, bf16[384,768]{1,0:T(8,128)(2,1)}, u32[]{:S(2)}, u32[]{:S(2)}) %collective-permute-start.15) | collective-permute-done | bytes 589856 | tf_op jit(solution)/shard_map/ppermute | solution.py:121
  217.7 1.9 collective-permute-start.16
  219.6 2.9 %collective-permute-start.17 = (bf16[384,768]{1,0:T(8,128)(2,1)}, bf16[384,768]{1,0:T(8,128)(2,1)S(1)}, u32[]{:S(2)}, u32[]{:S(2)}) collective-permute-start(bf16[384,768]{1,0:T(8,128)(2,1)} %collective-permute-done.15.refs_3_.refs_4_), channel_id=1, source_target_pairs={{1,0},{2,1},{3,2},{4,3},{5,4},{6,5},{7,6},{9,8},{10,9},{11,10},{12... | collective-permute-start | bytes 1769480 | tf_op jit(solution)/shard_map/ppermute | solution.py:90
  223.2 10.1 %shard_map.91 = bf16[384,512]{1,0:T(8,128)(2,1)} custom-call(bf16[384,1536]{1,0:T(8,128)(2,1)} %refs_0_.5, bf16[384,1536]{1,0:T(8,128)(2,1)} %refs_1_.5, bf16[384,1536]{1,0:T(8,128)(2,1)} %refs_2_.5, bf16[384,1024]{1,0:T(8,128)(2,1)} %collective-permute-done.refs_3_.refs_4_, bf16[384,1024]{1,0:T(8,128)(2,1)} %collective-permute-done.refs_3_.refs_4_, ...), custom_call_target="tpu_custom_call" | custom-call | tf_op jit(solution)/shard_map/pallas_call | solution.py:58
  233.3 1.1 broadcast_select_fusion.1
  234.5 0.9 copy-done.2
  235.4 1.0 copy-done.3
  236.4 12.2 %shard_map.92 = bf16[384,640]{1,0:T(8,128)(2,1)} custom-call(bf16[384,1536]{1,0:T(8,128)(2,1)} %refs_0_.5, bf16[384,1536]{1,0:T(8,128)(2,1)} %refs_1_.5, bf16[384,1536]{1,0:T(8,128)(2,1)} %refs_2_.5, bf16[384,1280]{1,0:T(8,128)(2,1)} %collective-permute-done.12.refs_3_.refs_4_, bf16[384,1280]{1,0:T(8,128)(2,1)} %collective-permute-done.12.refs_3_.refs_4_, ...), custom_call_target="tpu_custom_call" | custom-call | tf_op jit(solution)/shard_map/pallas_call | solution.py:58
  248.6 1.2 broadcast_select_fusion
  251.4 8.1 %shard_map.93 = bf16[384,384]{1,0:T(8,128)(2,1)} custom-call(bf16[384,1536]{1,0:T(8,128)(2,1)} %refs_0_.5, bf16[384,1536]{1,0:T(8,128)(2,1)} %refs_1_.5, bf16[384,1536]{1,0:T(8,128)(2,1)} %refs_2_.5, bf16[384,768]{1,0:T(8,128)(2,1)} %collective-permute-done.15.refs_3_.refs_4_, bf16[384,768]{1,0:T(8,128)(2,1)} %collective-permute-done.15.refs_3_.refs_4_, ...), custom_call_target="tpu_custom_call" | custom-call | tf_op jit(solution)/shard_map/pallas_call | solution.py:58
  259.5 1.1 broadcast_select_fusion.2
  260.6 9.0 %multiply_convert_fusion = bf16[384,3072]{1,0:T(8,128)(2,1)} fusion(bf16[1536,3072]{1,0:T(8,128)(2,1)} %all-gather.2.cloned.1.call-done, f32[3072]{0:T(1024)S(1)} %copy-done.9, bf16[384,384]{1,0:T(8,128)(2,1)S(1)} %broadcast_select_fusion.2, bf16[384,640]{1,0:T(8,128)(2,1)S(1)} %broadcast_select_fusion, bf16[384,512]{1,0:T(8,128)(2,1)S(1)} %broadcast_select_fusion.1), kind=kOutput, calls=%fused_computation | convolution fusion | flops 3629776896 | bytes 12988416 | tf_op jit(solution)/shard_map/dot_general | solution.py:139
  (57 shorter events, 8.3 us)
Async XLA Ops:
  6.5 1.0 slice-start
  6.5 1.1 slice-start.1
  6.5 254.1 %all-gather.2.cloned.1.call-start = ((), (), s32[]{:S(2)}) async-start(), calls=%async_computation | async-start | bytes 10027008 | tf_op jit(solution)/shard_map/all_gather | solution.py:92
  7.3 1.3 copy-start
  7.3 5.0 %copy-start.1 = (bf16[384,1536]{1,0:T(8,128)(2,1)S(1)}, bf16[384,1536]{1,0:T(8,128)(2,1)}, u32[]{:S(2)}) copy-start(bf16[384,1536]{1,0:T(8,128)(2,1)} %refs_2_.5) | copy-start | bytes 3538948
  7.7 12.0 %copy-start.6 = (s32[12,2]{0,1:T(2,128)S(1)}, s32[12,2]{0,1:T(2,128)}, u32[]{:S(2)}) copy-start(s32[12,2]{0,1:T(2,128)} %param.13) | copy-start | bytes 292
  7.7 56.2 %collective-permute-start = (bf16[384,1024]{1,0:T(8,128)(2,1)S(1)}, bf16[384,1024]{1,0:T(8,128)(2,1)}, u32[]{:S(2)}, u32[]{:S(2)}) collective-permute-start(bf16[384,1024]{1,0:T(8,128)(2,1)S(1)} %pad_maximum_fusion.1), channel_id=1, source_target_pairs={{0,8},{1,9},{2,10},{3,11},{4,12},{5,13},{6,14},{7,15},{8,0},{9,1},... | collective-permute-start | bytes 2359304 | tf_op jit(solution)/shard_map/ppermute | solution.py:121
  8.6 178.0 %collective-permute-start.1 = (bf16[384,1536]{1,0:T(8,128)(2,1)S(1)}, bf16[384,1536]{1,0:T(8,128)(2,1)}, u32[]{:S(2)}, u32[]{:S(2)}) collective-permute-start(bf16[384,1536]{1,0:T(8,128)(2,1)S(1)} %copy-done), channel_id=1, source_target_pairs={{0,1},{1,2},{2,3},{3,4},{4,5},{5,6},{6,7},{8,9},{9,10},{10,11},{11... | collective-permute-start | bytes 3538952 | tf_op jit(solution)/shard_map/ppermute | solution.py:90
  12.3 176.7 %collective-permute-start.2 = (bf16[384,1536]{1,0:T(8,128)(2,1)S(1)}, bf16[384,1536]{1,0:T(8,128)(2,1)}, u32[]{:S(2)}, u32[]{:S(2)}) collective-permute-start(bf16[384,1536]{1,0:T(8,128)(2,1)S(1)} %copy-done.1), channel_id=1, source_target_pairs={{0,1},{1,2},{2,3},{3,4},{4,5},{5,6},{6,7},{8,9},{9,10},{10,11},{11... | collective-permute-start | bytes 3538952 | tf_op jit(solution)/shard_map/ppermute | solution.py:90
  14.2 174.9 %collective-permute-start.4 = (bf16[384,1536]{1,0:T(8,128)(2,1)S(1)}, bf16[384,1536]{1,0:T(8,128)(2,1)}, u32[]{:S(2)}, u32[]{:S(2)}) collective-permute-start(bf16[384,1536]{1,0:T(8,128)(2,1)S(1)} %copy-done), channel_id=1, source_target_pairs={{1,0},{2,1},{3,2},{4,3},{5,4},{6,5},{7,6},{9,8},{10,9},{11,10},{12... | collective-permute-start | bytes 3538952 | tf_op jit(solution)/shard_map/ppermute | solution.py:90
  16.7 175.6 %collective-permute-start.5 = (bf16[384,1536]{1,0:T(8,128)(2,1)S(1)}, bf16[384,1536]{1,0:T(8,128)(2,1)}, u32[]{:S(2)}, u32[]{:S(2)}) collective-permute-start(bf16[384,1536]{1,0:T(8,128)(2,1)S(1)} %copy-done.1), channel_id=1, source_target_pairs={{1,0},{2,1},{3,2},{4,3},{5,4},{6,5},{7,6},{9,8},{10,9},{11,10},{12... | collective-permute-start | bytes 3538952 | tf_op jit(solution)/shard_map/ppermute | solution.py:90
  19.9 121.4 %copy-start.7 = (s32[6]{0:T(128)S(1)}, s32[6]{0:T(128)}, u32[]{:S(2)}) copy-start(s32[6]{0:T(128)} %constant.7.clone) | copy-start | bytes 76
  19.9 121.4 %copy-start.8 = (s32[6]{0:T(128)S(1)}, s32[6]{0:T(128)}, u32[]{:S(2)}) copy-start(s32[6]{0:T(128)} %constant.8.clone) | copy-start | bytes 76
  64.0 5.4 %collective-permute-start.10 = (s32[1]{0:T(128)}, s32[1]{0:T(128)}, u32[]{:S(2)}, u32[]{:S(2)}) collective-permute-start(s32[1]{0:T(128)} %param.12), channel_id=1, source_target_pairs={{1,0},{2,1},{3,2},{4,3},{5,4},{6,5},{7,6},{9,8},{10,9},{11,10},{12... | collective-permute-start | bytes 20 | tf_op jit(solution)/shard_map/ppermute | solution.py:96
  69.4 51.8 %collective-permute-start.11 = (s32[1]{0:T(128)}, s32[1]{0:T(128)}, u32[]{:S(2)}, u32[]{:S(2)}) collective-permute-start(s32[1]{0:T(128)} %param.12), channel_id=1, source_target_pairs={{1,8},{2,9},{3,10},{4,11},{5,12},{6,13},{7,14},{9,0},{10,1},{11,2}... | collective-permute-start | bytes 20 | tf_op jit(solution)/shard_map/ppermute | solution.py:96
  121.2 3.6 %collective-permute-start.7 = (s32[1]{0:T(128)}, s32[1]{0:T(128)}, u32[]{:S(2)}, u32[]{:S(2)}) collective-permute-start(s32[1]{0:T(128)} %param.12), channel_id=1, source_target_pairs={{0,8},{1,9},{2,10},{3,11},{4,12},{5,13},{6,14},{7,15},{8,0},{9,1},... | collective-permute-start | bytes 20 | tf_op jit(solution)/shard_map/ppermute | solution.py:96
  124.7 6.9 %collective-permute-start.8 = (s32[1]{0:T(128)}, s32[1]{0:T(128)}, u32[]{:S(2)}, u32[]{:S(2)}) collective-permute-start(s32[1]{0:T(128)} %param.12), channel_id=1, source_target_pairs={{0,1},{1,2},{2,3},{3,4},{4,5},{5,6},{6,7},{8,9},{9,10},{10,11},{11... | collective-permute-start | bytes 20 | tf_op jit(solution)/shard_map/ppermute | solution.py:96
  131.7 7.5 %collective-permute-start.9 = (s32[1]{0:T(128)}, s32[1]{0:T(128)}, u32[]{:S(2)}, u32[]{:S(2)}) collective-permute-start(s32[1]{0:T(128)} %param.12), channel_id=1, source_target_pairs={{0,9},{1,10},{2,11},{3,12},{4,13},{5,14},{6,15},{8,1},{9,2},{10,3}... | collective-permute-start | bytes 20 | tf_op jit(solution)/shard_map/ppermute | solution.py:96
  139.2 42.3 %collective-permute-start.12 = (bf16[384,1280]{1,0:T(8,128)(2,1)S(1)}, bf16[384,1280]{1,0:T(8,128)(2,1)}, u32[]{:S(2)}, u32[]{:S(2)}) collective-permute-start(bf16[384,1280]{1,0:T(8,128)(2,1)S(1)} %pad_maximum_fusion), channel_id=1, source_target_pairs={{0,8},{1,9},{2,10},{3,11},{4,12},{5,13},{6,14},{7,15},{8,0},{9,1},... | collective-permute-start | bytes 2949128 | tf_op jit(solution)/shard_map/ppermute | solution.py:121
  181.5 38.1 %collective-permute-start.3 = (bf16[384,1024]{1,0:T(8,128)(2,1)}, bf16[384,1024]{1,0:T(8,128)(2,1)}, u32[]{:S(2)}, u32[]{:S(2)}) collective-permute-start(bf16[384,1024]{1,0:T(8,128)(2,1)} %collective-permute-done.refs_3_.refs_4_), channel_id=1, source_target_pairs={{0,1},{1,2},{2,3},{3,4},{4,5},{5,6},{6,7},{8,9},{9,10},{10,11},{11... | collective-permute-start | bytes 2359304 | tf_op jit(solution)/shard_map/ppermute | solution.py:90
  186.6 36.6 %collective-permute-start.6 = (bf16[384,1024]{1,0:T(8,128)(2,1)}, bf16[384,1024]{1,0:T(8,128)(2,1)}, u32[]{:S(2)}, u32[]{:S(2)}) collective-permute-start(bf16[384,1024]{1,0:T(8,128)(2,1)} %collective-permute-done.refs_3_.refs_4_), channel_id=1, source_target_pairs={{1,0},{2,1},{3,2},{4,3},{5,4},{6,5},{7,6},{9,8},{10,9},{11,10},{12... | collective-permute-start | bytes 2359304 | tf_op jit(solution)/shard_map/ppermute | solution.py:90
  189.0 28.6 %collective-permute-start.15 = (bf16[384,768]{1,0:T(8,128)(2,1)}, bf16[384,768]{1,0:T(8,128)(2,1)}, u32[]{:S(2)}, u32[]{:S(2)}) collective-permute-start(bf16[384,768]{1,0:T(8,128)(2,1)} %pad_maximum_fusion.2), channel_id=1, source_target_pairs={{0,8},{1,9},{2,10},{3,11},{4,12},{5,13},{6,14},{7,15},{8,0},{9,1},... | collective-permute-start | bytes 1769480 | tf_op jit(solution)/shard_map/ppermute | solution.py:121
  189.1 45.3 %collective-permute-start.13 = (bf16[384,1280]{1,0:T(8,128)(2,1)}, bf16[384,1280]{1,0:T(8,128)(2,1)S(1)}, u32[]{:S(2)}, u32[]{:S(2)}) collective-permute-start(bf16[384,1280]{1,0:T(8,128)(2,1)} %collective-permute-done.12.refs_3_.refs_4_), channel_id=1, source_target_pairs={{0,1},{1,2},{2,3},{3,4},{4,5},{5,6},{6,7},{8,9},{9,10},{10,11},{11... | collective-permute-start | bytes 2949128 | tf_op jit(solution)/shard_map/ppermute | solution.py:90
  192.3 42.2 %collective-permute-start.14 = (bf16[384,1280]{1,0:T(8,128)(2,1)}, bf16[384,1280]{1,0:T(8,128)(2,1)S(1)}, u32[]{:S(2)}, u32[]{:S(2)}) collective-permute-start(bf16[384,1280]{1,0:T(8,128)(2,1)} %collective-permute-done.12.refs_3_.refs_4_), channel_id=1, source_target_pairs={{1,0},{2,1},{3,2},{4,3},{5,4},{6,5},{7,6},{9,8},{10,9},{11,10},{12... | collective-permute-start | bytes 2949128 | tf_op jit(solution)/shard_map/ppermute | solution.py:90
  217.7 32.1 %collective-permute-start.16 = (bf16[384,768]{1,0:T(8,128)(2,1)}, bf16[384,768]{1,0:T(8,128)(2,1)S(1)}, u32[]{:S(2)}, u32[]{:S(2)}) collective-permute-start(bf16[384,768]{1,0:T(8,128)(2,1)} %collective-permute-done.15.refs_3_.refs_4_), channel_id=1, source_target_pairs={{0,1},{1,2},{2,3},{3,4},{4,5},{5,6},{6,7},{8,9},{9,10},{10,11},{11... | collective-permute-start | bytes 1769480 | tf_op jit(solution)/shard_map/ppermute | solution.py:90
  219.6 30.2 %collective-permute-start.17 = (bf16[384,768]{1,0:T(8,128)(2,1)}, bf16[384,768]{1,0:T(8,128)(2,1)S(1)}, u32[]{:S(2)}, u32[]{:S(2)}) collective-permute-start(bf16[384,768]{1,0:T(8,128)(2,1)} %collective-permute-done.15.refs_3_.refs_4_), channel_id=1, source_target_pairs={{1,0},{2,1},{3,2},{4,3},{5,4},{6,5},{7,6},{9,8},{10,9},{11,10},{12... | collective-permute-start | bytes 1769480 | tf_op jit(solution)/shard_map/ppermute | solution.py:90
  234.5 0.9 copy-start.2
  235.4 1.0 copy-start.3
  249.8 10.9 %copy-start.9 = (f32[3072]{0:T(1024)S(1)}, f32[3072]{0:T(1024)}, u32[]{:S(2)}) copy-start(f32[3072]{0:T(1024)} %param.15) | copy-start | bytes 36868
  249.8 0.8 copy-start.4
  250.6 0.8 copy-start.5
Sparse Core Ops, SparseCore 0:
  9.6 106.1 all-gather.1
